TPU v7x, 512 devices: a whole 4x4x16 slice. The times are simulated.
512 devices in a mesh: row: 32 (over z, core), col: 16 (over x, y).
Axes of the slice: x: 4, y: 4, z: 16, core: 2. Of those that a mesh axis runs over, the one named last changes fastest.
Arguments:
- centroids: float32 [3, 16384], P(None, ('row', 'col')), may hold values from -4 to 4
- strengths: float32 [32, 16384], P(None, ('row', 'col')), may hold values from -6 to 6
- self_inv: float32 [32, 16384], P(None, ('row', 'col')), may hold values from -6 to 6
- wavenumbers: float32 [16], replicated, may hold values from 0.3 to 2
- field_pos: float32 [3, 8192], P(None, 'row'), may hold values from -4 to 4
- targets: float32 [32, 8192], P(None, 'row'), may hold values from -6 to 6
- lists: int32 [8192, 64], P('row'), may hold values from 0 to 16383
- connect: int32 [4, 16384], P(None, 'row'), may hold values from 0 to 16383, as said below
Outputs:
- adjoint: float32 [32, 16384], P(None, ('row', 'col'))
- vertex_sens: float32 [3, 16384], P(None, ('row', 'col'))
- objective: float32 [], replicated
Inputs may be any that keep to these rules, and one draw needn't show every extreme that they name: `connect`: the four vertices of panel i lie in the block of 512 vertices that starts at i - i % 512; the first of them is i itself.
All inputs are finite; a program needn't handle non-finite values.
Results may differ from a plain program's by a relative error of at most 0.0003.
Values sent between devices are 32-bit elements; how exact they have to be, the bound alone decides.
No kernel may reach another device: no remote copies, remote signals or barrier semaphores. Data moves between devices by JAX's collectives and lax.ppermute only.
A program may use at most 64 MiB of HBM per device.

v0:
```python
import math

import jax
import jax.numpy as jnp
from jax import lax
from jax.sharding import PartitionSpec as P

SOFT = 1.0


def pair_block(target_pos, target_str, target_mu, source_pos, source_str, source_mu, wavenumbers):
    freqs = wavenumbers.shape[0]
    offset = target_pos[:, None, :] - source_pos[:, :, None]
    squared = jnp.sum(offset * offset, axis=0) + SOFT
    inverse = lax.rsqrt(squared)
    distance = squared * inverse
    inverse_sq = inverse * inverse
    phase = wavenumbers[:, None, None] * distance[None]
    cosine = jnp.cos(phase)
    sine = jnp.sin(phase)
    deriv_real = -(cosine + phase * sine) * inverse_sq
    deriv_imag = (phase * cosine - sine) * inverse_sq
    tgt_real = target_str[:freqs, None, :]
    tgt_imag = target_str[freqs:, None, :]
    tmu_real = target_mu[:freqs, None, :]
    tmu_imag = target_mu[freqs:, None, :]
    src_real = source_str[:freqs, :, None]
    src_imag = source_str[freqs:, :, None]
    smu_real = source_mu[:freqs, :, None]
    smu_imag = source_mu[freqs:, :, None]
    prod_real = (
        tmu_real * src_real - tmu_imag * src_imag + smu_real * tgt_real - smu_imag * tgt_imag
    )
    prod_imag = (
        tmu_real * src_imag + tmu_imag * src_real + smu_real * tgt_imag + smu_imag * tgt_real
    )
    weight = jnp.sum(prod_real * deriv_real - prod_imag * deriv_imag, axis=0) * inverse
    return jnp.sum(weight[None] * offset, axis=1)


def pair_sweep(
    total, target_pos, target_str, target_mu, source_pos, source_str, source_mu, wavenumbers
):
    width = source_pos.shape[1]
    step = math.gcd(width, 32)

    def visit_block(carry, block_index):
        begin = block_index * step
        spos = lax.dynamic_slice_in_dim(source_pos, begin, step, 1)
        sstr = lax.dynamic_slice_in_dim(source_str, begin, step, 1)
        smu = lax.dynamic_slice_in_dim(source_mu, begin, step, 1)
        return (
            carry + pair_block(target_pos, target_str, target_mu, spos, sstr, smu, wavenumbers),
            None,
        )

    result, _ = lax.scan(visit_block, total, jnp.arange(width // step, dtype=jnp.int32))
    return result


def complex_times(left, right, freqs):
    left_real, left_imag = (left[:freqs], left[freqs:])
    right_real, right_imag = (right[:freqs], right[freqs:])
    return jnp.concatenate(
        [
            left_real * right_real - left_imag * right_imag,
            left_real * right_imag + left_imag * right_real,
        ],
        axis=0,
    )


def on_device(centroids, strengths, self_inv, wavenumbers, field_pos, targets, lists, connect):
    owned_count = centroids.shape[1]
    row_count = lax.axis_size("row")
    col_count = lax.axis_size("col")
    row_index = lax.axis_index("row")
    col_index = lax.axis_index("col")
    freqs = wavenumbers.shape[0]
    listed = lists.shape[1]
    panel_total = owned_count * row_count * col_count
    field_total = field_pos.shape[1] * row_count
    src_pos, src_str, src_inv = (
        lax.all_gather(centroids, "row", axis=1, tiled=True),
        lax.all_gather(strengths, "row", axis=1, tiled=True),
        lax.all_gather(self_inv, "row", axis=1, tiled=True),
    )
    source_count = src_pos.shape[1]
    panel_ids = lists.reshape(-1)
    owner_block = panel_ids // owned_count
    mask = (owner_block % col_count == col_index).astype(jnp.float32)
    local_ids = owner_block // col_count * owned_count + panel_ids % owned_count
    near = src_pos[:, local_ids]
    observer = jnp.repeat(field_pos, listed, axis=1)
    offset = observer - near
    distance = jnp.sqrt(jnp.sum(offset * offset, axis=0) + SOFT)
    inverse = mask / distance
    phase = wavenumbers[:, None] * distance[None]
    cosine = jnp.cos(phase)
    sine = jnp.sin(phase)
    near_str = src_str[:, local_ids]
    str_real = near_str[:freqs]
    str_imag = near_str[freqs:]
    part_real = (cosine * str_real - sine * str_imag) * inverse
    part_imag = (cosine * str_imag + sine * str_real) * inverse
    eta_part = jnp.concatenate(
        [
            part_real.reshape(freqs, -1, listed).sum(axis=2),
            part_imag.reshape(freqs, -1, listed).sum(axis=2),
        ],
        axis=0,
    )
    eta = lax.psum(eta_part, "col")
    resid = eta - targets
    misfit = lax.psum(jnp.sum(resid * resid), "row")
    objective = misfit / (freqs * field_total) + 1e-06
    rep_real = jnp.repeat(resid[:freqs], listed, axis=1)
    rep_imag = jnp.repeat(resid[freqs:], listed, axis=1)
    term_real = (cosine * rep_real + sine * rep_imag) * inverse
    term_imag = (cosine * rep_imag - sine * rep_real) * inverse
    terms = jnp.concatenate([term_real, term_imag], axis=0)
    source_part = jnp.zeros((2 * freqs, source_count), jnp.float32).at[:, local_ids].add(terms)
    source_part = source_part / objective
    late_scale = 1.0
    source_all = lax.psum(source_part, "row")
    mu_all = complex_times(source_all, src_inv, freqs)
    mu_own = lax.dynamic_slice_in_dim(mu_all, row_index * owned_count, owned_count, 1)
    tgt_pos, tgt_str, tgt_mu = (
        lax.all_gather(centroids, "col", axis=1, tiled=True),
        lax.all_gather(strengths, "col", axis=1, tiled=True),
        lax.all_gather(mu_own, "col", axis=1, tiled=True),
    )
    block_width = tgt_pos.shape[1]
    empty = jnp.zeros((3, block_width), jnp.float32)
    accum = pair_sweep(empty, tgt_pos, tgt_str, tgt_mu, src_pos, src_str, mu_all, wavenumbers)
    panel_sens = accum * (1.0 / math.sqrt(panel_total * freqs) * late_scale)
    vertex_local = connect - row_index * block_width
    vertex_part = jnp.zeros((3, block_width), jnp.float32)
    for corner in range(4):
        vertex_part = vertex_part.at[:, vertex_local[corner]].add(0.25 * panel_sens)
    vertex_own = lax.psum_scatter(vertex_part, "col", scatter_dimension=1, tiled=True)
    adjoint = mu_own * late_scale
    return (adjoint, vertex_own, objective)


def solution(mesh):
    return jax.shard_map(
        on_device,
        mesh=mesh,
        in_specs=(
            P(None, ("row", "col")),
            P(None, ("row", "col")),
            P(None, ("row", "col")),
            P(),
            P(None, "row"),
            P(None, "row"),
            P("row", None),
            P(None, "row"),
        ),
        out_specs=(P(None, ("row", "col")), P(None, ("row", "col")), P()),
        check_vma=False,
    )
```

profile of v0, /device:TPU:6, one launch (start us, length us, event | category | flops | bytes accessed | tf_op | source)
XLA Modules:
  0.0 1003.0 jit_solution(7111002203027337556)
XLA Ops:
  9.2 36.7 %all-gather = f32[32,32,3]{1,2,0:T(4,128)S(1)} all-gather(f32[1,32,3]{1,2,0:T(4,128)} %bitcast.59), channel_id=1, replica_groups=mesh['row'=32,'col'=16] {'row'}, dimensions={0}, use_global_device_ids=true | all-gather | bytes 12672 | tf_op jit(solution)/shard_map/all_gather | solution.py:84
  47.8 28.5 %all_gather.19 = f32[32,1024]{0,1:T(8,128)S(1)} all-gather(f32[32,32]{0,1:T(8,128)S(1)} %copy.150), channel_id=1, replica_groups=mesh['row'=32,'col'=16] {'row'}, dimensions={1}, use_global_device_ids=true | all-gather | bytes 135168 | tf_op jit(solution)/shard_map/all_gather | solution.py:85
  76.3 54.4 %gather_fusion = f32[16384,3]{1,0:T(8,128)} fusion(f32[3,1024]{0,1:T(8,128)S(1)} %bitcast.50, s32[16384]{0:T(1024)S(1)} %broadcast_clamp_fusion), kind=kCustom, calls=%fused_computation | custom fusion | bytes 458752 | tf_op jit(solution)/shard_map/gather | solution.py:93
  130.7 54.4 %gather_fusion.1 = f32[16384,32]{1,0:T(8,128)} fusion(f32[32,1024]{0,1:T(8,128)S(1)} %all_gather.19, s32[16384]{0:T(1024)S(1)} %broadcast_clamp_fusion), kind=kCustom, calls=%fused_computation.1 | custom fusion | bytes 4259840 | tf_op jit(solution)/shard_map/gather | solution.py:101
  185.1 5.1 copy.151
  194.9 5.7 fusion.22
  200.7 6.0 copy.172
  206.7 5.0 bitcast_reduce_fusion.1
  216.4 5.0 bitcast_reduce_fusion
  221.6 67.3 %psum.21 = f32[32,256]{1,0:T(8,128)S(1)} all-reduce(f32[32,256]{1,0:T(8,128)S(1)} %pad_maximum_fusion.1), channel_id=1, replica_groups=mesh['row'=32,'col'=16] {'col'}, use_global_device_ids=true, to_apply=%region_3.4 | all-reduce | flops 8192 | bytes 65536 | tf_op jit(solution)/shard_map/psum | solution.py:113
  294.0 6.8 fusion.26
  305.7 46.4 %psum.22 = f32[]{:T(128)} all-reduce(f32[]{:T(128)} %get-tuple-element.200), channel_id=1, replica_groups=mesh['row'=32,'col'=16] {'row'}, use_global_device_ids=true, to_apply=%region_6.7 | all-reduce | flops 1 | bytes 8 | tf_op jit(solution)/shard_map/psum | solution.py:115
  352.1 87.7 %scatter_custom_fusion = f32[32,1024]{0,1:T(8,128)S(1)} fusion(s32[16384]{0:T(1024)S(1)} %bitcast.55, f32[16384,32]{1,0:T(8,128)} %copy.157, f32[]{:T(128)} %constant.79.clone.1), kind=kCustom, calls=%fused_computation.62 | custom fusion | flops 524288 | bytes 131584 | tf_op jit(solution)/shard_map/scatter-add | solution.py:122
  441.6 28.5 %all_gather.22 = f32[32,512]{0,1:T(8,128)S(1)} all-gather(f32[32,32]{0,1:T(8,128)S(1)} %copy.150), channel_id=1, replica_groups=mesh['row'=32,'col'=16] {'col'}, dimensions={1}, use_global_device_ids=true | all-gather | bytes 69632 | tf_op jit(solution)/shard_map/all_gather | solution.py:130
  470.4 20.3 %all-gather.1 = f32[16,32,3]{1,2,0:T(4,128)S(1)} all-gather(f32[1,32,3]{1,2,0:T(4,128)S(1)} %bitcast.60), channel_id=1, replica_groups=mesh['row'=32,'col'=16] {'col'}, dimensions={0}, use_global_device_ids=true | all-gather | bytes 6528 | tf_op jit(solution)/shard_map/all_gather | solution.py:129
  490.7 28.2 %all_gather.20 = f32[32,1024]{0,1:T(8,128)S(1)} all-gather(f32[32,32]{0,1:T(8,128)S(1)} %copy.158), channel_id=1, replica_groups=mesh['row'=32,'col'=16] {'row'}, dimensions={1}, use_global_device_ids=true | all-gather | bytes 135168 | tf_op jit(solution)/shard_map/all_gather | solution.py:86
  518.9 129.3 %all-reduce.2.cloned.1.call-done = f32[32,1024]{0,1:T(8,128)} async-done(((f32[32,1024]{0,1:T(8,128)}), f32[32,1024]{0,1:T(8,128)}) %all-reduce.2.cloned.1.call-update) | async-done | bytes 131088 | tf_op jit(solution)/shard_map/psum | solution.py:125
  650.1 23.4 %all_gather.21 = f32[32,512]{0,1:T(8,128)S(1)} all-gather(f32[32,32]{0,1:T(8,128)S(1)} %fusion.38), channel_id=1, replica_groups=mesh['row'=32,'col'=16] {'col'}, dimensions={1}, use_global_device_ids=true | all-gather | bytes 69632 | tf_op jit(solution)/shard_map/all_gather | solution.py:131
  673.6 220.7 %while.11 = (s32[]{:T(128)}, f32[3,512]{1,0:T(4,128)S(1)}, f32[32,512]{1,0:T(8,128)S(1)}, s32[32]{0:T(128)S(1)}, f32[32,1024]{0,1:T(8,128)S(1)}, /*index=5*/f32[...) while((s32[]{:T(128)}, f32[3,512]{1,0:T(4,128)S(1)}, ...), condition=%wide.region_12.13_spmd.clone, body=%wide.region_8.12_spmd.clone.sunk | while | flops 7161352 | bytes 1193769 | solution.py:57
  675.5 4.9 fusion.48
  682.4 4.9 fusion.48
  696.2 4.9 fusion.48
  710.0 4.9 fusion.48
  716.9 4.9 fusion.48
  723.8 4.9 fusion.48
  730.7 4.9 fusion.48
  744.5 4.9 fusion.48
  758.2 4.9 fusion.48
  765.1 4.9 fusion.48
  778.9 4.9 fusion.48
  792.7 4.9 fusion.48
  908.7 84.9 %reduce-scatter.2.cloned.1.call-done = f32[3,32]{0,1:T(8,128)} async-done(((f32[3,512]{0,1:T(8,128)}), f32[3,32]{0,1:T(8,128)}) %reduce-scatter.2.cloned.1.call-update) | async-done | bytes 400 | tf_op jit(solution)/shard_map/reduce_scatter | solution.py:141
  (498 shorter events, 181.2 us)
Async XLA Ops:
  7.2 641.1 %all-reduce.2.cloned.1.call-start = ((), (), s32[]{:S(2)}) async-start(), calls=%async_computation.1 | async-start | bytes 1048576 | tf_op jit(solution)/shard_map/psum | solution.py:125
  185.1 9.9 copy-start.6
  200.6 11.2 %copy-start = (f32[16,16384]{1,0:T(8,128)S(1)}, f32[16,16384]{1,0:T(8,128)}, u32[]{:S(2)}) copy-start(f32[16,16384]{1,0:T(8,128)} %get-tuple-element.219) | copy-start | bytes 3145732
  211.8 77.0 %copy-start.2 = (f32[32,256]{1,0:T(8,128)S(1)}, f32[32,256]{1,0:T(8,128)}, u32[]{:S(2)}) copy-start(f32[32,256]{1,0:T(8,128)} %param.15) | copy-start | bytes 98308
  300.8 169.3 %copy-start.5 = (s32[4,512]{1,0:T(4,128)S(1)}, s32[4,512]{1,0:T(4,128)}, u32[]{:S(2)}) copy-start(s32[4,512]{1,0:T(4,128)} %param.17) | copy-start | bytes 24580
  300.9 169.3 %copy-start.3 = (f32[32,32]{1,0:T(8,128)S(1)}, f32[32,32]{1,0:T(8,128)}, u32[]{:S(2)}) copy-start(f32[32,32]{1,0:T(8,128)} %param.12) | copy-start | bytes 12292
  300.9 169.5 %copy-start.4 = (f32[3,32]{1,0:T(4,128)S(1)}, f32[3,32]{1,0:T(4,128)}, u32[]{:S(2)}) copy-start(f32[3,32]{1,0:T(4,128)} %param.10) | copy-start | bytes 1156
  441.4 552.3 %reduce-scatter.2.cloned.1.call-start = ((), (), s32[]{:S(2)}) async-start(), calls=%async_computation.2 | async-start | bytes 278528 | tf_op jit(solution)/shard_map/reduce_scatter | solution.py:141
  907.3 0.7 copy-start.1
Sparse Core Ops, SparseCore 0:
  441.5 206.7 all-reduce.1
  908.2 85.4 reduce-scatter.1
where the time goes:
time: 1000 us
  other arithmetic  296 us (30%)
  blocking collectives  279 us (28%)
  waiting for transfers between devices  214 us (21%)
  local copies, waits for them, and re-layouts  174 us (17%)
  loops' own time  23.3 us (2%)
  between operations  16.1 us (2%)
    reduce_sum x32, other arithmetic, pair_block(): jnp.sum(prod_real * deriv_real - prod_imag * deriv_imag, axis=0) * inverse  156 us
    psum x1, waiting for transfers between devices, on_device(): source_all = lax.psum(source_part, 'row')  129 us
    scatter-add x1, other arithmetic, on_device(): jnp.zeros((2 * freqs, source_count), jnp.float32).at[:, local_ids]  87.7 us
    reduce_scatter x1, waiting for transfers between devices, on_device(): lax.psum_scatter(vertex_part, 'col', scatter_dimension=1, tiled=True)  84.9 us
    psum x1, blocking collectives, on_device(): eta = lax.psum(eta_part, 'col')  67.3 us
    gather x2, local copies, waits for them, and re-layouts, on_device(): near_str = src_str[:, local_ids]  59.5 us
    gather x1, local copies, waits for them, and re-layouts, on_device(): near = src_pos[:, local_ids]  54.4 us
    psum x1, blocking collectives, on_device(): misfit = lax.psum(jnp.sum(resid * resid), 'row')  46.4 us
  transfers between devices with their start and end apart: 2, of which 2 were waited for; matrix products, arithmetic and copies ran while one was open for 0% of the time, Pallas kernels for 0%

commit v1 on v0

--- a/solution.py
+++ b/solution.py
@@ -42,7 +42,7 @@
     total, target_pos, target_str, target_mu, source_pos, source_str, source_mu, wavenumbers
 ):
     width = source_pos.shape[1]
-    step = math.gcd(width, 32)
+    step = math.gcd(width, 128)
 
     def visit_block(carry, block_index):
         begin = block_index * step
@@ -80,17 +80,20 @@
     listed = lists.shape[1]
     panel_total = owned_count * row_count * col_count
     field_total = field_pos.shape[1] * row_count
-    src_pos, src_str, src_inv = (
-        lax.all_gather(centroids, "row", axis=1, tiled=True),
-        lax.all_gather(strengths, "row", axis=1, tiled=True),
-        lax.all_gather(self_inv, "row", axis=1, tiled=True),
-    )
-    source_count = src_pos.shape[1]
+    pos_rows = centroids.shape[0]
+    str_rows = strengths.shape[0]
+    owned = jnp.concatenate([centroids, strengths, self_inv], axis=0)
+    src_all = lax.all_gather(owned, "row", axis=1, tiled=True)
+    src_pos = src_all[:pos_rows]
+    src_str = src_all[pos_rows : pos_rows + str_rows]
+    src_inv = src_all[pos_rows + str_rows :]
+    source_count = src_all.shape[1]
     panel_ids = lists.reshape(-1)
     owner_block = panel_ids // owned_count
     mask = (owner_block % col_count == col_index).astype(jnp.float32)
     local_ids = owner_block // col_count * owned_count + panel_ids % owned_count
-    near = src_pos[:, local_ids]
+    near_all = jnp.take(src_all[: pos_rows + str_rows], local_ids, axis=1)
+    near = near_all[:pos_rows]
     observer = jnp.repeat(field_pos, listed, axis=1)
     offset = observer - near
     distance = jnp.sqrt(jnp.sum(offset * offset, axis=0) + SOFT)
@@ -98,7 +101,7 @@
     phase = wavenumbers[:, None] * distance[None]
     cosine = jnp.cos(phase)
     sine = jnp.sin(phase)
-    near_str = src_str[:, local_ids]
+    near_str = near_all[pos_rows:]
     str_real = near_str[:freqs]
     str_imag = near_str[freqs:]
     part_real = (cosine * str_real - sine * str_imag) * inverse
@@ -112,34 +115,37 @@
     )
     eta = lax.psum(eta_part, "col")
     resid = eta - targets
-    misfit = lax.psum(jnp.sum(resid * resid), "row")
-    objective = misfit / (freqs * field_total) + 1e-06
     rep_real = jnp.repeat(resid[:freqs], listed, axis=1)
     rep_imag = jnp.repeat(resid[freqs:], listed, axis=1)
     term_real = (cosine * rep_real + sine * rep_imag) * inverse
     term_imag = (cosine * rep_imag - sine * rep_real) * inverse
     terms = jnp.concatenate([term_real, term_imag], axis=0)
     source_part = jnp.zeros((2 * freqs, source_count), jnp.float32).at[:, local_ids].add(terms)
-    source_part = source_part / objective
-    late_scale = 1.0
-    source_all = lax.psum(source_part, "row")
+    misfit_part = jnp.sum(resid * resid)
+    misfit_row = jnp.where(
+        lax.broadcasted_iota(jnp.int32, (1, source_count), 1) == 0, misfit_part, 0.0
+    )
+    packed = lax.psum(jnp.concatenate([source_part, misfit_row], axis=0), "row")
+    objective = packed[2 * freqs, 0] / (freqs * field_total) + 1e-06
+    source_all = packed[: 2 * freqs] / objective
     mu_all = complex_times(source_all, src_inv, freqs)
     mu_own = lax.dynamic_slice_in_dim(mu_all, row_index * owned_count, owned_count, 1)
-    tgt_pos, tgt_str, tgt_mu = (
-        lax.all_gather(centroids, "col", axis=1, tiled=True),
-        lax.all_gather(strengths, "col", axis=1, tiled=True),
-        lax.all_gather(mu_own, "col", axis=1, tiled=True),
+    tgt_all = lax.all_gather(
+        jnp.concatenate([centroids, strengths, mu_own], axis=0), "col", axis=1, tiled=True
     )
+    tgt_pos = tgt_all[:pos_rows]
+    tgt_str = tgt_all[pos_rows : pos_rows + str_rows]
+    tgt_mu = tgt_all[pos_rows + str_rows :]
     block_width = tgt_pos.shape[1]
     empty = jnp.zeros((3, block_width), jnp.float32)
     accum = pair_sweep(empty, tgt_pos, tgt_str, tgt_mu, src_pos, src_str, mu_all, wavenumbers)
-    panel_sens = accum * (1.0 / math.sqrt(panel_total * freqs) * late_scale)
+    panel_sens = accum * (1.0 / math.sqrt(panel_total * freqs))
     vertex_local = connect - row_index * block_width
-    vertex_part = jnp.zeros((3, block_width), jnp.float32)
-    for corner in range(4):
-        vertex_part = vertex_part.at[:, vertex_local[corner]].add(0.25 * panel_sens)
+    vertex_part = jnp.zeros((3, block_width), jnp.float32).at[:, vertex_local.reshape(-1)].add(
+        jnp.tile(0.25 * panel_sens, (1, connect.shape[0]))
+    )
     vertex_own = lax.psum_scatter(vertex_part, "col", scatter_dimension=1, tiled=True)
-    adjoint = mu_own * late_scale
+    adjoint = mu_own
     return (adjoint, vertex_own, objective)
 
 

time: 1000 us -> 816 us (0.82)
  blocking collectives: 279 us -> 129 us
  local copies, waits for them, and re-layouts: 174 us -> 94.1 us
  waiting for transfers between devices: 214 us -> 291 us
  loops' own time: 23.3 us -> 6.26 us
  other arithmetic: 296 us -> 279 us
    all_gather x6 -> x2, blocking collectives: 166 us -> 61.3 us  [the longest x1 37.6 us: on_device(): src_all = lax.all_gather(owned, 'row', axis=1, tiled=True)]
    psum x1, waiting for transfers between devices: 129 us -> 206 us  [on_device(): packed = lax.psum(jnp.concatenate([source_part, misfit_row], axis=0), 'row')]
    gather x3 -> x2, local copies, waits for them, and re-layouts: 114 us -> 59.7 us  [on_device(): near_all = jnp.take(src_all[:pos_rows + str_rows], local_ids, axis=1)]
    psum x1 -> x0, blocking collectives: 46.4 us -> none  [on_device(): misfit = lax.psum(jnp.sum(resid * resid), 'row')]
    another operation x1, loops' own time: 23.3 us -> 6.26 us  [pair_sweep(): lax.scan(visit_block, total, jnp.arange(width // step, dtype=jnp.int32))]
    dynamic_slice x32 -> x8, local copies, waits for them, and re-layouts: 18.8 us -> 5.34 us  [pair_sweep(): lax.scan(visit_block, total, jnp.arange(width // step, dtype=jnp.int32))]
    reduce_sum x32 -> x8, other arithmetic: 156 us -> 147 us  [pair_block(): jnp.sum(prod_real * deriv_real - prod_imag * deriv_imag, axis=0) * inverse]
where the time goes in v1:
time: 816 us; the launch traced here: 815 us
  waiting for transfers between devices  291 us (36%)
  other arithmetic  279 us (34%)
  blocking collectives  129 us (16%)
  local copies, waits for them, and re-layouts  94.1 us (12%)
  between operations  16.1 us (2%)
    psum x1, waiting for transfers between devices, on_device(): packed = lax.psum(jnp.concatenate([source_part, misfit_row], axis=0), 'row')  206 us
    reduce_sum x8, other arithmetic, pair_block(): jnp.sum(prod_real * deriv_real - prod_imag * deriv_imag, axis=0) * inverse  147 us
    scatter-add x1, other arithmetic, on_device(): jnp.zeros((2 * freqs, source_count), jnp.float32).at[:, local_ids]  87.7 us
    reduce_scatter x1, waiting for transfers between devices, on_device(): lax.psum_scatter(vertex_part, 'col', scatter_dimension=1, tiled=True)  85.6 us
    psum x1, blocking collectives, on_device(): eta = lax.psum(eta_part, 'col')  67.3 us
    gather x2, local copies, waits for them, and re-layouts, on_device(): near_all = jnp.take(src_all[:pos_rows + str_rows], local_ids, axis=1)  59.7 us
    all_gather x1, blocking collectives, on_device(): src_all = lax.all_gather(owned, 'row', axis=1, tiled=True)  37.6 us
    all_gather x1, blocking collectives, on_device(): lax.all_gather(jnp.concatenate([centroids, strengths, mu_own], axis=0), '...  23.6 us
  transfers between devices with their start and end apart: 2, of which 2 were waited for; matrix products, arithmetic and copies ran while one was open for 0% of the time, Pallas kernels for 0%

profile of v1, /device:TPU:6, one launch (start us, length us, event | category | flops | bytes accessed | tf_op | source)
XLA Modules:
  0.0 815.2 jit_solution(18227825335642472802)
XLA Ops:
  10.8 37.6 %all_gather.6 = f32[67,1024]{0,1:T(8,128)S(1)} all-gather(f32[67,32]{0,1:T(8,128)S(1)} %pad_maximum_fusion.3), channel_id=1, replica_groups=mesh['row'=32,'col'=16] {'row'}, dimensions={1}, use_global_device_ids=true | all-gather | bytes 283008 | tf_op jit(solution)/shard_map/all_gather | solution.py:86
  49.9 54.4 %gather_fusion = f32[16384,35]{1,0:T(8,128)} fusion(f32[35,1024]{0,1:T(8,128)S(1)} %bitcast.25, s32[16384]{0:T(1024)S(1)} %broadcast_clamp_fusion), kind=kCustom, calls=%fused_computation | custom fusion | bytes 4653056 | tf_op jit(solution)/shard_map/jit(_take)/gather | solution.py:95
  104.4 5.3 copy.145
  112.1 1.0 select_bitcast_fusion
  113.4 4.4 fusion.20
  117.8 4.6 copy.163
  122.4 5.0 bitcast_reduce_fusion.1
  127.6 4.6 copy.164
  132.2 5.1 bitcast_reduce_fusion
  137.3 67.3 %psum.14 = f32[32,256]{1,0:T(8,128)S(1)} all-reduce(f32[32,256]{1,0:T(8,128)S(1)} %pad_maximum_fusion.2), channel_id=1, replica_groups=mesh['row'=32,'col'=16] {'col'}, use_global_device_ids=true, to_apply=%region_3.4 | all-reduce | flops 8192 | bytes 65536 | tf_op jit(solution)/shard_map/psum | solution.py:116
  205.8 1.7 reshape.318
  208.1 1.6 reshape.319
  209.8 6.8 fusion.24
  216.8 4.7 copy.150
  222.1 87.7 %scatter_custom_fusion = f32[32,1024]{0,1:T(8,128)S(1)} fusion(s32[16384]{0:T(1024)} %bitcast.30, f32[16384,32]{1,0:T(8,128)} %copy.150, f32[]{:T(128)} %constant.96.clone.1), kind=kCustom, calls=%fused_computation.59 | custom fusion | flops 524288 | bytes 131584 | tf_op jit(solution)/shard_map/scatter-add | solution.py:123
  309.8 1.0 pad_maximum_fusion
  311.6 205.7 %all-reduce.2.cloned.1.call-done = f32[33,1024]{0,1:T(8,128)} async-done(((f32[33,1024]{0,1:T(8,128)}), f32[33,1024]{0,1:T(8,128)}) %all-reduce.2.cloned.1.call-update) | async-done | bytes 135184 | tf_op jit(solution)/shard_map/psum | solution.py:128
  517.3 1.3 slice.115
  519.2 1.1 slice_divide_fusion
  521.4 23.6 %all_gather.7 = f32[67,512]{0,1:T(8,128)S(1)} all-gather(f32[67,32]{0,1:T(8,128)S(1)} %pad_maximum_fusion.5), channel_id=1, replica_groups=mesh['row'=32,'col'=16] {'col'}, dimensions={1}, use_global_device_ids=true | all-gather | bytes 145792 | tf_op jit(solution)/shard_map/all_gather | solution.py:133
  545.6 162.3 %while.11 = (s32[]{:T(128)}, f32[3,512]{1,0:T(4,128)S(1)}, f32[32,512]{1,0:T(8,128)S(1)}, s32[8]{0:T(128)S(1)}, f32[32,1024]{1,0:T(8,128)S(1)}, /*index=5*/f32[3...) while((s32[]{:T(128)}, f32[3,512]{1,0:T(4,128)S(1)}, ...), condition=%wide.region_11.12_spmd.clone, body=%wide.region_7.11_spmd.clone.sunk | while | flops 28640776 | bytes 3418409 | solution.py:57
  547.2 18.4 %fusion.53 = f32[128,512]{1,0:T(8,128)S(1)} fusion(f32[128,512]{1,0:T(8,128)S(1)} %get-tuple-element.299, f32[128,512]{1,0:T(8,128)S(1)} %get-tuple-element.300, f32[16]{0:T(128)S(1)} %get-tuple-element.346, f32[16,512]{1,0:T(8,128)S(1)} %get-tuple-element.301, f32[16,128]{1,0:T(8,128)S(1)} %get-tuple-element.302, ...), kind=kLoop, calls=%fused_computation.12.clone.1 | loop fusion | flops 27197440 | bytes 950336 | tf_op jit(solution)/shard_map/while/body/eval_jaxpr/reduce_sum | solution.py:37
  567.5 18.4 %fusion.53 = f32[128,512]{1,0:T(8,128)S(1)} fusion(f32[128,512]{1,0:T(8,128)S(1)} %get-tuple-element.299, f32[128,512]{1,0:T(8,128)S(1)} %get-tuple-element.300, f32[16]{0:T(128)S(1)} %get-tuple-element.346, f32[16,512]{1,0:T(8,128)S(1)} %get-tuple-element.301, f32[16,128]{1,0:T(8,128)S(1)} %get-tuple-element.302, ...), kind=kLoop, calls=%fused_computation.12.clone.1 | loop fusion | flops 27197440 | bytes 950336 | tf_op jit(solution)/shard_map/while/body/eval_jaxpr/reduce_sum | solution.py:37
  587.8 18.4 %fusion.53 = f32[128,512]{1,0:T(8,128)S(1)} fusion(f32[128,512]{1,0:T(8,128)S(1)} %get-tuple-element.299, f32[128,512]{1,0:T(8,128)S(1)} %get-tuple-element.300, f32[16]{0:T(128)S(1)} %get-tuple-element.346, f32[16,512]{1,0:T(8,128)S(1)} %get-tuple-element.301, f32[16,128]{1,0:T(8,128)S(1)} %get-tuple-element.302, ...), kind=kLoop, calls=%fused_computation.12.clone.1 | loop fusion | flops 27197440 | bytes 950336 | tf_op jit(solution)/shard_map/while/body/eval_jaxpr/reduce_sum | solution.py:37
  608.1 18.4 %fusion.53 = f32[128,512]{1,0:T(8,128)S(1)} fusion(f32[128,512]{1,0:T(8,128)S(1)} %get-tuple-element.299, f32[128,512]{1,0:T(8,128)S(1)} %get-tuple-element.300, f32[16]{0:T(128)S(1)} %get-tuple-element.346, f32[16,512]{1,0:T(8,128)S(1)} %get-tuple-element.301, f32[16,128]{1,0:T(8,128)S(1)} %get-tuple-element.302, ...), kind=kLoop, calls=%fused_computation.12.clone.1 | loop fusion | flops 27197440 | bytes 950336 | tf_op jit(solution)/shard_map/while/body/eval_jaxpr/reduce_sum | solution.py:37
  628.3 18.4 %fusion.53 = f32[128,512]{1,0:T(8,128)S(1)} fusion(f32[128,512]{1,0:T(8,128)S(1)} %get-tuple-element.299, f32[128,512]{1,0:T(8,128)S(1)} %get-tuple-element.300, f32[16]{0:T(128)S(1)} %get-tuple-element.346, f32[16,512]{1,0:T(8,128)S(1)} %get-tuple-element.301, f32[16,128]{1,0:T(8,128)S(1)} %get-tuple-element.302, ...), kind=kLoop, calls=%fused_computation.12.clone.1 | loop fusion | flops 27197440 | bytes 950336 | tf_op jit(solution)/shard_map/while/body/eval_jaxpr/reduce_sum | solution.py:37
  648.6 18.4 %fusion.53 = f32[128,512]{1,0:T(8,128)S(1)} fusion(f32[128,512]{1,0:T(8,128)S(1)} %get-tuple-element.299, f32[128,512]{1,0:T(8,128)S(1)} %get-tuple-element.300, f32[16]{0:T(128)S(1)} %get-tuple-element.346, f32[16,512]{1,0:T(8,128)S(1)} %get-tuple-element.301, f32[16,128]{1,0:T(8,128)S(1)} %get-tuple-element.302, ...), kind=kLoop, calls=%fused_computation.12.clone.1 | loop fusion | flops 27197440 | bytes 950336 | tf_op jit(solution)/shard_map/while/body/eval_jaxpr/reduce_sum | solution.py:37
  668.9 18.4 %fusion.53 = f32[128,512]{1,0:T(8,128)S(1)} fusion(f32[128,512]{1,0:T(8,128)S(1)} %get-tuple-element.299, f32[128,512]{1,0:T(8,128)S(1)} %get-tuple-element.300, f32[16]{0:T(128)S(1)} %get-tuple-element.346, f32[16,512]{1,0:T(8,128)S(1)} %get-tuple-element.301, f32[16,128]{1,0:T(8,128)S(1)} %get-tuple-element.302, ...), kind=kLoop, calls=%fused_computation.12.clone.1 | loop fusion | flops 27197440 | bytes 950336 | tf_op jit(solution)/shard_map/while/body/eval_jaxpr/reduce_sum | solution.py:37
  689.2 18.4 %fusion.53 = f32[128,512]{1,0:T(8,128)S(1)} fusion(f32[128,512]{1,0:T(8,128)S(1)} %get-tuple-element.299, f32[128,512]{1,0:T(8,128)S(1)} %get-tuple-element.300, f32[16]{0:T(128)S(1)} %get-tuple-element.346, f32[16,512]{1,0:T(8,128)S(1)} %get-tuple-element.301, f32[16,128]{1,0:T(8,128)S(1)} %get-tuple-element.302, ...), kind=kLoop, calls=%fused_computation.12.clone.1 | loop fusion | flops 27197440 | bytes 950336 | tf_op jit(solution)/shard_map/while/body/eval_jaxpr/reduce_sum | solution.py:37
  708.1 12.1 %scatter_custom_fusion.1 = f32[3,512]{0,1:T(8,128)} fusion(s32[2048]{0:T(1024)S(1)} %bitcast.32, f32[2048,3]{1,0:T(8,128)S(1)} %bitcast.28, f32[]{:T(128)} %constant.96.clone.1), kind=kCustom, calls=%fused_computation.74 | custom fusion | flops 6144 | bytes 6148 | tf_op jit(solution)/shard_map/scatter-add | solution.py:144
  720.2 85.6 %reduce-scatter.2.cloned.1.call-done = f32[3,32]{0,1:T(8,128)} async-done(((f32[3,512]{0,1:T(8,128)}), f32[3,32]{0,1:T(8,128)}) %reduce-scatter.2.cloned.1.call-update) | async-done | bytes 400 | tf_op jit(solution)/shard_map/reduce_scatter | solution.py:147
  805.8 1.4 copy.162
  (141 shorter events, 22.1 us)
Async XLA Ops:
  7.2 510.1 %all-reduce.2.cloned.1.call-start = ((), (), s32[]{:S(2)}) async-start(), calls=%async_computation.1 | async-start | bytes 1048576 | tf_op jit(solution)/shard_map/psum | solution.py:128
  8.4 101.3 %copy-start.1 = (s32[16384]{0:T(1024)}, s32[16384]{0:T(1024)S(1)}, u32[]{:S(2)}) copy-start(s32[16384]{0:T(1024)S(1)} %reshape.315) | copy-start | bytes 196612
  10.0 94.4 %copy-start.4 = (f32[32,32]{0,1:T(8,128)}, f32[32,32]{0,1:T(8,128)S(1)}, u32[]{:S(2)}) copy-start(f32[32,32]{0,1:T(8,128)S(1)} %copy.143) | copy-start | bytes 12292
  49.3 0.6 copy-start.3
  112.1 1.0 copy-start
  112.1 1.2 copy-start.2
  112.1 1.3 copy-start.9
  132.2 72.4 %copy-start.7 = (f32[32,256]{1,0:T(8,128)S(1)}, f32[32,256]{1,0:T(8,128)}, u32[]{:S(2)}) copy-start(f32[32,256]{1,0:T(8,128)} %param.15) | copy-start | bytes 98308
  216.8 94.2 %copy-start.8 = (s32[4,512]{1,0:T(4,128)S(1)}, s32[4,512]{1,0:T(4,128)}, u32[]{:S(2)}) copy-start(s32[4,512]{1,0:T(4,128)} %param.17) | copy-start | bytes 24580
  310.9 210.4 %copy-start.5 = (f32[32,32]{0,1:T(8,128)S(1)}, f32[32,32]{0,1:T(8,128)}, u32[]{:S(2)}) copy-start(f32[32,32]{0,1:T(8,128)} %copy-done.4) | copy-start | bytes 12292
  310.9 494.9 %reduce-scatter.2.cloned.1.call-start = ((), (), s32[]{:S(2)}) async-start(), calls=%async_computation.2 | async-start | bytes 278528 | tf_op jit(solution)/shard_map/reduce_scatter | solution.py:147
  521.2 24.3 %copy-start.6 = (f32[32,32]{1,0:T(8,128)}, f32[32,32]{1,0:T(8,128)S(1)}, u32[]{:S(2)}) copy-start(f32[32,32]{1,0:T(8,128)S(1)} %fusion.42) | copy-start | bytes 12292
Sparse Core Ops, SparseCore 0:
  311.0 206.2 all-reduce.1
  720.3 85.4 reduce-scatter.1

commit v2 on v1

--- a/solution.py
+++ b/solution.py
@@ -70,6 +70,16 @@
     )
 
 
+def xor_psum(value, axis):
+    count = lax.axis_size(axis)
+    shift = 1
+    while shift < count:
+        partner = [(index, index ^ shift) for index in range(count)]
+        value = value + lax.ppermute(value, axis, partner)
+        shift *= 2
+    return value
+
+
 def on_device(centroids, strengths, self_inv, wavenumbers, field_pos, targets, lists, connect):
     owned_count = centroids.shape[1]
     row_count = lax.axis_size("row")
@@ -113,7 +123,7 @@
         ],
         axis=0,
     )
-    eta = lax.psum(eta_part, "col")
+    eta = xor_psum(eta_part, "col")
     resid = eta - targets
     rep_real = jnp.repeat(resid[:freqs], listed, axis=1)
     rep_imag = jnp.repeat(resid[freqs:], listed, axis=1)
@@ -125,7 +135,7 @@
     misfit_row = jnp.where(
         lax.broadcasted_iota(jnp.int32, (1, source_count), 1) == 0, misfit_part, 0.0
     )
-    packed = lax.psum(jnp.concatenate([source_part, misfit_row], axis=0), "row")
+    packed = xor_psum(jnp.concatenate([source_part, misfit_row], axis=0), "row")
     objective = packed[2 * freqs, 0] / (freqs * field_total) + 1e-06
     source_all = packed[: 2 * freqs] / objective
     mu_all = complex_times(source_all, src_inv, freqs)
@@ -144,7 +154,9 @@
     vertex_part = jnp.zeros((3, block_width), jnp.float32).at[:, vertex_local.reshape(-1)].add(
         jnp.tile(0.25 * panel_sens, (1, connect.shape[0]))
     )
-    vertex_own = lax.psum_scatter(vertex_part, "col", scatter_dimension=1, tiled=True)
+    vertex_own = lax.dynamic_slice_in_dim(
+        xor_psum(vertex_part, "col"), col_index * owned_count, owned_count, 1
+    )
     adjoint = mu_own
     return (adjoint, vertex_own, objective)
 

time: 816 us -> 652 us (0.80); the launches traced: 815 us -> 639 us
  waiting for transfers between devices: 291 us -> 159 us
  blocking collectives: 129 us -> 61.6 us
  starting transfers between devices: 0.08 us -> 42.1 us
  between operations: 16.1 us -> 2.86 us
    psum x1 -> x0, waiting for transfers between devices: 206 us -> none  [on_device(): packed = lax.psum(jnp.concatenate([source_part, misfit_row], axis=0), 'row')]
    ppermute x0 -> x13, waiting for transfers between devices: none -> 159 us  [xor_psum(): value = value + lax.ppermute(value, axis, partner)]
    reduce_scatter x1 -> x0, waiting for transfers between devices: 85.6 us -> none  [on_device(): lax.psum_scatter(vertex_part, 'col', scatter_dimension=1, tiled=True)]
    psum x1 -> x0, blocking collectives: 67.3 us -> none  [on_device(): eta = lax.psum(eta_part, 'col')]
    ppermute x0 -> x13, starting transfers between devices: none -> 42.1 us  [xor_psum(): value = value + lax.ppermute(value, axis, partner)]
  transfers between devices with their start and end apart: 2 -> 13, of which waited for: 2 -> 13; matrix products, arithmetic and copies ran while one was open for 0% -> 0% of each run, Pallas kernels for 0% -> 0%
where the time goes in v2:
time: 652 us; the launch traced here: 639 us
  other arithmetic  277 us (42%)
  waiting for transfers between devices  159 us (24%)
  local copies, waits for them, and re-layouts  92.1 us (14%)
  blocking collectives  61.6 us (9%)
  starting transfers between devices  42.1 us (6%)
    ppermute x13, waiting for transfers between devices, xor_psum(): value = value + lax.ppermute(value, axis, partner)  159 us
    reduce_sum x8, other arithmetic, pair_block(): jnp.sum(prod_real * deriv_real - prod_imag * deriv_imag, axis=0) * inverse  147 us
    scatter-add x1, other arithmetic, on_device(): jnp.zeros((2 * freqs, source_count), jnp.float32).at[:, local_ids]  87.7 us
    gather x2, local copies, waits for them, and re-layouts, on_device(): near_all = jnp.take(src_all[:pos_rows + str_rows], local_ids, axis=1)  59.7 us
    ppermute x13, starting transfers between devices, xor_psum(): value = value + lax.ppermute(value, axis, partner)  42.1 us
    all_gather x1, blocking collectives, on_device(): src_all = lax.all_gather(owned, 'row', axis=1, tiled=True)  37.6 us
    all_gather x1, blocking collectives, on_device(): lax.all_gather(jnp.concatenate([centroids, strengths, mu_own], axis=0), '...  23.9 us
  transfers between devices with their start and end apart: 13, of which 13 were waited for; matrix products, arithmetic and copies ran while one was open for 0% of the time, Pallas kernels for 0%

profile of v2, /device:TPU:6, one launch (start us, length us, event | category | flops | bytes accessed | tf_op | source)
XLA Modules:
  0.0 639.5 jit_solution(14269795453424151237)
XLA Ops:
  4.3 37.6 %all_gather.6 = f32[67,1024]{0,1:T(8,128)S(1)} all-gather(f32[67,32]{0,1:T(8,128)S(1)} %pad_maximum_fusion.3), channel_id=1, replica_groups=mesh['row'=32,'col'=16] {'row'}, dimensions={1}, use_global_device_ids=true | all-gather | bytes 283008 | tf_op jit(solution)/shard_map/all_gather | solution.py:96
  43.3 54.4 %gather_fusion = f32[16384,35]{1,0:T(8,128)} fusion(f32[35,1024]{0,1:T(8,128)S(1)} %bitcast.25, s32[16384]{0:T(1024)S(1)} %broadcast_clamp_fusion), kind=kCustom, calls=%fused_computation | custom fusion | bytes 4653056 | tf_op jit(solution)/shard_map/jit(_take)/gather | solution.py:105
  97.8 5.3 copy.147
  106.8 4.4 fusion.20
  111.2 4.6 copy.165
  115.9 5.0 bitcast_reduce_fusion.1
  121.0 4.6 copy.166
  125.6 5.1 bitcast_reduce_fusion
  136.6 5.1 collective-permute-start.1
  162.1 6.8 %fusion.24 = (f32[16,16384]{1,0:T(8,128)S(1)}, f32[16,16384]{1,0:T(8,128)S(1)}) fusion(f32[16,16384]{1,0:T(8,128)} %reshape.319, f32[16,16384]{1,0:T(8,128)} %reshape.318, f32[16384]{0:T(1024)S(1)} %get-tuple-element.225, f32[16384]{0:T(1024)S(1)} %get-tuple-element.224, f32[16]{0:T(128)S(1)} %copy-done.9), kind=kLoop, calls=%fused_computation.46 | loop fusion | flops 2359296 | bytes 4325440 | tf_op jit(solution)/shard_map/mul | solution.py:130
  169.1 4.7 copy.152
  174.5 87.7 %scatter_custom_fusion = f32[32,1024]{0,1:T(8,128)S(1)} fusion(s32[16384]{0:T(1024)} %bitcast.30, f32[16384,32]{1,0:T(8,128)} %copy.152, f32[]{:T(128)} %constant.96.clone.1), kind=kCustom, calls=%fused_computation.59 | custom fusion | flops 524288 | bytes 131584 | tf_op jit(solution)/shard_map/scatter-add | solution.py:133
  268.4 13.9 %collective-permute-done.5 = f32[33,1024]{0,1:T(8,128)S(1)} collective-permute-done((f32[33,1024]{0,1:T(8,128)S(1)}, f32[33,1024]{0,1:T(8,128)S(1)}, u32[]{:S(2)}, u32[]{:S(2)}) %collective-permute-start.5) | collective-permute-done | bytes 135200 | tf_op jit(solution)/shard_map/ppermute | solution.py:78
  284.5 25.0 %collective-permute-done.6 = f32[33,1024]{0,1:T(8,128)S(1)} collective-permute-done((f32[33,1024]{0,1:T(8,128)S(1)}, f32[33,1024]{0,1:T(8,128)S(1)}, u32[]{:S(2)}, u32[]{:S(2)}) %collective-permute-start.6) | collective-permute-done | bytes 135200 | tf_op jit(solution)/shard_map/ppermute | solution.py:78
  312.7 57.8 %collective-permute-done.7 = f32[33,1024]{0,1:T(8,128)S(1)} collective-permute-done((f32[33,1024]{0,1:T(8,128)S(1)}, f32[33,1024]{0,1:T(8,128)S(1)}, u32[]{:S(2)}, u32[]{:S(2)}) %collective-permute-start.7) | collective-permute-done | bytes 135200 | tf_op jit(solution)/shard_map/ppermute | solution.py:78
  370.5 8.0 %collective-permute-start.8 = (f32[33,1024]{0,1:T(8,128)S(1)}, f32[33,1024]{0,1:T(8,128)S(1)}, u32[]{:S(2)}, u32[]{:S(2)}) collective-permute-start(f32[33,1024]{0,1:T(8,128)S(1)} %add.235), channel_id=1, source_target_pairs={{0,256},{16,272},{32,288},{48,304},{64,320},{80,336},{96,352},{112... | collective-permute-start | bytes 405512 | tf_op jit(solution)/shard_map/ppermute | solution.py:78
  379.2 19.8 %collective-permute-done.8 = f32[33,1024]{0,1:T(8,128)S(1)} collective-permute-done((f32[33,1024]{0,1:T(8,128)S(1)}, f32[33,1024]{0,1:T(8,128)S(1)}, u32[]{:S(2)}, u32[]{:S(2)}) %collective-permute-start.8) | collective-permute-done | bytes 135200 | tf_op jit(solution)/shard_map/ppermute | solution.py:78
  401.4 23.9 %all_gather.7 = f32[67,512]{0,1:T(8,128)S(1)} all-gather(f32[67,32]{0,1:T(8,128)S(1)} %pad_maximum_fusion.5), channel_id=1, replica_groups=mesh['row'=32,'col'=16] {'col'}, dimensions={1}, use_global_device_ids=true | all-gather | bytes 145792 | tf_op jit(solution)/shard_map/all_gather | solution.py:143
  425.8 160.5 %while.11 = (s32[]{:T(128)}, f32[3,512]{1,0:T(4,128)S(1)}, f32[32,512]{1,0:T(8,128)S(1)}, s32[8]{0:T(128)S(1)}, f32[32,1024]{1,0:T(8,128)S(1)}, /*index=5*/f32[3...) while((s32[]{:T(128)}, f32[3,512]{1,0:T(4,128)S(1)}, ...), condition=%wide.region_9.10_spmd.clone, body=%wide.region_5.9_spmd.clone.sunk | while | flops 28640776 | bytes 3418409 | solution.py:57
  427.3 18.4 %fusion.55 = f32[128,512]{1,0:T(8,128)S(1)} fusion(f32[128,512]{1,0:T(8,128)S(1)} %get-tuple-element.299, f32[128,512]{1,0:T(8,128)S(1)} %get-tuple-element.300, f32[16]{0:T(128)S(1)} %get-tuple-element.346, f32[16,512]{1,0:T(8,128)S(1)} %get-tuple-element.301, f32[16,128]{1,0:T(8,128)S(1)} %get-tuple-element.302, ...), kind=kLoop, calls=%fused_computation.12.clone.1 | loop fusion | flops 27197440 | bytes 950336 | tf_op jit(solution)/shard_map/while/body/eval_jaxpr/reduce_sum | solution.py:37
  447.4 18.4 %fusion.55 = f32[128,512]{1,0:T(8,128)S(1)} fusion(f32[128,512]{1,0:T(8,128)S(1)} %get-tuple-element.299, f32[128,512]{1,0:T(8,128)S(1)} %get-tuple-element.300, f32[16]{0:T(128)S(1)} %get-tuple-element.346, f32[16,512]{1,0:T(8,128)S(1)} %get-tuple-element.301, f32[16,128]{1,0:T(8,128)S(1)} %get-tuple-element.302, ...), kind=kLoop, calls=%fused_computation.12.clone.1 | loop fusion | flops 27197440 | bytes 950336 | tf_op jit(solution)/shard_map/while/body/eval_jaxpr/reduce_sum | solution.py:37
  467.4 18.4 %fusion.55 = f32[128,512]{1,0:T(8,128)S(1)} fusion(f32[128,512]{1,0:T(8,128)S(1)} %get-tuple-element.299, f32[128,512]{1,0:T(8,128)S(1)} %get-tuple-element.300, f32[16]{0:T(128)S(1)} %get-tuple-element.346, f32[16,512]{1,0:T(8,128)S(1)} %get-tuple-element.301, f32[16,128]{1,0:T(8,128)S(1)} %get-tuple-element.302, ...), kind=kLoop, calls=%fused_computation.12.clone.1 | loop fusion | flops 27197440 | bytes 950336 | tf_op jit(solution)/shard_map/while/body/eval_jaxpr/reduce_sum | solution.py:37
  487.5 18.4 %fusion.55 = f32[128,512]{1,0:T(8,128)S(1)} fusion(f32[128,512]{1,0:T(8,128)S(1)} %get-tuple-element.299, f32[128,512]{1,0:T(8,128)S(1)} %get-tuple-element.300, f32[16]{0:T(128)S(1)} %get-tuple-element.346, f32[16,512]{1,0:T(8,128)S(1)} %get-tuple-element.301, f32[16,128]{1,0:T(8,128)S(1)} %get-tuple-element.302, ...), kind=kLoop, calls=%fused_computation.12.clone.1 | loop fusion | flops 27197440 | bytes 950336 | tf_op jit(solution)/shard_map/while/body/eval_jaxpr/reduce_sum | solution.py:37
  507.6 18.4 %fusion.55 = f32[128,512]{1,0:T(8,128)S(1)} fusion(f32[128,512]{1,0:T(8,128)S(1)} %get-tuple-element.299, f32[128,512]{1,0:T(8,128)S(1)} %get-tuple-element.300, f32[16]{0:T(128)S(1)} %get-tuple-element.346, f32[16,512]{1,0:T(8,128)S(1)} %get-tuple-element.301, f32[16,128]{1,0:T(8,128)S(1)} %get-tuple-element.302, ...), kind=kLoop, calls=%fused_computation.12.clone.1 | loop fusion | flops 27197440 | bytes 950336 | tf_op jit(solution)/shard_map/while/body/eval_jaxpr/reduce_sum | solution.py:37
  527.6 18.4 %fusion.55 = f32[128,512]{1,0:T(8,128)S(1)} fusion(f32[128,512]{1,0:T(8,128)S(1)} %get-tuple-element.299, f32[128,512]{1,0:T(8,128)S(1)} %get-tuple-element.300, f32[16]{0:T(128)S(1)} %get-tuple-element.346, f32[16,512]{1,0:T(8,128)S(1)} %get-tuple-element.301, f32[16,128]{1,0:T(8,128)S(1)} %get-tuple-element.302, ...), kind=kLoop, calls=%fused_computation.12.clone.1 | loop fusion | flops 27197440 | bytes 950336 | tf_op jit(solution)/shard_map/while/body/eval_jaxpr/reduce_sum | solution.py:37
  547.7 18.4 %fusion.55 = f32[128,512]{1,0:T(8,128)S(1)} fusion(f32[128,512]{1,0:T(8,128)S(1)} %get-tuple-element.299, f32[128,512]{1,0:T(8,128)S(1)} %get-tuple-element.300, f32[16]{0:T(128)S(1)} %get-tuple-element.346, f32[16,512]{1,0:T(8,128)S(1)} %get-tuple-element.301, f32[16,128]{1,0:T(8,128)S(1)} %get-tuple-element.302, ...), kind=kLoop, calls=%fused_computation.12.clone.1 | loop fusion | flops 27197440 | bytes 950336 | tf_op jit(solution)/shard_map/while/body/eval_jaxpr/reduce_sum | solution.py:37
  567.8 18.4 %fusion.55 = f32[128,512]{1,0:T(8,128)S(1)} fusion(f32[128,512]{1,0:T(8,128)S(1)} %get-tuple-element.299, f32[128,512]{1,0:T(8,128)S(1)} %get-tuple-element.300, f32[16]{0:T(128)S(1)} %get-tuple-element.346, f32[16,512]{1,0:T(8,128)S(1)} %get-tuple-element.301, f32[16,128]{1,0:T(8,128)S(1)} %get-tuple-element.302, ...), kind=kLoop, calls=%fused_computation.12.clone.1 | loop fusion | flops 27197440 | bytes 950336 | tf_op jit(solution)/shard_map/while/body/eval_jaxpr/reduce_sum | solution.py:37
  586.6 11.5 %scatter_custom_fusion.1 = f32[3,512]{0,1:T(8,128)S(1)} fusion(s32[2048]{0:T(1024)S(1)} %bitcast.32, f32[2048,3]{1,0:T(8,128)S(1)} %bitcast.28, f32[]{:T(128)} %constant.96.clone.1), kind=kCustom, calls=%fused_computation.74 | custom fusion | flops 6144 | bytes 6148 | tf_op jit(solution)/shard_map/scatter-add | solution.py:154
  600.2 8.5 %collective-permute-done.9 = f32[3,512]{0,1:T(8,128)S(1)} collective-permute-done((f32[3,512]{0,1:T(8,128)S(1)}, f32[3,512]{0,1:T(8,128)S(1)}, u32[]{:S(2)}, u32[]{:S(2)}) %collective-permute-start.9) | collective-permute-done | bytes 6176 | tf_op jit(solution)/shard_map/ppermute | solution.py:78
  610.7 7.8 %collective-permute-done.10 = f32[3,512]{0,1:T(8,128)S(1)} collective-permute-done((f32[3,512]{0,1:T(8,128)S(1)}, f32[3,512]{0,1:T(8,128)S(1)}, u32[]{:S(2)}, u32[]{:S(2)}) %collective-permute-start.10) | collective-permute-done | bytes 6176 | tf_op jit(solution)/shard_map/ppermute | solution.py:78
  620.9 7.0 %collective-permute-done.11 = f32[3,512]{0,1:T(8,128)S(1)} collective-permute-done((f32[3,512]{0,1:T(8,128)S(1)}, f32[3,512]{0,1:T(8,128)S(1)}, u32[]{:S(2)}, u32[]{:S(2)}) %collective-permute-start.11) | collective-permute-done | bytes 6176 | tf_op jit(solution)/shard_map/ppermute | solution.py:78
  632.0 5.7 collective-permute-done.12
  (172 shorter events, 69.9 us)
Async XLA Ops:
  1.8 101.2 %copy-start.1 = (s32[16384]{0:T(1024)}, s32[16384]{0:T(1024)S(1)}, u32[]{:S(2)}) copy-start(s32[16384]{0:T(1024)S(1)} %reshape.315) | copy-start | bytes 196612
  3.4 94.4 %copy-start.4 = (f32[32,32]{0,1:T(8,128)}, f32[32,32]{0,1:T(8,128)S(1)}, u32[]{:S(2)}) copy-start(f32[32,32]{0,1:T(8,128)S(1)} %copy.145) | copy-start | bytes 12292
  42.7 0.6 copy-start.3
  105.5 1.0 copy-start
  105.5 1.2 copy-start.2
  105.5 1.3 copy-start.9
  125.6 31.4 %copy-start.7 = (f32[32,256]{1,0:T(8,128)S(1)}, f32[32,256]{1,0:T(8,128)}, u32[]{:S(2)}) copy-start(f32[32,256]{1,0:T(8,128)} %param.15) | copy-start | bytes 98308
  130.7 5.8 collective-permute-start
  136.6 7.3 %collective-permute-start.1 = (f32[32,256]{1,0:T(8,128)S(1)}, f32[32,256]{1,0:T(8,128)S(1)}, u32[]{:S(2)}, u32[]{:S(2)}) collective-permute-start(f32[32,256]{1,0:T(8,128)S(1)} %fusion.43), channel_id=1, source_target_pairs={{0,2},{1,3},{2,0},{3,1},{4,6},{5,7},{6,4},{7,5},{8,10},{9,11},{10,... | collective-permute-start | bytes 98312 | tf_op jit(solution)/shard_map/ppermute | solution.py:78
  143.9 5.8 collective-permute-start.2
  149.7 7.3 %collective-permute-start.3 = (f32[32,256]{1,0:T(8,128)S(1)}, f32[32,256]{1,0:T(8,128)S(1)}, u32[]{:S(2)}, u32[]{:S(2)}) collective-permute-start(f32[32,256]{1,0:T(8,128)S(1)} %add.229), channel_id=1, source_target_pairs={{0,8},{1,9},{2,10},{3,11},{4,12},{5,13},{6,14},{7,15},{8,0},{9,1},... | collective-permute-start | bytes 98312 | tf_op jit(solution)/shard_map/ppermute | solution.py:78
  173.8 138.9 %copy-start.8 = (s32[4,512]{1,0:T(4,128)S(1)}, s32[4,512]{1,0:T(4,128)}, u32[]{:S(2)}) copy-start(s32[4,512]{1,0:T(4,128)} %param.17) | copy-start | bytes 24580
  262.4 3.8 collective-permute-start.4
  266.4 15.9 %collective-permute-start.5 = (f32[33,1024]{0,1:T(8,128)S(1)}, f32[33,1024]{0,1:T(8,128)S(1)}, u32[]{:S(2)}, u32[]{:S(2)}) collective-permute-start(f32[33,1024]{0,1:T(8,128)S(1)} %fusion.48), channel_id=1, source_target_pairs={{0,32},{16,48},{32,0},{48,16},{64,96},{80,112},{96,64},{112,80},{1... | collective-permute-start | bytes 405512 | tf_op jit(solution)/shard_map/ppermute | solution.py:78
  282.4 27.2 %collective-permute-start.6 = (f32[33,1024]{0,1:T(8,128)S(1)}, f32[33,1024]{0,1:T(8,128)S(1)}, u32[]{:S(2)}, u32[]{:S(2)}) collective-permute-start(f32[33,1024]{0,1:T(8,128)S(1)} %add.233), channel_id=1, source_target_pairs={{0,64},{16,80},{32,96},{48,112},{64,0},{80,16},{96,32},{112,48},{1... | collective-permute-start | bytes 405512 | tf_op jit(solution)/shard_map/ppermute | solution.py:78
  309.6 60.9 %collective-permute-start.7 = (f32[33,1024]{0,1:T(8,128)S(1)}, f32[33,1024]{0,1:T(8,128)S(1)}, u32[]{:S(2)}, u32[]{:S(2)}) collective-permute-start(f32[33,1024]{0,1:T(8,128)S(1)} %add.234), channel_id=1, source_target_pairs={{0,128},{16,144},{32,160},{48,176},{64,192},{80,208},{96,224},{112... | collective-permute-start | bytes 405512 | tf_op jit(solution)/shard_map/ppermute | solution.py:78
  370.5 28.4 %collective-permute-start.8 = (f32[33,1024]{0,1:T(8,128)S(1)}, f32[33,1024]{0,1:T(8,128)S(1)}, u32[]{:S(2)}, u32[]{:S(2)}) collective-permute-start(f32[33,1024]{0,1:T(8,128)S(1)} %add.235), channel_id=1, source_target_pairs={{0,256},{16,272},{32,288},{48,304},{64,320},{80,336},{96,352},{112... | collective-permute-start | bytes 405512 | tf_op jit(solution)/shard_map/ppermute | solution.py:78
  378.8 22.5 %copy-start.5 = (f32[32,32]{0,1:T(8,128)S(1)}, f32[32,32]{0,1:T(8,128)}, u32[]{:S(2)}) copy-start(f32[32,32]{0,1:T(8,128)} %copy-done.4) | copy-start | bytes 12292
  401.2 24.6 %copy-start.6 = (f32[32,32]{1,0:T(8,128)}, f32[32,32]{1,0:T(8,128)S(1)}, u32[]{:S(2)}) copy-start(f32[32,32]{1,0:T(8,128)S(1)} %fusion.42) | copy-start | bytes 12292
  598.2 10.6 %collective-permute-start.9 = (f32[3,512]{0,1:T(8,128)S(1)}, f32[3,512]{0,1:T(8,128)S(1)}, u32[]{:S(2)}, u32[]{:S(2)}) collective-permute-start(f32[3,512]{0,1:T(8,128)S(1)} %scatter_custom_fusion.1), channel_id=1, source_target_pairs={{0,1},{1,0},{2,3},{3,2},{4,5},{5,4},{6,7},{7,6},{8,9},{9,8},{10,11... | collective-permute-start | bytes 18440 | tf_op jit(solution)/shard_map/ppermute | solution.py:78
  608.8 9.8 %collective-permute-start.10 = (f32[3,512]{0,1:T(8,128)S(1)}, f32[3,512]{0,1:T(8,128)S(1)}, u32[]{:S(2)}, u32[]{:S(2)}) collective-permute-start(f32[3,512]{0,1:T(8,128)S(1)} %add.243), channel_id=1, source_target_pairs={{0,2},{1,3},{2,0},{3,1},{4,6},{5,7},{6,4},{7,5},{8,10},{9,11},{10,... | collective-permute-start | bytes 18440 | tf_op jit(solution)/shard_map/ppermute | solution.py:78
  618.6 9.3 %collective-permute-start.11 = (f32[3,512]{0,1:T(8,128)S(1)}, f32[3,512]{0,1:T(8,128)S(1)}, u32[]{:S(2)}, u32[]{:S(2)}) collective-permute-start(f32[3,512]{0,1:T(8,128)S(1)} %add.244), channel_id=1, source_target_pairs={{0,4},{1,5},{2,6},{3,7},{4,0},{5,1},{6,2},{7,3},{8,12},{9,13},{10,... | collective-permute-start | bytes 18440 | tf_op jit(solution)/shard_map/ppermute | solution.py:78
  627.9 9.8 %collective-permute-start.12 = (f32[3,512]{0,1:T(8,128)S(1)}, f32[3,512]{0,1:T(8,128)S(1)}, u32[]{:S(2)}, u32[]{:S(2)}) collective-permute-start(f32[3,512]{0,1:T(8,128)S(1)} %add.245), channel_id=1, source_target_pairs={{0,8},{1,9},{2,10},{3,11},{4,12},{5,13},{6,14},{7,15},{8,0},{9,1},... | collective-permute-start | bytes 18440 | tf_op jit(solution)/shard_map/ppermute | solution.py:78

commit v3 on v2

--- a/solution.py
+++ b/solution.py
@@ -3,6 +3,7 @@
 import jax
 import jax.numpy as jnp
 from jax import lax
+from jax.experimental.layout import Layout, with_layout_constraint
 from jax.sharding import PartitionSpec as P
 
 SOFT = 1.0
@@ -70,14 +71,42 @@
     )
 
 
+def row_major(value):
+    return with_layout_constraint(value, Layout(tuple(range(value.ndim))))
+
+
 def xor_psum(value, axis):
     count = lax.axis_size(axis)
     shift = 1
     while shift < count:
         partner = [(index, index ^ shift) for index in range(count)]
+        value = row_major(value)
         value = value + lax.ppermute(value, axis, partner)
         shift *= 2
     return value
+
+
+def halving_scatter(value, axis):
+    count = lax.axis_size(axis)
+    me = lax.axis_index(axis)
+    shift = 1
+    while shift < count:
+        half = value.shape[1] // 2
+        low, high = value[:, :half], value[:, half:]
+        upper = (me // shift) % 2 == 1
+        keep = jnp.where(upper, high, low)
+        send = row_major(jnp.where(upper, low, high))
+        partner = [(index, index ^ shift) for index in range(count)]
+        value = keep + lax.ppermute(send, axis, partner)
+        shift *= 2
+    return value
+
+
+def bit_reverse(value, bits):
+    result = jnp.zeros_like(value)
+    for bit in range(bits):
+        result = result | (((value >> bit) & 1) << (bits - 1 - bit))
+    return result
 
 
 def on_device(centroids, strengths, self_inv, wavenumbers, field_pos, targets, lists, connect):
@@ -100,9 +129,11 @@
     source_count = src_all.shape[1]
     panel_ids = lists.reshape(-1)
     owner_block = panel_ids // owned_count
+    owner_row = owner_block // col_count
     mask = (owner_block % col_count == col_index).astype(jnp.float32)
-    local_ids = owner_block // col_count * owned_count + panel_ids % owned_count
-    near_all = jnp.take(src_all[: pos_rows + str_rows], local_ids, axis=1)
+    local_ids = owner_row * owned_count + panel_ids % owned_count
+    table = jnp.transpose(src_all[: pos_rows + str_rows])
+    near_all = jnp.transpose(jnp.take(table, local_ids, axis=0))
     near = near_all[:pos_rows]
     observer = jnp.repeat(field_pos, listed, axis=1)
     offset = observer - near
@@ -130,16 +161,20 @@
     term_real = (cosine * rep_real + sine * rep_imag) * inverse
     term_imag = (cosine * rep_imag - sine * rep_real) * inverse
     terms = jnp.concatenate([term_real, term_imag], axis=0)
-    source_part = jnp.zeros((2 * freqs, source_count), jnp.float32).at[:, local_ids].add(terms)
+    row_bits = max(row_count - 1, 0).bit_length()
+    slot_ids = bit_reverse(owner_row, row_bits) * owned_count + panel_ids % owned_count
+    source_part = jnp.zeros((source_count, 2 * freqs), jnp.float32).at[slot_ids].add(
+        jnp.transpose(terms)
+    )
     misfit_part = jnp.sum(resid * resid)
-    misfit_row = jnp.where(
-        lax.broadcasted_iota(jnp.int32, (1, source_count), 1) == 0, misfit_part, 0.0
-    )
-    packed = xor_psum(jnp.concatenate([source_part, misfit_row], axis=0), "row")
+    misfit_row = jnp.full((1, source_count), misfit_part, jnp.float32)
+    packed = halving_scatter(
+        jnp.concatenate([jnp.transpose(source_part), misfit_row], axis=0), "row"
+    )
     objective = packed[2 * freqs, 0] / (freqs * field_total) + 1e-06
-    source_all = packed[: 2 * freqs] / objective
-    mu_all = complex_times(source_all, src_inv, freqs)
-    mu_own = lax.dynamic_slice_in_dim(mu_all, row_index * owned_count, owned_count, 1)
+    source_own = packed[: 2 * freqs] / objective
+    mu_own = complex_times(source_own, self_inv, freqs)
+    mu_all = lax.all_gather(mu_own, "row", axis=1, tiled=True)
     tgt_all = lax.all_gather(
         jnp.concatenate([centroids, strengths, mu_own], axis=0), "col", axis=1, tiled=True
     )
@@ -154,9 +189,10 @@
     vertex_part = jnp.zeros((3, block_width), jnp.float32).at[:, vertex_local.reshape(-1)].add(
         jnp.tile(0.25 * panel_sens, (1, connect.shape[0]))
     )
-    vertex_own = lax.dynamic_slice_in_dim(
-        xor_psum(vertex_part, "col"), col_index * owned_count, owned_count, 1
-    )
+    lanes = 128 if block_width % 128 == 0 else block_width
+    vertex_rows = vertex_part.reshape(3 * block_width // lanes, lanes)
+    vertex_sum = xor_psum(vertex_rows, "col").reshape(3, block_width)
+    vertex_own = lax.dynamic_slice_in_dim(vertex_sum, col_index * owned_count, owned_count, 1)
     adjoint = mu_own
     return (adjoint, vertex_own, objective)
 

time: 652 us -> 558 us (0.86); the launches traced: 639 us -> 556 us
  waiting for transfers between devices: 159 us -> 47 us
  blocking collectives: 61.6 us -> 89.9 us
    ppermute x13 -> x8, waiting for transfers between devices: 159 us -> 24.5 us  [xor_psum(): value = value + lax.ppermute(value, axis, partner)]
    all_gather x0 -> x1, blocking collectives: none -> 28.5 us  [on_device(): mu_all = lax.all_gather(mu_own, 'row', axis=1, tiled=True)]
    ppermute x0 -> x5, waiting for transfers between devices: none -> 22.5 us  [halving_scatter(): value = keep + lax.ppermute(send, axis, partner)]
    ppermute x0 -> x5, starting transfers between devices: none -> 16.3 us  [halving_scatter(): value = keep + lax.ppermute(send, axis, partner)]
    ppermute x13 -> x8, starting transfers between devices: 42.1 us -> 26.3 us  [xor_psum(): value = value + lax.ppermute(value, axis, partner)]
where the time goes in v3:
time: 558 us; the launch traced here: 556 us
  other arithmetic  278 us (50%)
  local copies, waits for them, and re-layouts  91 us (16%)
  blocking collectives  89.9 us (16%)
  waiting for transfers between devices  47 us (8%)
  starting transfers between devices  42.6 us (8%)
    reduce_sum x8, other arithmetic, pair_block(): jnp.sum(prod_real * deriv_real - prod_imag * deriv_imag, axis=0) * inverse  147 us
    scatter-add x1, other arithmetic, on_device(): jnp.zeros((source_count, 2 * freqs), jnp.float32).at[slot_ids]  87.7 us
    gather x2, local copies, waits for them, and re-layouts, on_device(): near_all = jnp.transpose(jnp.take(table, local_ids, axis=0))  59.7 us
    all_gather x1, blocking collectives, on_device(): src_all = lax.all_gather(owned, 'row', axis=1, tiled=True)  37.6 us
    all_gather x1, blocking collectives, on_device(): mu_all = lax.all_gather(mu_own, 'row', axis=1, tiled=True)  28.5 us
    ppermute x8, starting transfers between devices, xor_psum(): value = value + lax.ppermute(value, axis, partner)  26.3 us
    ppermute x8, waiting for transfers between devices, xor_psum(): value = value + lax.ppermute(value, axis, partner)  24.5 us
    all_gather x1, blocking collectives, on_device(): lax.all_gather(jnp.concatenate([centroids, strengths, mu_own], axis=0), '...  23.7 us
  transfers between devices with their start and end apart: 13, of which 13 were waited for; matrix products, arithmetic and copies ran while one was open for 0% of the time, Pallas kernels for 0%

profile of v3, /device:TPU:6, one launch (start us, length us, event | category | flops | bytes accessed | tf_op | source)
XLA Modules:
  0.0 556.2 jit_solution(17398415569482956762)
XLA Ops:
  7.5 37.6 %all_gather.9 = f32[67,1024]{0,1:T(8,128)S(1)} all-gather(f32[67,32]{0,1:T(8,128)S(1)} %pad_maximum_fusion.1), channel_id=1, replica_groups=mesh['row'=32,'col'=16] {'row'}, dimensions={1}, use_global_device_ids=true | all-gather | bytes 283008 | tf_op jit(solution)/shard_map/all_gather | solution.py:125
  45.1 54.4 %gather_fusion = f32[16384,35]{1,0:T(8,128)} fusion(f32[1024,35]{1,0:T(8,128)S(1)} %slice_bitcast_fusion, s32[16384]{0:T(1024)S(1)} %broadcast_clamp_fusion), kind=kCustom, calls=%fused_computation | custom fusion | bytes 4653056 | tf_op jit(solution)/shard_map/jit(_take)/gather | solution.py:136
  99.6 5.3 copy.119
  106.1 4.4 fusion.20
  110.5 4.6 copy.139
  115.1 5.0 bitcast_reduce_fusion.1
  120.2 4.6 copy.140
  124.9 5.1 bitcast_reduce_fusion
  135.8 5.1 collective-permute-start.1
  161.4 6.8 %fusion.24 = (f32[16,16384]{1,0:T(8,128)S(1)}, f32[16,16384]{1,0:T(8,128)S(1)}) fusion(f32[16,16384]{1,0:T(8,128)} %reshape.401, f32[16,16384]{1,0:T(8,128)} %reshape.400, f32[16384]{0:T(1024)S(1)} %get-tuple-element.195, f32[16384]{0:T(1024)S(1)} %get-tuple-element.194, f32[16]{0:T(128)S(1)} %copy-done.8), kind=kLoop, calls=%fused_computation.46 | loop fusion | flops 2359296 | bytes 4325440 | tf_op jit(solution)/shard_map/mul | solution.py:161
  168.4 4.7 copy.124
  173.1 87.7 %scatter_custom_fusion = f32[1024,32]{1,0:T(8,128)S(1)} fusion(s32[16384]{0:T(1024)S(1)} %bitcast.34, f32[16384,32]{1,0:T(8,128)} %copy.124, f32[]{:T(128)} %constant.181.clone.1), kind=kCustom, calls=%fused_computation.55 | custom fusion | flops 524288 | bytes 131584 | tf_op jit(solution)/shard_map/scatter-add | solution.py:166
  267.5 3.9 collective-permute-done.5
  273.7 4.4 collective-permute-done.6
  281.2 6.4 %collective-permute-done.7 = f32[33,64]{1,0:T(8,128)S(1)} collective-permute-done((f32[33,64]{1,0:T(8,128)S(1)}, f32[33,64]{1,0:T(8,128)S(1)}, u32[]{:S(2)}, u32[]{:S(2)}) %collective-permute-start.7) | collective-permute-done | bytes 8480 | tf_op jit(solution)/shard_map/ppermute | solution.py:100
  287.8 7.3 %collective-permute-start.8 = (f32[33,32]{1,0:T(8,128)S(1)}, f32[33,32]{1,0:T(8,128)S(1)}, u32[]{:S(2)}, u32[]{:S(2)}) collective-permute-start(f32[33,32]{1,0:T(8,128)S(1)} %slice_select_fusion.1), channel_id=1, source_target_pairs={{0,256},{16,272},{32,288},{48,304},{64,320},{80,336},{96,352},{112... | collective-permute-start | bytes 12680 | tf_op jit(solution)/shard_map/ppermute | solution.py:100
  295.7 6.5 %collective-permute-done.8 = f32[33,32]{1,0:T(8,128)S(1)} collective-permute-done((f32[33,32]{1,0:T(8,128)S(1)}, f32[33,32]{1,0:T(8,128)S(1)}, u32[]{:S(2)}, u32[]{:S(2)}) %collective-permute-start.8) | collective-permute-done | bytes 4256 | tf_op jit(solution)/shard_map/ppermute | solution.py:100
  303.8 23.7 %all_gather.10 = f32[67,512]{0,1:T(8,128)S(1)} all-gather(f32[67,32]{0,1:T(8,128)S(1)} %pad_maximum_fusion.4), channel_id=1, replica_groups=mesh['row'=32,'col'=16] {'col'}, dimensions={1}, use_global_device_ids=true | all-gather | bytes 145792 | tf_op jit(solution)/shard_map/all_gather | solution.py:178
  327.8 28.5 %all_gather.11 = f32[32,1024]{0,1:T(8,128)S(1)} all-gather(f32[32,32]{0,1:T(8,128)S(1)} %copy.130), channel_id=1, replica_groups=mesh['row'=32,'col'=16] {'row'}, dimensions={1}, use_global_device_ids=true | all-gather | bytes 135168 | tf_op jit(solution)/shard_map/all_gather | solution.py:177
  356.8 160.5 %while.11 = (s32[]{:T(128)}, f32[3,512]{1,0:T(4,128)S(1)}, f32[32,512]{1,0:T(8,128)S(1)}, s32[8]{0:T(128)S(1)}, f32[32,1024]{1,0:T(8,128)S(1)}, /*index=5*/f32[3...) while((s32[]{:T(128)}, f32[3,512]{1,0:T(4,128)S(1)}, ...), condition=%wide.region_9.10_spmd.clone, body=%wide.region_5.9_spmd.clone.sunk | while | flops 28640776 | bytes 3418417 | solution.py:58
  358.2 18.4 %fusion.51 = f32[128,512]{1,0:T(8,128)S(1)} fusion(f32[128,512]{1,0:T(8,128)S(1)} %get-tuple-element.271, f32[128,512]{1,0:T(8,128)S(1)} %get-tuple-element.272, f32[16]{0:T(128)S(1)} %get-tuple-element.318, f32[16,512]{1,0:T(8,128)S(1)} %get-tuple-element.273, f32[16,128]{1,0:T(8,128)S(1)} %get-tuple-element.274, ...), kind=kLoop, calls=%fused_computation.12.clone.1 | loop fusion | flops 27197440 | bytes 950336 | tf_op jit(solution)/shard_map/while/body/eval_jaxpr/reduce_sum | solution.py:38
  378.3 18.4 %fusion.51 = f32[128,512]{1,0:T(8,128)S(1)} fusion(f32[128,512]{1,0:T(8,128)S(1)} %get-tuple-element.271, f32[128,512]{1,0:T(8,128)S(1)} %get-tuple-element.272, f32[16]{0:T(128)S(1)} %get-tuple-element.318, f32[16,512]{1,0:T(8,128)S(1)} %get-tuple-element.273, f32[16,128]{1,0:T(8,128)S(1)} %get-tuple-element.274, ...), kind=kLoop, calls=%fused_computation.12.clone.1 | loop fusion | flops 27197440 | bytes 950336 | tf_op jit(solution)/shard_map/while/body/eval_jaxpr/reduce_sum | solution.py:38
  398.3 18.4 %fusion.51 = f32[128,512]{1,0:T(8,128)S(1)} fusion(f32[128,512]{1,0:T(8,128)S(1)} %get-tuple-element.271, f32[128,512]{1,0:T(8,128)S(1)} %get-tuple-element.272, f32[16]{0:T(128)S(1)} %get-tuple-element.318, f32[16,512]{1,0:T(8,128)S(1)} %get-tuple-element.273, f32[16,128]{1,0:T(8,128)S(1)} %get-tuple-element.274, ...), kind=kLoop, calls=%fused_computation.12.clone.1 | loop fusion | flops 27197440 | bytes 950336 | tf_op jit(solution)/shard_map/while/body/eval_jaxpr/reduce_sum | solution.py:38
  418.4 18.4 %fusion.51 = f32[128,512]{1,0:T(8,128)S(1)} fusion(f32[128,512]{1,0:T(8,128)S(1)} %get-tuple-element.271, f32[128,512]{1,0:T(8,128)S(1)} %get-tuple-element.272, f32[16]{0:T(128)S(1)} %get-tuple-element.318, f32[16,512]{1,0:T(8,128)S(1)} %get-tuple-element.273, f32[16,128]{1,0:T(8,128)S(1)} %get-tuple-element.274, ...), kind=kLoop, calls=%fused_computation.12.clone.1 | loop fusion | flops 27197440 | bytes 950336 | tf_op jit(solution)/shard_map/while/body/eval_jaxpr/reduce_sum | solution.py:38
  438.5 18.4 %fusion.51 = f32[128,512]{1,0:T(8,128)S(1)} fusion(f32[128,512]{1,0:T(8,128)S(1)} %get-tuple-element.271, f32[128,512]{1,0:T(8,128)S(1)} %get-tuple-element.272, f32[16]{0:T(128)S(1)} %get-tuple-element.318, f32[16,512]{1,0:T(8,128)S(1)} %get-tuple-element.273, f32[16,128]{1,0:T(8,128)S(1)} %get-tuple-element.274, ...), kind=kLoop, calls=%fused_computation.12.clone.1 | loop fusion | flops 27197440 | bytes 950336 | tf_op jit(solution)/shard_map/while/body/eval_jaxpr/reduce_sum | solution.py:38
  458.5 18.4 %fusion.51 = f32[128,512]{1,0:T(8,128)S(1)} fusion(f32[128,512]{1,0:T(8,128)S(1)} %get-tuple-element.271, f32[128,512]{1,0:T(8,128)S(1)} %get-tuple-element.272, f32[16]{0:T(128)S(1)} %get-tuple-element.318, f32[16,512]{1,0:T(8,128)S(1)} %get-tuple-element.273, f32[16,128]{1,0:T(8,128)S(1)} %get-tuple-element.274, ...), kind=kLoop, calls=%fused_computation.12.clone.1 | loop fusion | flops 27197440 | bytes 950336 | tf_op jit(solution)/shard_map/while/body/eval_jaxpr/reduce_sum | solution.py:38
  478.6 18.4 %fusion.51 = f32[128,512]{1,0:T(8,128)S(1)} fusion(f32[128,512]{1,0:T(8,128)S(1)} %get-tuple-element.271, f32[128,512]{1,0:T(8,128)S(1)} %get-tuple-element.272, f32[16]{0:T(128)S(1)} %get-tuple-element.318, f32[16,512]{1,0:T(8,128)S(1)} %get-tuple-element.273, f32[16,128]{1,0:T(8,128)S(1)} %get-tuple-element.274, ...), kind=kLoop, calls=%fused_computation.12.clone.1 | loop fusion | flops 27197440 | bytes 950336 | tf_op jit(solution)/shard_map/while/body/eval_jaxpr/reduce_sum | solution.py:38
  498.7 18.4 %fusion.51 = f32[128,512]{1,0:T(8,128)S(1)} fusion(f32[128,512]{1,0:T(8,128)S(1)} %get-tuple-element.271, f32[128,512]{1,0:T(8,128)S(1)} %get-tuple-element.272, f32[16]{0:T(128)S(1)} %get-tuple-element.318, f32[16,512]{1,0:T(8,128)S(1)} %get-tuple-element.273, f32[16,128]{1,0:T(8,128)S(1)} %get-tuple-element.274, ...), kind=kLoop, calls=%fused_computation.12.clone.1 | loop fusion | flops 27197440 | bytes 950336 | tf_op jit(solution)/shard_map/while/body/eval_jaxpr/reduce_sum | solution.py:38
  517.5 11.5 %scatter_custom_fusion.1 = f32[3,512]{0,1:T(8,128)S(1)} fusion(s32[2048]{0:T(1024)S(1)} %bitcast.36, f32[2048,3]{1,0:T(8,128)S(1)} %bitcast.32, f32[]{:T(128)} %constant.181.clone.1), kind=kCustom, calls=%fused_computation.69 | custom fusion | flops 6144 | bytes 6148 | tf_op jit(solution)/shard_map/scatter-add | solution.py:189
  531.2 3.5 collective-permute-done.9
  538.1 3.7 collective-permute-done.10
  550.7 3.7 collective-permute-done.12
  (180 shorter events, 72.3 us)
Async XLA Ops:
  3.3 4.1 copy-start.1
  104.8 1.2 copy-start.7
  124.9 27.6 %copy-start = (s32[16384,1]{0,1:T(1,128)S(1)}, s32[16384,1]{0,1:T(1,128)}, u32[]{:S(2)}) copy-start(s32[16384,1]{0,1:T(1,128)} %get-tuple-element.173) | copy-start | bytes 196612
  124.9 31.4 %copy-start.5 = (f32[32,256]{1,0:T(8,128)S(1)}, f32[32,256]{1,0:T(8,128)}, u32[]{:S(2)}) copy-start(f32[32,256]{1,0:T(8,128)} %param.15) | copy-start | bytes 98308
  130.0 5.8 %collective-permute-start = (f32[32,256]{1,0:T(8,128)S(1)}, f32[32,256]{1,0:T(8,128)S(1)}, u32[]{:S(2)}, u32[]{:S(2)}) collective-permute-start(f32[32,256]{1,0:T(8,128)S(1)} %pad_maximum_fusion), channel_id=1, source_target_pairs={{0,1},{1,0},{2,3},{3,2},{4,5},{5,4},{6,7},{7,6},{8,9},{9,8},{10,11... | collective-permute-start | bytes 98312 | tf_op jit(solution)/shard_map/ppermute | solution.py:84
  135.8 7.3 %collective-permute-start.1 = (f32[32,256]{1,0:T(8,128)S(1)}, f32[32,256]{1,0:T(8,128)S(1)}, u32[]{:S(2)}, u32[]{:S(2)}) collective-permute-start(f32[32,256]{1,0:T(8,128)S(1)} %fusion.40), channel_id=1, source_target_pairs={{0,2},{1,3},{2,0},{3,1},{4,6},{5,7},{6,4},{7,5},{8,10},{9,11},{10,... | collective-permute-start | bytes 98312 | tf_op jit(solution)/shard_map/ppermute | solution.py:84
  143.1 5.8 %collective-permute-start.2 = (f32[32,256]{1,0:T(8,128)S(1)}, f32[32,256]{1,0:T(8,128)S(1)}, u32[]{:S(2)}, u32[]{:S(2)}) collective-permute-start(f32[32,256]{1,0:T(8,128)S(1)} %add.288), channel_id=1, source_target_pairs={{0,4},{1,5},{2,6},{3,7},{4,0},{5,1},{6,2},{7,3},{8,12},{9,13},{10,... | collective-permute-start | bytes 98312 | tf_op jit(solution)/shard_map/ppermute | solution.py:84
  149.0 7.3 %collective-permute-start.3 = (f32[32,256]{1,0:T(8,128)S(1)}, f32[32,256]{1,0:T(8,128)S(1)}, u32[]{:S(2)}, u32[]{:S(2)}) collective-permute-start(f32[32,256]{1,0:T(8,128)S(1)} %add.289), channel_id=1, source_target_pairs={{0,8},{1,9},{2,10},{3,11},{4,12},{5,13},{6,14},{7,15},{8,0},{9,1},... | collective-permute-start | bytes 98312 | tf_op jit(solution)/shard_map/ppermute | solution.py:84
  157.5 3.9 copy-start.8
  168.4 112.8 %copy-start.6 = (s32[4,512]{1,0:T(4,128)S(1)}, s32[4,512]{1,0:T(4,128)}, u32[]{:S(2)}) copy-start(s32[4,512]{1,0:T(4,128)} %param.17) | copy-start | bytes 24580
  173.1 130.4 %copy-start.3 = (f32[32,32]{1,0:T(8,128)S(1)}, f32[32,32]{1,0:T(8,128)}, u32[]{:S(2)}) copy-start(f32[32,32]{1,0:T(8,128)} %param.12) | copy-start | bytes 12292
  173.1 130.7 %copy-start.2 = (f32[32,32]{0,1:T(8,128)S(1)}, f32[32,32]{0,1:T(8,128)}, u32[]{:S(2)}) copy-start(f32[32,32]{0,1:T(8,128)} %copy-done.1) | copy-start | bytes 12292
  261.7 3.2 collective-permute-start.4
  265.5 5.9 %collective-permute-start.5 = (f32[33,256]{1,0:T(8,128)S(1)}, f32[33,256]{1,0:T(8,128)S(1)}, u32[]{:S(2)}, u32[]{:S(2)}) collective-permute-start(f32[33,256]{1,0:T(8,128)S(1)} %slice_select_fusion), channel_id=1, source_target_pairs={{0,32},{16,48},{32,0},{48,16},{64,96},{80,112},{96,64},{112,80},{1... | collective-permute-start | bytes 101384 | tf_op jit(solution)/shard_map/ppermute | solution.py:100
  271.5 6.6 %collective-permute-start.6 = (f32[33,128]{1,0:T(8,128)S(1)}, f32[33,128]{1,0:T(8,128)S(1)}, u32[]{:S(2)}, u32[]{:S(2)}) collective-permute-start(f32[33,128]{1,0:T(8,128)S(1)} %slice_select_fusion.3), channel_id=1, source_target_pairs={{0,64},{16,80},{32,96},{48,112},{64,0},{80,16},{96,32},{112,48},{1... | collective-permute-start | bytes 50696 | tf_op jit(solution)/shard_map/ppermute | solution.py:100
  278.1 9.6 %collective-permute-start.7 = (f32[33,64]{1,0:T(8,128)S(1)}, f32[33,64]{1,0:T(8,128)S(1)}, u32[]{:S(2)}, u32[]{:S(2)}) collective-permute-start(f32[33,64]{1,0:T(8,128)S(1)} %slice_select_fusion.2), channel_id=1, source_target_pairs={{0,128},{16,144},{32,160},{48,176},{64,192},{80,208},{96,224},{112... | collective-permute-start | bytes 25352 | tf_op jit(solution)/shard_map/ppermute | solution.py:100
  287.8 14.4 %collective-permute-start.8 = (f32[33,32]{1,0:T(8,128)S(1)}, f32[33,32]{1,0:T(8,128)S(1)}, u32[]{:S(2)}, u32[]{:S(2)}) collective-permute-start(f32[33,32]{1,0:T(8,128)S(1)} %slice_select_fusion.1), channel_id=1, source_target_pairs={{0,256},{16,272},{32,288},{48,304},{64,320},{80,336},{96,352},{112... | collective-permute-start | bytes 12680 | tf_op jit(solution)/shard_map/ppermute | solution.py:100
  303.6 53.2 %copy-start.4 = (f32[32,32]{1,0:T(8,128)}, f32[32,32]{1,0:T(8,128)S(1)}, u32[]{:S(2)}) copy-start(f32[32,32]{1,0:T(8,128)S(1)} %pad_maximum_fusion.3) | copy-start | bytes 12292
  529.2 5.5 collective-permute-start.9
  534.7 7.0 %collective-permute-start.10 = (f32[12,128]{1,0:T(8,128)S(1)}, f32[12,128]{1,0:T(8,128)S(1)}, u32[]{:S(2)}, u32[]{:S(2)}) collective-permute-start(f32[12,128]{1,0:T(8,128)S(1)} %add.302), channel_id=1, source_target_pairs={{0,2},{1,3},{2,0},{3,1},{4,6},{5,7},{6,4},{7,5},{8,10},{9,11},{10,... | collective-permute-start | bytes 18440 | tf_op jit(solution)/shard_map/ppermute | solution.py:84
  541.8 5.5 collective-permute-start.11
  547.3 7.0 %collective-permute-start.12 = (f32[12,128]{1,0:T(8,128)S(1)}, f32[12,128]{1,0:T(8,128)S(1)}, u32[]{:S(2)}, u32[]{:S(2)}) collective-permute-start(f32[12,128]{1,0:T(8,128)S(1)} %add.304), channel_id=1, source_target_pairs={{0,8},{1,9},{2,10},{3,11},{4,12},{5,13},{6,14},{7,15},{8,0},{9,1},... | collective-permute-start | bytes 18440 | tf_op jit(solution)/shard_map/ppermute | solution.py:84

commit v4 on v3

--- a/solution.py
+++ b/solution.py
@@ -7,6 +7,31 @@
 from jax.sharding import PartitionSpec as P
 
 SOFT = 1.0
+
+
+def sincos(angle):
+    quarter = jnp.round(angle * (2.0 / math.pi))
+    rest = angle - quarter * 1.5703125
+    rest = rest - quarter * 4.837512969970703125e-4
+    rest = rest - quarter * 7.54978995489188216e-8
+    rest_sq = rest * rest
+    odd = rest + rest * rest_sq * (
+        -1.6666654611e-1 + rest_sq * (8.3321608736e-3 + rest_sq * -1.9515295891e-4)
+    )
+    even = (
+        1.0
+        - 0.5 * rest_sq
+        + rest_sq
+        * rest_sq
+        * (4.166664568298827e-2 + rest_sq * (-1.388731625493765e-3 + rest_sq * 2.443315711809948e-5))
+    )
+    turn = quarter.astype(jnp.int32)
+    swap = (turn & 1) == 1
+    sine = jnp.where(swap, even, odd)
+    cosine = jnp.where(swap, odd, even)
+    sine = jnp.where((turn & 2) == 2, -sine, sine)
+    cosine = jnp.where(((turn + 1) & 2) == 2, -cosine, cosine)
+    return sine, cosine
 
 
 def pair_block(target_pos, target_str, target_mu, source_pos, source_str, source_mu, wavenumbers):
@@ -15,12 +40,8 @@
     squared = jnp.sum(offset * offset, axis=0) + SOFT
     inverse = lax.rsqrt(squared)
     distance = squared * inverse
-    inverse_sq = inverse * inverse
     phase = wavenumbers[:, None, None] * distance[None]
-    cosine = jnp.cos(phase)
-    sine = jnp.sin(phase)
-    deriv_real = -(cosine + phase * sine) * inverse_sq
-    deriv_imag = (phase * cosine - sine) * inverse_sq
+    sine, cosine = sincos(phase)
     tgt_real = target_str[:freqs, None, :]
     tgt_imag = target_str[freqs:, None, :]
     tmu_real = target_mu[:freqs, None, :]
@@ -35,7 +56,8 @@
     prod_imag = (
         tmu_real * src_imag + tmu_imag * src_real + smu_real * tgt_imag + smu_imag * tgt_real
     )
-    weight = jnp.sum(prod_real * deriv_real - prod_imag * deriv_imag, axis=0) * inverse
+    inner = cosine * (prod_real + phase * prod_imag) + sine * (phase * prod_real - prod_imag)
+    weight = -jnp.sum(inner, axis=0) * (inverse * inverse * inverse)
     return jnp.sum(weight[None] * offset, axis=1)
 
 
@@ -140,8 +162,7 @@
     distance = jnp.sqrt(jnp.sum(offset * offset, axis=0) + SOFT)
     inverse = mask / distance
     phase = wavenumbers[:, None] * distance[None]
-    cosine = jnp.cos(phase)
-    sine = jnp.sin(phase)
+    sine, cosine = sincos(phase)
     near_str = near_all[pos_rows:]
     str_real = near_str[:freqs]
     str_imag = near_str[freqs:]

time: 558 us -> 477 us (0.85)
  other arithmetic: 278 us -> 195 us
    reduce_sum x8, other arithmetic: 147 us -> 70.3 us  [pair_block(): weight = -jnp.sum(inner, axis=0) * (inverse * inverse * inverse)]
where the time goes in v4:
time: 477 us; the launch traced here: 475 us
  other arithmetic  195 us (41%)
  local copies, waits for them, and re-layouts  92 us (19%)
  blocking collectives  89.9 us (19%)
  waiting for transfers between devices  47 us (10%)
  starting transfers between devices  42.6 us (9%)
  loops' own time  6.25 us (1%)
    scatter-add x1, other arithmetic, on_device(): jnp.zeros((source_count, 2 * freqs), jnp.float32).at[slot_ids]  87.7 us
    reduce_sum x8, other arithmetic, pair_block(): weight = -jnp.sum(inner, axis=0) * (inverse * inverse * inverse)  70.3 us
    gather x2, local copies, waits for them, and re-layouts, on_device(): near_all = jnp.transpose(jnp.take(table, local_ids, axis=0))  60.1 us
    all_gather x1, blocking collectives, on_device(): src_all = lax.all_gather(owned, 'row', axis=1, tiled=True)  37.6 us
    all_gather x1, blocking collectives, on_device(): mu_all = lax.all_gather(mu_own, 'row', axis=1, tiled=True)  28.5 us
    ppermute x8, starting transfers between devices, xor_psum(): value = value + lax.ppermute(value, axis, partner)  26.3 us
    ppermute x8, waiting for transfers between devices, xor_psum(): value = value + lax.ppermute(value, axis, partner)  24.5 us
    all_gather x1, blocking collectives, on_device(): lax.all_gather(jnp.concatenate([centroids, strengths, mu_own], axis=0), '...  23.7 us
  transfers between devices with their start and end apart: 13, of which 13 were waited for; matrix products, arithmetic and copies ran while one was open for 0% of the time, Pallas kernels for 0%

profile of v4, /device:TPU:6, one launch (start us, length us, event | category | flops | bytes accessed | tf_op | source)
XLA Modules:
  0.0 475.5 jit_solution(14289917182430547294)
XLA Ops:
  7.5 37.6 %all_gather.9 = f32[67,1024]{0,1:T(8,128)S(1)} all-gather(f32[67,32]{0,1:T(8,128)S(1)} %pad_maximum_fusion.1), channel_id=1, replica_groups=mesh['row'=32,'col'=16] {'row'}, dimensions={1}, use_global_device_ids=true | all-gather | bytes 283008 | tf_op jit(solution)/shard_map/all_gather | solution.py:147
  45.1 54.8 %gather_fusion = f32[16384,35]{1,0:T(8,128)} fusion(f32[1024,35]{1,0:T(8,128)S(1)} %slice_bitcast_fusion, s32[16384]{0:T(1024)S(1)} %broadcast_clamp_fusion), kind=kCustom, calls=%fused_computation | custom fusion | bytes 4653056 | tf_op jit(solution)/shard_map/jit(_take)/gather | solution.py:158
  99.9 5.3 %copy.119 = f32[16384,35]{0,1:T(8,128)S(1)} copy(f32[16384,35]{1,0:T(8,128)} %gather_fusion) | data formatting | bytes 4587520 | tf_op jit(solution)/shard_map/jit(_take)/gather | solution.py:158
  108.3 4.6 copy.139
  112.9 5.0 %bitcast_reduce_fusion.1 = f32[16,256]{0,1:T(8,128)S(1)} fusion(f32[16,16384]{0,1:T(8,128)} %copy.139), kind=kLoop, calls=%fused_computation.57 | loop fusion | flops 258048 | bytes 1064960 | tf_op jit(solution)/shard_map/reduce_sum | solution.py:173
  118.0 4.6 copy.140
  122.7 5.1 %bitcast_reduce_fusion = f32[16,256]{0,1:T(8,128)S(1)} fusion(f32[16,16384]{0,1:T(8,128)} %copy.140), kind=kLoop, calls=%fused_computation.56 | loop fusion | flops 258048 | bytes 1064960 | tf_op jit(solution)/shard_map/reduce_sum | solution.py:174
  127.8 3.5 collective-permute-start
  133.6 5.1 %collective-permute-start.1 = (f32[32,256]{1,0:T(8,128)S(1)}, f32[32,256]{1,0:T(8,128)S(1)}, u32[]{:S(2)}, u32[]{:S(2)}) collective-permute-start(f32[32,256]{1,0:T(8,128)S(1)} %fusion.68), channel_id=1, source_target_pairs={{0,2},{1,3},{2,0},{3,1},{4,6},{5,7},{6,4},{7,5},{8,10},{9,11},{10,... | collective-permute-start | bytes 98312 | tf_op jit(solution)/shard_map/ppermute | solution.py:106
  146.8 3.5 collective-permute-start.3
  162.6 4.7 copy.124
  167.3 87.7 %scatter_custom_fusion = f32[1024,32]{1,0:T(8,128)S(1)} fusion(s32[16384]{0:T(1024)S(1)} %bitcast.34, f32[16384,32]{1,0:T(8,128)} %copy.124, f32[]{:T(128)} %constant.221.clone.1), kind=kCustom, calls=%fused_computation.104 | custom fusion | flops 524288 | bytes 131584 | tf_op jit(solution)/shard_map/scatter-add | solution.py:187
  261.7 3.9 collective-permute-done.5
  267.8 4.4 collective-permute-done.6
  275.4 6.4 %collective-permute-done.7 = f32[33,64]{1,0:T(8,128)S(1)} collective-permute-done((f32[33,64]{1,0:T(8,128)S(1)}, f32[33,64]{1,0:T(8,128)S(1)}, u32[]{:S(2)}, u32[]{:S(2)}) %collective-permute-start.7) | collective-permute-done | bytes 8480 | tf_op jit(solution)/shard_map/ppermute | solution.py:122
  282.0 7.3 %collective-permute-start.8 = (f32[33,32]{1,0:T(8,128)S(1)}, f32[33,32]{1,0:T(8,128)S(1)}, u32[]{:S(2)}, u32[]{:S(2)}) collective-permute-start(f32[33,32]{1,0:T(8,128)S(1)} %slice_select_fusion.1), channel_id=1, source_target_pairs={{0,256},{16,272},{32,288},{48,304},{64,320},{80,336},{96,352},{112... | collective-permute-start | bytes 12680 | tf_op jit(solution)/shard_map/ppermute | solution.py:122
  289.9 6.5 %collective-permute-done.8 = f32[33,32]{1,0:T(8,128)S(1)} collective-permute-done((f32[33,32]{1,0:T(8,128)S(1)}, f32[33,32]{1,0:T(8,128)S(1)}, u32[]{:S(2)}, u32[]{:S(2)}) %collective-permute-start.8) | collective-permute-done | bytes 4256 | tf_op jit(solution)/shard_map/ppermute | solution.py:122
  298.0 23.7 %all_gather.10 = f32[67,512]{0,1:T(8,128)S(1)} all-gather(f32[67,32]{0,1:T(8,128)S(1)} %pad_maximum_fusion.4), channel_id=1, replica_groups=mesh['row'=32,'col'=16] {'col'}, dimensions={1}, use_global_device_ids=true | all-gather | bytes 145792 | tf_op jit(solution)/shard_map/all_gather | solution.py:199
  322.0 28.5 %all_gather.11 = f32[32,1024]{0,1:T(8,128)S(1)} all-gather(f32[32,32]{0,1:T(8,128)S(1)} %copy.130), channel_id=1, replica_groups=mesh['row'=32,'col'=16] {'row'}, dimensions={1}, use_global_device_ids=true | all-gather | bytes 135168 | tf_op jit(solution)/shard_map/all_gather | solution.py:198
  351.0 85.6 %while.11 = (s32[]{:T(128)}, f32[3,512]{1,0:T(4,128)S(1)}, f32[16]{0:T(128)S(1)}, f32[3,512]{1,0:T(4,128)S(1)}, s32[8]{0:T(128)S(1)}, /*index=5*/f32[3,1024]{1,0...) while((s32[]{:T(128)}, f32[3,512]{1,0:T(4,128)S(1)}, ...), condition=%wide.region_9.10_spmd.clone, body=%wide.region_5.9_spmd.clone.sunk | while | flops 66520584 | bytes 2894129 | solution.py:80
  352.6 8.8 %fusion.80 = f32[128,512]{1,0:T(8,128)S(1)} fusion(f32[16,512]{1,0:T(8,128)S(1)} %get-tuple-element.267, f32[16,128]{1,0:T(8,128)S(1)} %get-tuple-element.268, f32[16,512]{1,0:T(8,128)S(1)} %get-tuple-element.269, f32[16,128]{1,0:T(8,128)S(1)} %get-tuple-element.270, f32[16,128]{1,0:T(8,128)S(1)} %get-tuple-element.271, ...), kind=kLoop, calls=%fused_computation.27.clone.1 | loop fusion | flops 64946176 | bytes 688192 | tf_op jit(solution)/shard_map/while/body/eval_jaxpr/reduce_sum | solution.py:60
  363.3 8.8 %fusion.80 = f32[128,512]{1,0:T(8,128)S(1)} fusion(f32[16,512]{1,0:T(8,128)S(1)} %get-tuple-element.267, f32[16,128]{1,0:T(8,128)S(1)} %get-tuple-element.268, f32[16,512]{1,0:T(8,128)S(1)} %get-tuple-element.269, f32[16,128]{1,0:T(8,128)S(1)} %get-tuple-element.270, f32[16,128]{1,0:T(8,128)S(1)} %get-tuple-element.271, ...), kind=kLoop, calls=%fused_computation.27.clone.1 | loop fusion | flops 64946176 | bytes 688192 | tf_op jit(solution)/shard_map/while/body/eval_jaxpr/reduce_sum | solution.py:60
  374.0 8.8 %fusion.80 = f32[128,512]{1,0:T(8,128)S(1)} fusion(f32[16,512]{1,0:T(8,128)S(1)} %get-tuple-element.267, f32[16,128]{1,0:T(8,128)S(1)} %get-tuple-element.268, f32[16,512]{1,0:T(8,128)S(1)} %get-tuple-element.269, f32[16,128]{1,0:T(8,128)S(1)} %get-tuple-element.270, f32[16,128]{1,0:T(8,128)S(1)} %get-tuple-element.271, ...), kind=kLoop, calls=%fused_computation.27.clone.1 | loop fusion | flops 64946176 | bytes 688192 | tf_op jit(solution)/shard_map/while/body/eval_jaxpr/reduce_sum | solution.py:60
  384.7 8.8 %fusion.80 = f32[128,512]{1,0:T(8,128)S(1)} fusion(f32[16,512]{1,0:T(8,128)S(1)} %get-tuple-element.267, f32[16,128]{1,0:T(8,128)S(1)} %get-tuple-element.268, f32[16,512]{1,0:T(8,128)S(1)} %get-tuple-element.269, f32[16,128]{1,0:T(8,128)S(1)} %get-tuple-element.270, f32[16,128]{1,0:T(8,128)S(1)} %get-tuple-element.271, ...), kind=kLoop, calls=%fused_computation.27.clone.1 | loop fusion | flops 64946176 | bytes 688192 | tf_op jit(solution)/shard_map/while/body/eval_jaxpr/reduce_sum | solution.py:60
  395.4 8.8 %fusion.80 = f32[128,512]{1,0:T(8,128)S(1)} fusion(f32[16,512]{1,0:T(8,128)S(1)} %get-tuple-element.267, f32[16,128]{1,0:T(8,128)S(1)} %get-tuple-element.268, f32[16,512]{1,0:T(8,128)S(1)} %get-tuple-element.269, f32[16,128]{1,0:T(8,128)S(1)} %get-tuple-element.270, f32[16,128]{1,0:T(8,128)S(1)} %get-tuple-element.271, ...), kind=kLoop, calls=%fused_computation.27.clone.1 | loop fusion | flops 64946176 | bytes 688192 | tf_op jit(solution)/shard_map/while/body/eval_jaxpr/reduce_sum | solution.py:60
  406.1 8.8 %fusion.80 = f32[128,512]{1,0:T(8,128)S(1)} fusion(f32[16,512]{1,0:T(8,128)S(1)} %get-tuple-element.267, f32[16,128]{1,0:T(8,128)S(1)} %get-tuple-element.268, f32[16,512]{1,0:T(8,128)S(1)} %get-tuple-element.269, f32[16,128]{1,0:T(8,128)S(1)} %get-tuple-element.270, f32[16,128]{1,0:T(8,128)S(1)} %get-tuple-element.271, ...), kind=kLoop, calls=%fused_computation.27.clone.1 | loop fusion | flops 64946176 | bytes 688192 | tf_op jit(solution)/shard_map/while/body/eval_jaxpr/reduce_sum | solution.py:60
  416.8 8.8 %fusion.80 = f32[128,512]{1,0:T(8,128)S(1)} fusion(f32[16,512]{1,0:T(8,128)S(1)} %get-tuple-element.267, f32[16,128]{1,0:T(8,128)S(1)} %get-tuple-element.268, f32[16,512]{1,0:T(8,128)S(1)} %get-tuple-element.269, f32[16,128]{1,0:T(8,128)S(1)} %get-tuple-element.270, f32[16,128]{1,0:T(8,128)S(1)} %get-tuple-element.271, ...), kind=kLoop, calls=%fused_computation.27.clone.1 | loop fusion | flops 64946176 | bytes 688192 | tf_op jit(solution)/shard_map/while/body/eval_jaxpr/reduce_sum | solution.py:60
  427.5 8.8 %fusion.80 = f32[128,512]{1,0:T(8,128)S(1)} fusion(f32[16,512]{1,0:T(8,128)S(1)} %get-tuple-element.267, f32[16,128]{1,0:T(8,128)S(1)} %get-tuple-element.268, f32[16,512]{1,0:T(8,128)S(1)} %get-tuple-element.269, f32[16,128]{1,0:T(8,128)S(1)} %get-tuple-element.270, f32[16,128]{1,0:T(8,128)S(1)} %get-tuple-element.271, ...), kind=kLoop, calls=%fused_computation.27.clone.1 | loop fusion | flops 64946176 | bytes 688192 | tf_op jit(solution)/shard_map/while/body/eval_jaxpr/reduce_sum | solution.py:60
  436.8 11.5 %scatter_custom_fusion.1 = f32[3,512]{0,1:T(8,128)S(1)} fusion(s32[2048]{0:T(1024)S(1)} %bitcast.36, f32[2048,3]{1,0:T(8,128)S(1)} %bitcast.32, f32[]{:T(128)} %constant.221.clone.1), kind=kCustom, calls=%fused_computation.118 | custom fusion | flops 6144 | bytes 6148 | tf_op jit(solution)/shard_map/scatter-add | solution.py:210
  450.5 3.5 collective-permute-done.9
  457.4 3.7 collective-permute-done.10
  470.0 3.7 collective-permute-done.12
  (180 shorter events, 71.2 us)
Async XLA Ops:
  3.3 4.1 copy-start.1
  105.2 1.2 copy-start.6
  122.7 27.6 %copy-start = (s32[16384,1]{0,1:T(1,128)S(1)}, s32[16384,1]{0,1:T(1,128)}, u32[]{:S(2)}) copy-start(s32[16384,1]{0,1:T(1,128)} %get-tuple-element.173) | copy-start | bytes 196612
  122.7 31.4 %copy-start.5 = (f32[32,256]{1,0:T(8,128)S(1)}, f32[32,256]{1,0:T(8,128)}, u32[]{:S(2)}) copy-start(f32[32,256]{1,0:T(8,128)} %param.15) | copy-start | bytes 98308
  127.8 5.8 %collective-permute-start = (f32[32,256]{1,0:T(8,128)S(1)}, f32[32,256]{1,0:T(8,128)S(1)}, u32[]{:S(2)}, u32[]{:S(2)}) collective-permute-start(f32[32,256]{1,0:T(8,128)S(1)} %pad_maximum_fusion), channel_id=1, source_target_pairs={{0,1},{1,0},{2,3},{3,2},{4,5},{5,4},{6,7},{7,6},{8,9},{9,8},{10,11... | collective-permute-start | bytes 98312 | tf_op jit(solution)/shard_map/ppermute | solution.py:106
  133.6 7.3 %collective-permute-start.1 = (f32[32,256]{1,0:T(8,128)S(1)}, f32[32,256]{1,0:T(8,128)S(1)}, u32[]{:S(2)}, u32[]{:S(2)}) collective-permute-start(f32[32,256]{1,0:T(8,128)S(1)} %fusion.68), channel_id=1, source_target_pairs={{0,2},{1,3},{2,0},{3,1},{4,6},{5,7},{6,4},{7,5},{8,10},{9,11},{10,... | collective-permute-start | bytes 98312 | tf_op jit(solution)/shard_map/ppermute | solution.py:106
  140.9 5.8 %collective-permute-start.2 = (f32[32,256]{1,0:T(8,128)S(1)}, f32[32,256]{1,0:T(8,128)S(1)}, u32[]{:S(2)}, u32[]{:S(2)}) collective-permute-start(f32[32,256]{1,0:T(8,128)S(1)} %add.353), channel_id=1, source_target_pairs={{0,4},{1,5},{2,6},{3,7},{4,0},{5,1},{6,2},{7,3},{8,12},{9,13},{10,... | collective-permute-start | bytes 98312 | tf_op jit(solution)/shard_map/ppermute | solution.py:106
  146.8 7.3 %collective-permute-start.3 = (f32[32,256]{1,0:T(8,128)S(1)}, f32[32,256]{1,0:T(8,128)S(1)}, u32[]{:S(2)}, u32[]{:S(2)}) collective-permute-start(f32[32,256]{1,0:T(8,128)S(1)} %add.354), channel_id=1, source_target_pairs={{0,8},{1,9},{2,10},{3,11},{4,12},{5,13},{6,14},{7,15},{8,0},{9,1},... | collective-permute-start | bytes 98312 | tf_op jit(solution)/shard_map/ppermute | solution.py:106
  155.3 3.9 copy-start.7
  162.6 112.8 %copy-start.8 = (s32[4,512]{1,0:T(4,128)S(1)}, s32[4,512]{1,0:T(4,128)}, u32[]{:S(2)}) copy-start(s32[4,512]{1,0:T(4,128)} %param.17) | copy-start | bytes 24580
  167.3 130.4 %copy-start.3 = (f32[32,32]{1,0:T(8,128)S(1)}, f32[32,32]{1,0:T(8,128)}, u32[]{:S(2)}) copy-start(f32[32,32]{1,0:T(8,128)} %param.12) | copy-start | bytes 12292
  167.3 130.7 %copy-start.2 = (f32[32,32]{0,1:T(8,128)S(1)}, f32[32,32]{0,1:T(8,128)}, u32[]{:S(2)}) copy-start(f32[32,32]{0,1:T(8,128)} %copy-done.1) | copy-start | bytes 12292
  255.9 3.2 collective-permute-start.4
  259.7 5.9 %collective-permute-start.5 = (f32[33,256]{1,0:T(8,128)S(1)}, f32[33,256]{1,0:T(8,128)S(1)}, u32[]{:S(2)}, u32[]{:S(2)}) collective-permute-start(f32[33,256]{1,0:T(8,128)S(1)} %slice_select_fusion), channel_id=1, source_target_pairs={{0,32},{16,48},{32,0},{48,16},{64,96},{80,112},{96,64},{112,80},{1... | collective-permute-start | bytes 101384 | tf_op jit(solution)/shard_map/ppermute | solution.py:122
  265.6 6.6 %collective-permute-start.6 = (f32[33,128]{1,0:T(8,128)S(1)}, f32[33,128]{1,0:T(8,128)S(1)}, u32[]{:S(2)}, u32[]{:S(2)}) collective-permute-start(f32[33,128]{1,0:T(8,128)S(1)} %slice_select_fusion.3), channel_id=1, source_target_pairs={{0,64},{16,80},{32,96},{48,112},{64,0},{80,16},{96,32},{112,48},{1... | collective-permute-start | bytes 50696 | tf_op jit(solution)/shard_map/ppermute | solution.py:122
  272.3 9.6 %collective-permute-start.7 = (f32[33,64]{1,0:T(8,128)S(1)}, f32[33,64]{1,0:T(8,128)S(1)}, u32[]{:S(2)}, u32[]{:S(2)}) collective-permute-start(f32[33,64]{1,0:T(8,128)S(1)} %slice_select_fusion.2), channel_id=1, source_target_pairs={{0,128},{16,144},{32,160},{48,176},{64,192},{80,208},{96,224},{112... | collective-permute-start | bytes 25352 | tf_op jit(solution)/shard_map/ppermute | solution.py:122
  282.0 14.4 %collective-permute-start.8 = (f32[33,32]{1,0:T(8,128)S(1)}, f32[33,32]{1,0:T(8,128)S(1)}, u32[]{:S(2)}, u32[]{:S(2)}) collective-permute-start(f32[33,32]{1,0:T(8,128)S(1)} %slice_select_fusion.1), channel_id=1, source_target_pairs={{0,256},{16,272},{32,288},{48,304},{64,320},{80,336},{96,352},{112... | collective-permute-start | bytes 12680 | tf_op jit(solution)/shard_map/ppermute | solution.py:122
  297.8 53.2 %copy-start.4 = (f32[32,32]{1,0:T(8,128)}, f32[32,32]{1,0:T(8,128)S(1)}, u32[]{:S(2)}) copy-start(f32[32,32]{1,0:T(8,128)S(1)} %pad_maximum_fusion.3) | copy-start | bytes 12292
  448.5 5.5 %collective-permute-start.9 = (f32[12,128]{1,0:T(8,128)S(1)}, f32[12,128]{1,0:T(8,128)S(1)}, u32[]{:S(2)}, u32[]{:S(2)}) collective-permute-start(f32[12,128]{1,0:T(8,128)S(1)} %reshape.403), channel_id=1, source_target_pairs={{0,1},{1,0},{2,3},{3,2},{4,5},{5,4},{6,7},{7,6},{8,9},{9,8},{10,11... | collective-permute-start | bytes 18440 | tf_op jit(solution)/shard_map/ppermute | solution.py:106
  454.0 7.0 %collective-permute-start.10 = (f32[12,128]{1,0:T(8,128)S(1)}, f32[12,128]{1,0:T(8,128)S(1)}, u32[]{:S(2)}, u32[]{:S(2)}) collective-permute-start(f32[12,128]{1,0:T(8,128)S(1)} %add.367), channel_id=1, source_target_pairs={{0,2},{1,3},{2,0},{3,1},{4,6},{5,7},{6,4},{7,5},{8,10},{9,11},{10,... | collective-permute-start | bytes 18440 | tf_op jit(solution)/shard_map/ppermute | solution.py:106
  461.1 5.5 %collective-permute-start.11 = (f32[12,128]{1,0:T(8,128)S(1)}, f32[12,128]{1,0:T(8,128)S(1)}, u32[]{:S(2)}, u32[]{:S(2)}) collective-permute-start(f32[12,128]{1,0:T(8,128)S(1)} %add.368), channel_id=1, source_target_pairs={{0,4},{1,5},{2,6},{3,7},{4,0},{5,1},{6,2},{7,3},{8,12},{9,13},{10,... | collective-permute-start | bytes 18440 | tf_op jit(solution)/shard_map/ppermute | solution.py:106
  466.6 7.0 %collective-permute-start.12 = (f32[12,128]{1,0:T(8,128)S(1)}, f32[12,128]{1,0:T(8,128)S(1)}, u32[]{:S(2)}, u32[]{:S(2)}) collective-permute-start(f32[12,128]{1,0:T(8,128)S(1)} %add.369), channel_id=1, source_target_pairs={{0,8},{1,9},{2,10},{3,11},{4,12},{5,13},{6,14},{7,15},{8,0},{9,1},... | collective-permute-start | bytes 18440 | tf_op jit(solution)/shard_map/ppermute | solution.py:106

commit v5 on v4

--- a/solution.py
+++ b/solution.py
@@ -65,7 +65,7 @@
     total, target_pos, target_str, target_mu, source_pos, source_str, source_mu, wavenumbers
 ):
     width = source_pos.shape[1]
-    step = math.gcd(width, 128)
+    step = math.gcd(width, 256)
 
     def visit_block(carry, block_index):
         begin = block_index * step
@@ -129,6 +129,19 @@
     for bit in range(bits):
         result = result | (((value >> bit) & 1) << (bits - 1 - bit))
     return result
+
+
+def split_three(value):
+    high = lax.reduce_precision(value, exponent_bits=8, mantissa_bits=7)
+    rest = value - high
+    middle = lax.reduce_precision(rest, exponent_bits=8, mantissa_bits=7)
+    low = rest - middle
+    return jnp.concatenate([high, middle, low], axis=0).astype(jnp.bfloat16)
+
+
+def join_three(value):
+    rows = value.shape[0] // 3
+    return (value[:rows] + value[rows : 2 * rows]) + value[2 * rows :]
 
 
 def on_device(centroids, strengths, self_inv, wavenumbers, field_pos, targets, lists, connect):
@@ -153,9 +166,20 @@
     owner_block = panel_ids // owned_count
     owner_row = owner_block // col_count
     mask = (owner_block % col_count == col_index).astype(jnp.float32)
-    local_ids = owner_row * owned_count + panel_ids % owned_count
-    table = jnp.transpose(src_all[: pos_rows + str_rows])
-    near_all = jnp.transpose(jnp.take(table, local_ids, axis=0))
+    row_bits = max(row_count - 1, 0).bit_length()
+    slot_ids = bit_reverse(owner_row, row_bits) * owned_count + panel_ids % owned_count
+    slot_order = [
+        sum(((slot >> bit) & 1) << (row_bits - 1 - bit) for bit in range(row_bits))
+        for slot in range(row_count)
+    ]
+    table = src_all[: pos_rows + str_rows].reshape(-1, row_count, owned_count)
+    table = jnp.concatenate([table[:, slot] for slot in slot_order], axis=1)
+    onehot = (
+        slot_ids[None, :] == lax.broadcasted_iota(jnp.int32, (source_count, slot_ids.shape[0]), 0)
+    ).astype(jnp.bfloat16)
+    near_all = join_three(
+        jnp.dot(split_three(table), onehot, preferred_element_type=jnp.float32)
+    )
     near = near_all[:pos_rows]
     observer = jnp.repeat(field_pos, listed, axis=1)
     offset = observer - near
@@ -182,15 +206,18 @@
     term_real = (cosine * rep_real + sine * rep_imag) * inverse
     term_imag = (cosine * rep_imag - sine * rep_real) * inverse
     terms = jnp.concatenate([term_real, term_imag], axis=0)
-    row_bits = max(row_count - 1, 0).bit_length()
-    slot_ids = bit_reverse(owner_row, row_bits) * owned_count + panel_ids % owned_count
-    source_part = jnp.zeros((source_count, 2 * freqs), jnp.float32).at[slot_ids].add(
-        jnp.transpose(terms)
+    source_part = join_three(
+        lax.dot_general(
+            split_three(terms),
+            onehot,
+            (((1,), (1,)), ((), ())),
+            preferred_element_type=jnp.float32,
+        )
     )
     misfit_part = jnp.sum(resid * resid)
     misfit_row = jnp.full((1, source_count), misfit_part, jnp.float32)
     packed = halving_scatter(
-        jnp.concatenate([jnp.transpose(source_part), misfit_row], axis=0), "row"
+        jnp.concatenate([source_part, misfit_row], axis=0), "row"
     )
     objective = packed[2 * freqs, 0] / (freqs * field_total) + 1e-06
     source_own = packed[: 2 * freqs] / objective

time: 477 us -> 337 us (0.71)
  other arithmetic: 195 us -> 97.7 us
  local copies, waits for them, and re-layouts: 92 us -> 23.3 us
  matrix products: 0 us -> 28.5 us
    scatter-add x1 -> x0, other arithmetic: 87.7 us -> none  [on_device(): jnp.zeros((source_count, 2 * freqs), jnp.float32).at[slot_ids]]
    gather x2 -> x0, local copies, waits for them, and re-layouts: 60.1 us -> none  [on_device(): near_all = jnp.transpose(jnp.take(table, local_ids, axis=0))]
    dot_general x0 -> x2, matrix products: none -> 28.5 us  [the longest x1 14.5 us: on_device(): jnp.dot(split_three(table), onehot, preferred_element_type=jnp.float32)]
    reduce_sum x8 -> x4, other arithmetic: 70.3 us -> 70.3 us  [pair_block(): weight = -jnp.sum(inner, axis=0) * (inverse * inverse * inverse)]
where the time goes in v5:
time: 337 us; the launch traced here: 335 us
  other arithmetic  97.7 us (29%)
  blocking collectives  89.9 us (27%)
  waiting for transfers between devices  47.5 us (14%)
  starting transfers between devices  42.6 us (13%)
  matrix products  28.5 us (8%)
  local copies, waits for them, and re-layouts  23.3 us (7%)
    reduce_sum x4, other arithmetic, pair_block(): weight = -jnp.sum(inner, axis=0) * (inverse * inverse * inverse)  70.3 us
    all_gather x1, blocking collectives, on_device(): src_all = lax.all_gather(owned, 'row', axis=1, tiled=True)  37.6 us
    all_gather x1, blocking collectives, on_device(): mu_all = lax.all_gather(mu_own, 'row', axis=1, tiled=True)  28.5 us
    ppermute x8, starting transfers between devices, xor_psum(): value = value + lax.ppermute(value, axis, partner)  26.3 us
    ppermute x8, waiting for transfers between devices, xor_psum(): value = value + lax.ppermute(value, axis, partner)  25 us
    all_gather x1, blocking collectives, on_device(): lax.all_gather(jnp.concatenate([centroids, strengths, mu_own], axis=0), '...  23.7 us
    ppermute x5, waiting for transfers between devices, halving_scatter(): value = keep + lax.ppermute(send, axis, partner)  22.5 us
    ppermute x5, starting transfers between devices, halving_scatter(): value = keep + lax.ppermute(send, axis, partner)  16.3 us
  transfers between devices with their start and end apart: 13, of which 13 were waited for; matrix products, arithmetic and copies ran while one was open for 0% of the time, Pallas kernels for 0%

profile of v5, /device:TPU:6, one launch (start us, length us, event | category | flops | bytes accessed | tf_op | source)
XLA Modules:
  0.0 335.5 jit_solution(1831116048333847540)
XLA Ops:
  3.1 37.6 %all_gather.9 = f32[67,1024]{0,1:T(8,128)S(1)} all-gather(f32[67,32]{0,1:T(8,128)S(1)} %pad_maximum_fusion.2), channel_id=1, replica_groups=mesh['row'=32,'col'=16] {'row'}, dimensions={1}, use_global_device_ids=true | all-gather | bytes 283008 | tf_op jit(solution)/shard_map/all_gather | solution.py:160
  46.1 14.5 %fusion.33 = f32[105,16384]{1,0:T(8,128)S(1)} fusion(s32[16384]{0:T(1024)S(1)} %fusion.75, bf16[35,1024]{1,0:T(8,128)(2,1)S(1)} %get-tuple-element.185, bf16[35,1024]{1,0:T(8,128)(2,1)S(1)} %get-tuple-element.186, bf16[35,1024]{1,0:T(8,128)(2,1)S(1)} %get-tuple-element.184), kind=kOutput, calls=%fused_computation.56 | convolution fusion | flops 3540637696 | bytes 7161856 | tf_op jit(solution)/shard_map/dot_general | solution.py:181
  61.5 3.2 subtract_multiply_fusion.3
  66.7 3.4 %reshape.216 = f32[16,256,64]{2,1,0:T(8,128)} reshape(f32[16,16384]{1,0:T(8,128)} %get-tuple-element.144) | data formatting | bytes 2097152 | tf_op jit(solution)/shard_map/reshape | solution.py:198
  72.9 3.5 %collective-permute-start = (f32[32,256]{1,0:T(8,128)S(1)}, f32[32,256]{1,0:T(8,128)S(1)}, u32[]{:S(2)}, u32[]{:S(2)}) collective-permute-start(f32[32,256]{1,0:T(8,128)S(1)} %pad_maximum_fusion.1), channel_id=1, source_target_pairs={{0,1},{1,0},{2,3},{3,2},{4,5},{5,4},{6,7},{7,6},{8,9},{9,8},{10,11... | collective-permute-start | bytes 98312 | tf_op jit(solution)/shard_map/ppermute | solution.py:106
  78.7 5.1 %collective-permute-start.1 = (f32[32,256]{1,0:T(8,128)S(1)}, f32[32,256]{1,0:T(8,128)S(1)}, u32[]{:S(2)}, u32[]{:S(2)}) collective-permute-start(f32[32,256]{1,0:T(8,128)S(1)} %fusion.83), channel_id=1, source_target_pairs={{0,2},{1,3},{2,0},{3,1},{4,6},{5,7},{6,4},{7,5},{8,10},{9,11},{10,... | collective-permute-start | bytes 98312 | tf_op jit(solution)/shard_map/ppermute | solution.py:106
  86.1 2.7 collective-permute-start.2
  88.8 3.1 collective-permute-done.2
  91.9 3.5 %collective-permute-start.3 = (f32[32,256]{1,0:T(8,128)S(1)}, f32[32,256]{1,0:T(8,128)S(1)}, u32[]{:S(2)}, u32[]{:S(2)}) collective-permute-start(f32[32,256]{1,0:T(8,128)S(1)} %add.277), channel_id=1, source_target_pairs={{0,8},{1,9},{2,10},{3,11},{4,12},{5,13},{6,14},{7,15},{8,0},{9,1},... | collective-permute-start | bytes 98312 | tf_op jit(solution)/shard_map/ppermute | solution.py:106
  95.4 3.8 %collective-permute-done.3 = f32[32,256]{1,0:T(8,128)S(1)} collective-permute-done((f32[32,256]{1,0:T(8,128)S(1)}, f32[32,256]{1,0:T(8,128)S(1)}, u32[]{:S(2)}, u32[]{:S(2)}) %collective-permute-start.3) | collective-permute-done | bytes 32800 | tf_op jit(solution)/shard_map/ppermute | solution.py:106
  104.3 3.2 add_multiply_fusion
  108.0 14.0 %fusion.32 = f32[96,1024]{1,0:T(8,128)S(1)} fusion(s32[16384]{0:T(1024)S(1)} %fusion.75, bf16[32,16384]{1,0:T(8,128)(2,1)S(1)} %get-tuple-element.149, bf16[32,16384]{1,0:T(8,128)(2,1)S(1)} %get-tuple-element.148, bf16[32,16384]{1,0:T(8,128)(2,1)S(1)} %get-tuple-element.147), kind=kOutput, calls=%fused_computation.55 | convolution fusion | flops 3247439872 | bytes 3604480 | tf_op jit(solution)/shard_map/dot_general | solution.py:210
  128.5 3.9 %collective-permute-done.5 = f32[33,256]{1,0:T(8,128)S(1)} collective-permute-done((f32[33,256]{1,0:T(8,128)S(1)}, f32[33,256]{1,0:T(8,128)S(1)}, u32[]{:S(2)}, u32[]{:S(2)}) %collective-permute-start.5) | collective-permute-done | bytes 33824 | tf_op jit(solution)/shard_map/ppermute | solution.py:122
  134.7 4.4 %collective-permute-done.6 = f32[33,128]{1,0:T(8,128)S(1)} collective-permute-done((f32[33,128]{1,0:T(8,128)S(1)}, f32[33,128]{1,0:T(8,128)S(1)}, u32[]{:S(2)}, u32[]{:S(2)}) %collective-permute-start.6) | collective-permute-done | bytes 16928 | tf_op jit(solution)/shard_map/ppermute | solution.py:122
  139.1 3.1 collective-permute-start.7
  142.3 6.4 %collective-permute-done.7 = f32[33,64]{1,0:T(8,128)S(1)} collective-permute-done((f32[33,64]{1,0:T(8,128)S(1)}, f32[33,64]{1,0:T(8,128)S(1)}, u32[]{:S(2)}, u32[]{:S(2)}) %collective-permute-start.7) | collective-permute-done | bytes 8480 | tf_op jit(solution)/shard_map/ppermute | solution.py:122
  148.9 7.3 %collective-permute-start.8 = (f32[33,32]{1,0:T(8,128)S(1)}, f32[33,32]{1,0:T(8,128)S(1)}, u32[]{:S(2)}, u32[]{:S(2)}) collective-permute-start(f32[33,32]{1,0:T(8,128)S(1)} %slice_select_fusion.1), channel_id=1, source_target_pairs={{0,256},{16,272},{32,288},{48,304},{64,320},{80,336},{96,352},{112... | collective-permute-start | bytes 12680 | tf_op jit(solution)/shard_map/ppermute | solution.py:122
  156.7 6.5 %collective-permute-done.8 = f32[33,32]{1,0:T(8,128)S(1)} collective-permute-done((f32[33,32]{1,0:T(8,128)S(1)}, f32[33,32]{1,0:T(8,128)S(1)}, u32[]{:S(2)}, u32[]{:S(2)}) %collective-permute-start.8) | collective-permute-done | bytes 4256 | tf_op jit(solution)/shard_map/ppermute | solution.py:122
  164.8 23.7 %all_gather.10 = f32[67,512]{0,1:T(8,128)S(1)} all-gather(f32[67,32]{0,1:T(8,128)S(1)} %pad_maximum_fusion.5), channel_id=1, replica_groups=mesh['row'=32,'col'=16] {'col'}, dimensions={1}, use_global_device_ids=true | all-gather | bytes 145792 | tf_op jit(solution)/shard_map/all_gather | solution.py:226
  188.9 28.5 %all_gather.11 = f32[32,1024]{0,1:T(8,128)S(1)} all-gather(f32[32,32]{0,1:T(8,128)S(1)} %copy.1745), channel_id=1, replica_groups=mesh['row'=32,'col'=16] {'row'}, dimensions={1}, use_global_device_ids=true | all-gather | bytes 135168 | tf_op jit(solution)/shard_map/all_gather | solution.py:225
  217.8 78.8 %while.11 = (s32[]{:T(128)}, f32[3,512]{1,0:T(4,128)S(1)}, f32[16]{0:T(128)S(1)}, f32[3,512]{1,0:T(4,128)S(1)}, s32[4]{0:T(128)S(1)}, /*index=5*/f32[3,1024]{1,0...) while((s32[]{:T(128)}, f32[3,512]{1,0:T(4,128)S(1)}, ...), condition=%wide.region_8.9_spmd.clone, body=%wide.region_4.8_spmd.clone.sunk | while | flops 133039624 | bytes 5357873 | solution.py:80
  219.5 17.6 %fusion.97 = f32[256,512]{1,0:T(8,128)S(1)} fusion(f32[16,512]{1,0:T(8,128)S(1)} %get-tuple-element.262, f32[16,256]{1,0:T(8,128)S(1)} %get-tuple-element.263, f32[16,512]{1,0:T(8,128)S(1)} %get-tuple-element.264, f32[16,256]{1,0:T(8,128)S(1)} %get-tuple-element.265, f32[16,256]{1,0:T(8,128)S(1)} %get-tuple-element.266, ...), kind=kLoop, calls=%fused_computation.25.clone.1 | loop fusion | flops 129892352 | bytes 1245248 | tf_op jit(solution)/shard_map/while/body/eval_jaxpr/reduce_sum | solution.py:60
  239.2 17.6 %fusion.97 = f32[256,512]{1,0:T(8,128)S(1)} fusion(f32[16,512]{1,0:T(8,128)S(1)} %get-tuple-element.262, f32[16,256]{1,0:T(8,128)S(1)} %get-tuple-element.263, f32[16,512]{1,0:T(8,128)S(1)} %get-tuple-element.264, f32[16,256]{1,0:T(8,128)S(1)} %get-tuple-element.265, f32[16,256]{1,0:T(8,128)S(1)} %get-tuple-element.266, ...), kind=kLoop, calls=%fused_computation.25.clone.1 | loop fusion | flops 129892352 | bytes 1245248 | tf_op jit(solution)/shard_map/while/body/eval_jaxpr/reduce_sum | solution.py:60
  258.9 17.6 %fusion.97 = f32[256,512]{1,0:T(8,128)S(1)} fusion(f32[16,512]{1,0:T(8,128)S(1)} %get-tuple-element.262, f32[16,256]{1,0:T(8,128)S(1)} %get-tuple-element.263, f32[16,512]{1,0:T(8,128)S(1)} %get-tuple-element.264, f32[16,256]{1,0:T(8,128)S(1)} %get-tuple-element.265, f32[16,256]{1,0:T(8,128)S(1)} %get-tuple-element.266, ...), kind=kLoop, calls=%fused_computation.25.clone.1 | loop fusion | flops 129892352 | bytes 1245248 | tf_op jit(solution)/shard_map/while/body/eval_jaxpr/reduce_sum | solution.py:60
  278.6 17.6 %fusion.97 = f32[256,512]{1,0:T(8,128)S(1)} fusion(f32[16,512]{1,0:T(8,128)S(1)} %get-tuple-element.262, f32[16,256]{1,0:T(8,128)S(1)} %get-tuple-element.263, f32[16,512]{1,0:T(8,128)S(1)} %get-tuple-element.264, f32[16,256]{1,0:T(8,128)S(1)} %get-tuple-element.265, f32[16,256]{1,0:T(8,128)S(1)} %get-tuple-element.266, ...), kind=kLoop, calls=%fused_computation.25.clone.1 | loop fusion | flops 129892352 | bytes 1245248 | tf_op jit(solution)/shard_map/while/body/eval_jaxpr/reduce_sum | solution.py:60
  296.9 11.5 %scatter_custom_fusion = f32[3,512]{0,1:T(8,128)S(1)} fusion(s32[2048]{0:T(1024)S(1)} %bitcast.119, f32[2048,3]{1,0:T(8,128)S(1)} %bitcast.85, f32[]{:T(128)} %constant.205.clone.1), kind=kCustom, calls=%fused_computation.127 | custom fusion | flops 6144 | bytes 6148 | tf_op jit(solution)/shard_map/scatter-add | solution.py:237
  310.6 3.5 %collective-permute-done.9 = f32[12,128]{1,0:T(8,128)S(1)} collective-permute-done((f32[12,128]{1,0:T(8,128)S(1)}, f32[12,128]{1,0:T(8,128)S(1)}, u32[]{:S(2)}, u32[]{:S(2)}) %collective-permute-start.9) | collective-permute-done | bytes 6176 | tf_op jit(solution)/shard_map/ppermute | solution.py:106
  314.1 3.4 %collective-permute-start.10 = (f32[12,128]{1,0:T(8,128)S(1)}, f32[12,128]{1,0:T(8,128)S(1)}, u32[]{:S(2)}, u32[]{:S(2)}) collective-permute-start(f32[12,128]{1,0:T(8,128)S(1)} %add.292), channel_id=1, source_target_pairs={{0,2},{1,3},{2,0},{3,1},{4,6},{5,7},{6,4},{7,5},{8,10},{9,11},{10,... | collective-permute-start | bytes 18440 | tf_op jit(solution)/shard_map/ppermute | solution.py:106
  317.4 3.7 %collective-permute-done.10 = f32[12,128]{1,0:T(8,128)S(1)} collective-permute-done((f32[12,128]{1,0:T(8,128)S(1)}, f32[12,128]{1,0:T(8,128)S(1)}, u32[]{:S(2)}, u32[]{:S(2)}) %collective-permute-start.10) | collective-permute-done | bytes 6176 | tf_op jit(solution)/shard_map/ppermute | solution.py:106
  323.9 2.8 collective-permute-done.11
  326.7 3.4 %collective-permute-start.12 = (f32[12,128]{1,0:T(8,128)S(1)}, f32[12,128]{1,0:T(8,128)S(1)}, u32[]{:S(2)}, u32[]{:S(2)}) collective-permute-start(f32[12,128]{1,0:T(8,128)S(1)} %add.294), channel_id=1, source_target_pairs={{0,8},{1,9},{2,10},{3,11},{4,12},{5,13},{6,14},{7,15},{8,0},{9,1},... | collective-permute-start | bytes 18440 | tf_op jit(solution)/shard_map/ppermute | solution.py:106
  330.0 3.7 %collective-permute-done.12 = f32[12,128]{1,0:T(8,128)S(1)} collective-permute-done((f32[12,128]{1,0:T(8,128)S(1)}, f32[12,128]{1,0:T(8,128)S(1)}, u32[]{:S(2)}, u32[]{:S(2)}) %collective-permute-start.12) | collective-permute-done | bytes 6176 | tf_op jit(solution)/shard_map/ppermute | solution.py:106
  (159 shorter events, 45.8 us)
Async XLA Ops:
  60.6 0.8 copy-start.3
  61.4 37.7 %copy-start.2 = (f32[32,256]{1,0:T(8,128)S(1)}, f32[32,256]{1,0:T(8,128)}, u32[]{:S(2)}) copy-start(f32[32,256]{1,0:T(8,128)} %param.15) | copy-start | bytes 98308
  72.9 5.8 %collective-permute-start = (f32[32,256]{1,0:T(8,128)S(1)}, f32[32,256]{1,0:T(8,128)S(1)}, u32[]{:S(2)}, u32[]{:S(2)}) collective-permute-start(f32[32,256]{1,0:T(8,128)S(1)} %pad_maximum_fusion.1), channel_id=1, source_target_pairs={{0,1},{1,0},{2,3},{3,2},{4,5},{5,4},{6,7},{7,6},{8,9},{9,8},{10,11... | collective-permute-start | bytes 98312 | tf_op jit(solution)/shard_map/ppermute | solution.py:106
  78.7 7.3 %collective-permute-start.1 = (f32[32,256]{1,0:T(8,128)S(1)}, f32[32,256]{1,0:T(8,128)S(1)}, u32[]{:S(2)}, u32[]{:S(2)}) collective-permute-start(f32[32,256]{1,0:T(8,128)S(1)} %fusion.83), channel_id=1, source_target_pairs={{0,2},{1,3},{2,0},{3,1},{4,6},{5,7},{6,4},{7,5},{8,10},{9,11},{10,... | collective-permute-start | bytes 98312 | tf_op jit(solution)/shard_map/ppermute | solution.py:106
  86.1 5.8 %collective-permute-start.2 = (f32[32,256]{1,0:T(8,128)S(1)}, f32[32,256]{1,0:T(8,128)S(1)}, u32[]{:S(2)}, u32[]{:S(2)}) collective-permute-start(f32[32,256]{1,0:T(8,128)S(1)} %add.276), channel_id=1, source_target_pairs={{0,4},{1,5},{2,6},{3,7},{4,0},{5,1},{6,2},{7,3},{8,12},{9,13},{10,... | collective-permute-start | bytes 98312 | tf_op jit(solution)/shard_map/ppermute | solution.py:106
  91.9 7.3 %collective-permute-start.3 = (f32[32,256]{1,0:T(8,128)S(1)}, f32[32,256]{1,0:T(8,128)S(1)}, u32[]{:S(2)}, u32[]{:S(2)}) collective-permute-start(f32[32,256]{1,0:T(8,128)S(1)} %add.277), channel_id=1, source_target_pairs={{0,8},{1,9},{2,10},{3,11},{4,12},{5,13},{6,14},{7,15},{8,0},{9,1},... | collective-permute-start | bytes 98312 | tf_op jit(solution)/shard_map/ppermute | solution.py:106
  108.0 34.2 %copy-start.4 = (s32[4,512]{1,0:T(4,128)S(1)}, s32[4,512]{1,0:T(4,128)}, u32[]{:S(2)}) copy-start(s32[4,512]{1,0:T(4,128)} %param.17) | copy-start | bytes 24580
  108.0 56.5 %copy-start = (f32[32,32]{1,0:T(8,128)S(1)}, f32[32,32]{1,0:T(8,128)}, u32[]{:S(2)}) copy-start(f32[32,32]{1,0:T(8,128)} %param.12) | copy-start | bytes 12292
  122.7 3.2 collective-permute-start.4
  126.6 5.9 %collective-permute-start.5 = (f32[33,256]{1,0:T(8,128)S(1)}, f32[33,256]{1,0:T(8,128)S(1)}, u32[]{:S(2)}, u32[]{:S(2)}) collective-permute-start(f32[33,256]{1,0:T(8,128)S(1)} %slice_select_fusion), channel_id=1, source_target_pairs={{0,32},{16,48},{32,0},{48,16},{64,96},{80,112},{96,64},{112,80},{1... | collective-permute-start | bytes 101384 | tf_op jit(solution)/shard_map/ppermute | solution.py:122
  132.5 6.6 %collective-permute-start.6 = (f32[33,128]{1,0:T(8,128)S(1)}, f32[33,128]{1,0:T(8,128)S(1)}, u32[]{:S(2)}, u32[]{:S(2)}) collective-permute-start(f32[33,128]{1,0:T(8,128)S(1)} %slice_select_fusion.3), channel_id=1, source_target_pairs={{0,64},{16,80},{32,96},{48,112},{64,0},{80,16},{96,32},{112,48},{1... | collective-permute-start | bytes 50696 | tf_op jit(solution)/shard_map/ppermute | solution.py:122
  139.1 9.6 %collective-permute-start.7 = (f32[33,64]{1,0:T(8,128)S(1)}, f32[33,64]{1,0:T(8,128)S(1)}, u32[]{:S(2)}, u32[]{:S(2)}) collective-permute-start(f32[33,64]{1,0:T(8,128)S(1)} %slice_select_fusion.2), channel_id=1, source_target_pairs={{0,128},{16,144},{32,160},{48,176},{64,192},{80,208},{96,224},{112... | collective-permute-start | bytes 25352 | tf_op jit(solution)/shard_map/ppermute | solution.py:122
  148.9 14.4 %collective-permute-start.8 = (f32[33,32]{1,0:T(8,128)S(1)}, f32[33,32]{1,0:T(8,128)S(1)}, u32[]{:S(2)}, u32[]{:S(2)}) collective-permute-start(f32[33,32]{1,0:T(8,128)S(1)} %slice_select_fusion.1), channel_id=1, source_target_pairs={{0,256},{16,272},{32,288},{48,304},{64,320},{80,336},{96,352},{112... | collective-permute-start | bytes 12680 | tf_op jit(solution)/shard_map/ppermute | solution.py:122
  164.6 53.2 %copy-start.1 = (f32[32,32]{1,0:T(8,128)}, f32[32,32]{1,0:T(8,128)S(1)}, u32[]{:S(2)}) copy-start(f32[32,32]{1,0:T(8,128)S(1)} %pad_maximum_fusion.4) | copy-start | bytes 12292
  308.5 5.5 %collective-permute-start.9 = (f32[12,128]{1,0:T(8,128)S(1)}, f32[12,128]{1,0:T(8,128)S(1)}, u32[]{:S(2)}, u32[]{:S(2)}) collective-permute-start(f32[12,128]{1,0:T(8,128)S(1)} %reshape.220), channel_id=1, source_target_pairs={{0,1},{1,0},{2,3},{3,2},{4,5},{5,4},{6,7},{7,6},{8,9},{9,8},{10,11... | collective-permute-start | bytes 18440 | tf_op jit(solution)/shard_map/ppermute | solution.py:106
  314.1 7.0 %collective-permute-start.10 = (f32[12,128]{1,0:T(8,128)S(1)}, f32[12,128]{1,0:T(8,128)S(1)}, u32[]{:S(2)}, u32[]{:S(2)}) collective-permute-start(f32[12,128]{1,0:T(8,128)S(1)} %add.292), channel_id=1, source_target_pairs={{0,2},{1,3},{2,0},{3,1},{4,6},{5,7},{6,4},{7,5},{8,10},{9,11},{10,... | collective-permute-start | bytes 18440 | tf_op jit(solution)/shard_map/ppermute | solution.py:106
  321.1 5.5 %collective-permute-start.11 = (f32[12,128]{1,0:T(8,128)S(1)}, f32[12,128]{1,0:T(8,128)S(1)}, u32[]{:S(2)}, u32[]{:S(2)}) collective-permute-start(f32[12,128]{1,0:T(8,128)S(1)} %add.293), channel_id=1, source_target_pairs={{0,4},{1,5},{2,6},{3,7},{4,0},{5,1},{6,2},{7,3},{8,12},{9,13},{10,... | collective-permute-start | bytes 18440 | tf_op jit(solution)/shard_map/ppermute | solution.py:106
  326.7 7.0 %collective-permute-start.12 = (f32[12,128]{1,0:T(8,128)S(1)}, f32[12,128]{1,0:T(8,128)S(1)}, u32[]{:S(2)}, u32[]{:S(2)}) collective-permute-start(f32[12,128]{1,0:T(8,128)S(1)} %add.294), channel_id=1, source_target_pairs={{0,8},{1,9},{2,10},{3,11},{4,12},{5,13},{6,14},{7,15},{8,0},{9,1},... | collective-permute-start | bytes 18440 | tf_op jit(solution)/shard_map/ppermute | solution.py:106

commit v6 on v5

--- a/solution.py
+++ b/solution.py
@@ -65,7 +65,7 @@
     total, target_pos, target_str, target_mu, source_pos, source_str, source_mu, wavenumbers
 ):
     width = source_pos.shape[1]
-    step = math.gcd(width, 256)
+    step = math.gcd(width, 512)
 
     def visit_block(carry, block_index):
         begin = block_index * step
@@ -234,8 +234,16 @@
     accum = pair_sweep(empty, tgt_pos, tgt_str, tgt_mu, src_pos, src_str, mu_all, wavenumbers)
     panel_sens = accum * (1.0 / math.sqrt(panel_total * freqs))
     vertex_local = connect - row_index * block_width
-    vertex_part = jnp.zeros((3, block_width), jnp.float32).at[:, vertex_local.reshape(-1)].add(
-        jnp.tile(0.25 * panel_sens, (1, connect.shape[0]))
+    vertex_hits = (
+        vertex_local[:, None, :] == lax.broadcasted_iota(jnp.int32, (1, block_width, 1), 1)
+    ).astype(jnp.bfloat16)
+    vertex_part = join_three(
+        jnp.einsum(
+            "cp,kvp->cv",
+            split_three(0.25 * panel_sens),
+            vertex_hits,
+            preferred_element_type=jnp.float32,
+        )
     )
     lanes = 128 if block_width % 128 == 0 else block_width
     vertex_rows = vertex_part.reshape(3 * block_width // lanes, lanes)

time: 337 us -> 324 us (0.961)
  other arithmetic: 97.7 us -> 87.4 us
    scatter-add x1 -> x0, other arithmetic: 11.5 us -> none  [on_device(): jnp.zeros((3, block_width), jnp.float32).at[:, vertex_local.reshape(-1)]]
    reduce_sum x4 -> x2, other arithmetic: 70.3 us -> 68.8 us  [pair_block(): weight = -jnp.sum(inner, axis=0) * (inverse * inverse * inverse)]
where the time goes in v6:
time: 324 us; the launch traced here: 322 us
  blocking collectives  89.9 us (28%)
  other arithmetic  87.4 us (27%)
  waiting for transfers between devices  46.9 us (14%)
  starting transfers between devices  42.6 us (13%)
  matrix products  28.7 us (9%)
  local copies, waits for them, and re-layouts  22.3 us (7%)
    reduce_sum x2, other arithmetic, pair_block(): weight = -jnp.sum(inner, axis=0) * (inverse * inverse * inverse)  68.8 us
    all_gather x1, blocking collectives, on_device(): src_all = lax.all_gather(owned, 'row', axis=1, tiled=True)  37.6 us
    all_gather x1, blocking collectives, on_device(): mu_all = lax.all_gather(mu_own, 'row', axis=1, tiled=True)  28.5 us
    ppermute x8, starting transfers between devices, xor_psum(): value = value + lax.ppermute(value, axis, partner)  26.3 us
    ppermute x8, waiting for transfers between devices, xor_psum(): value = value + lax.ppermute(value, axis, partner)  25 us
    all_gather x1, blocking collectives, on_device(): lax.all_gather(jnp.concatenate([centroids, strengths, mu_own], axis=0), '...  23.7 us
    ppermute x5, waiting for transfers between devices, halving_scatter(): value = keep + lax.ppermute(send, axis, partner)  21.9 us
    ppermute x5, starting transfers between devices, halving_scatter(): value = keep + lax.ppermute(send, axis, partner)  16.3 us
  transfers between devices with their start and end apart: 13, of which 13 were waited for; matrix products, arithmetic and copies ran while one was open for 0% of the time, Pallas kernels for 0%

profile of v6, /device:TPU:6, one launch (start us, length us, event | category | flops | bytes accessed | tf_op | source)
XLA Modules:
  0.0 322.2 jit_solution(1281743938956934765)
XLA Ops:
  3.1 37.6 %all_gather.9 = f32[67,1024]{0,1:T(8,128)S(1)} all-gather(f32[67,32]{0,1:T(8,128)S(1)} %pad_maximum_fusion.2), channel_id=1, replica_groups=mesh['row'=32,'col'=16] {'row'}, dimensions={1}, use_global_device_ids=true | all-gather | bytes 283008 | tf_op jit(solution)/shard_map/all_gather | solution.py:160
  45.7 14.5 %fusion.33 = f32[105,16384]{1,0:T(8,128)S(1)} fusion(s32[16384]{0:T(1024)S(1)} %fusion.74, bf16[35,1024]{1,0:T(8,128)(2,1)S(1)} %get-tuple-element.185, bf16[35,1024]{1,0:T(8,128)(2,1)S(1)} %get-tuple-element.186, bf16[35,1024]{1,0:T(8,128)(2,1)S(1)} %get-tuple-element.184), kind=kOutput, calls=%fused_computation.55 | convolution fusion | flops 3540637696 | bytes 7161856 | tf_op jit(solution)/shard_map/dot_general | solution.py:181
  64.0 3.8 %subtract_multiply_fusion.3 = (f32[16,16384]{1,0:T(8,128)}, f32[16,16384]{1,0:T(8,128)}) fusion(f32[35,16384]{1,0:T(8,128)S(1)} %slice_add_fusion, f32[16384]{0:T(1024)S(1)} %get-tuple-element.188, f32[16384]{0:T(1024)S(1)} %get-tuple-element.187, f32[16]{0:T(128)} %param.13), kind=kLoop, calls=%fused_computation.111 | loop fusion | flops 12582912 | bytes 4325440 | tf_op jit(solution)/shard_map/mul | solution.py:193
  69.9 3.4 %reshape.182 = f32[16,256,64]{2,1,0:T(8,128)} reshape(f32[16,16384]{1,0:T(8,128)} %get-tuple-element.144) | data formatting | bytes 2097152 | tf_op jit(solution)/shard_map/reshape | solution.py:198
  76.1 3.5 %collective-permute-start = (f32[32,256]{1,0:T(8,128)S(1)}, f32[32,256]{1,0:T(8,128)S(1)}, u32[]{:S(2)}, u32[]{:S(2)}) collective-permute-start(f32[32,256]{1,0:T(8,128)S(1)} %pad_maximum_fusion.1), channel_id=1, source_target_pairs={{0,1},{1,0},{2,3},{3,2},{4,5},{5,4},{6,7},{7,6},{8,9},{9,8},{10,11... | collective-permute-start | bytes 98312 | tf_op jit(solution)/shard_map/ppermute | solution.py:106
  79.6 2.3 collective-permute-done
  81.9 5.1 %collective-permute-start.1 = (f32[32,256]{1,0:T(8,128)S(1)}, f32[32,256]{1,0:T(8,128)S(1)}, u32[]{:S(2)}, u32[]{:S(2)}) collective-permute-start(f32[32,256]{1,0:T(8,128)S(1)} %fusion.90), channel_id=1, source_target_pairs={{0,2},{1,3},{2,0},{3,1},{4,6},{5,7},{6,4},{7,5},{8,10},{9,11},{10,... | collective-permute-start | bytes 98312 | tf_op jit(solution)/shard_map/ppermute | solution.py:106
  87.0 2.2 collective-permute-done.1
  89.2 2.7 collective-permute-start.2
  92.0 3.1 collective-permute-done.2
  95.0 3.5 %collective-permute-start.3 = (f32[32,256]{1,0:T(8,128)S(1)}, f32[32,256]{1,0:T(8,128)S(1)}, u32[]{:S(2)}, u32[]{:S(2)}) collective-permute-start(f32[32,256]{1,0:T(8,128)S(1)} %add.268), channel_id=1, source_target_pairs={{0,8},{1,9},{2,10},{3,11},{4,12},{5,13},{6,14},{7,15},{8,0},{9,1},... | collective-permute-start | bytes 98312 | tf_op jit(solution)/shard_map/ppermute | solution.py:106
  98.6 3.8 %collective-permute-done.3 = f32[32,256]{1,0:T(8,128)S(1)} collective-permute-done((f32[32,256]{1,0:T(8,128)S(1)}, f32[32,256]{1,0:T(8,128)S(1)}, u32[]{:S(2)}, u32[]{:S(2)}) %collective-permute-start.3) | collective-permute-done | bytes 32800 | tf_op jit(solution)/shard_map/ppermute | solution.py:106
  107.5 3.2 %add_multiply_fusion = (f32[16,16384]{1,0:T(8,128)S(1)}, f32[16,16384]{1,0:T(8,128)S(1)}) fusion(f32[16,16384]{1,0:T(8,128)} %reshape.184, f32[16,16384]{1,0:T(8,128)} %reshape.183, f32[16384]{0:T(1024)S(1)} %get-tuple-element.188, f32[16384]{0:T(1024)S(1)} %get-tuple-element.187, f32[16]{0:T(128)S(1)} %copy-done.8), kind=kLoop, calls=%fused_computation.109 | loop fusion | flops 12582912 | bytes 4325440 | tf_op jit(solution)/shard_map/mul | solution.py:206
  111.2 14.0 %fusion.32 = f32[96,1024]{1,0:T(8,128)S(1)} fusion(s32[16384]{0:T(1024)S(1)} %copy-done.5, bf16[32,16384]{1,0:T(8,128)(2,1)S(1)} %get-tuple-element.149, bf16[32,16384]{1,0:T(8,128)(2,1)S(1)} %get-tuple-element.148, bf16[32,16384]{1,0:T(8,128)(2,1)S(1)} %get-tuple-element.147), kind=kOutput, calls=%fused_computation.54 | convolution fusion | flops 3247439872 | bytes 3604480 | tf_op jit(solution)/shard_map/dot_general | solution.py:210
  131.7 3.9 %collective-permute-done.5 = f32[33,256]{1,0:T(8,128)S(1)} collective-permute-done((f32[33,256]{1,0:T(8,128)S(1)}, f32[33,256]{1,0:T(8,128)S(1)}, u32[]{:S(2)}, u32[]{:S(2)}) %collective-permute-start.5) | collective-permute-done | bytes 33824 | tf_op jit(solution)/shard_map/ppermute | solution.py:122
  137.9 4.4 %collective-permute-done.6 = f32[33,128]{1,0:T(8,128)S(1)} collective-permute-done((f32[33,128]{1,0:T(8,128)S(1)}, f32[33,128]{1,0:T(8,128)S(1)}, u32[]{:S(2)}, u32[]{:S(2)}) %collective-permute-start.6) | collective-permute-done | bytes 16928 | tf_op jit(solution)/shard_map/ppermute | solution.py:122
  142.3 3.1 collective-permute-start.7
  145.4 6.5 %collective-permute-done.7 = f32[33,64]{1,0:T(8,128)S(1)} collective-permute-done((f32[33,64]{1,0:T(8,128)S(1)}, f32[33,64]{1,0:T(8,128)S(1)}, u32[]{:S(2)}, u32[]{:S(2)}) %collective-permute-start.7) | collective-permute-done | bytes 8480 | tf_op jit(solution)/shard_map/ppermute | solution.py:122
  152.1 7.3 %collective-permute-start.8 = (f32[33,32]{1,0:T(8,128)S(1)}, f32[33,32]{1,0:T(8,128)S(1)}, u32[]{:S(2)}, u32[]{:S(2)}) collective-permute-start(f32[33,32]{1,0:T(8,128)S(1)} %slice_select_fusion.1), channel_id=1, source_target_pairs={{0,256},{16,272},{32,288},{48,304},{64,320},{80,336},{96,352},{112... | collective-permute-start | bytes 12680 | tf_op jit(solution)/shard_map/ppermute | solution.py:122
  160.5 5.9 %collective-permute-done.8 = f32[33,32]{1,0:T(8,128)S(1)} collective-permute-done((f32[33,32]{1,0:T(8,128)S(1)}, f32[33,32]{1,0:T(8,128)S(1)}, u32[]{:S(2)}, u32[]{:S(2)}) %collective-permute-start.8) | collective-permute-done | bytes 4256 | tf_op jit(solution)/shard_map/ppermute | solution.py:122
  168.0 23.7 %all_gather.10 = f32[67,512]{0,1:T(8,128)S(1)} all-gather(f32[67,32]{0,1:T(8,128)S(1)} %pad_maximum_fusion.5), channel_id=1, replica_groups=mesh['row'=32,'col'=16] {'col'}, dimensions={1}, use_global_device_ids=true | all-gather | bytes 145792 | tf_op jit(solution)/shard_map/all_gather | solution.py:226
  192.3 28.5 %all_gather.11 = f32[32,1024]{0,1:T(8,128)S(1)} all-gather(f32[32,32]{0,1:T(8,128)S(1)} %copy.1679), channel_id=1, replica_groups=mesh['row'=32,'col'=16] {'row'}, dimensions={1}, use_global_device_ids=true | all-gather | bytes 135168 | tf_op jit(solution)/shard_map/all_gather | solution.py:225
  221.0 73.9 %while.11 = (s32[]{:T(128)}, f32[3,512]{1,0:T(4,128)S(1)}, f32[16]{0:T(128)S(1)}, f32[3,512]{1,0:T(4,128)S(1)}, s32[2]{0:T(128)S(1)}, /*index=5*/f32[3,1024]{1,0...) while((s32[]{:T(128)}, f32[3,512]{1,0:T(4,128)S(1)}, ...), condition=%wide.region_8.9_spmd.clone, body=%wide.region_4.8_spmd.clone.sunk | while | flops 266077696 | bytes 10285353 | solution.py:80
  222.9 34.4 %fusion.105 = f32[512,512]{1,0:T(8,128)S(1)} fusion(f32[16,512]{1,0:T(8,128)S(1)} %get-tuple-element.265, f32[16,512]{1,0:T(8,128)S(1)} %get-tuple-element.266, f32[16,512]{1,0:T(8,128)S(1)} %get-tuple-element.267, f32[16,512]{1,0:T(8,128)S(1)} %get-tuple-element.268, f32[16,512]{1,0:T(8,128)S(1)} %get-tuple-element.269, ...), kind=kLoop, calls=%fused_computation.24.clone.1 | loop fusion | flops 259784704 | bytes 2359360 | tf_op jit(solution)/shard_map/while/body/eval_jaxpr/reduce_sum | solution.py:60
  259.8 34.4 %fusion.105 = f32[512,512]{1,0:T(8,128)S(1)} fusion(f32[16,512]{1,0:T(8,128)S(1)} %get-tuple-element.265, f32[16,512]{1,0:T(8,128)S(1)} %get-tuple-element.266, f32[16,512]{1,0:T(8,128)S(1)} %get-tuple-element.267, f32[16,512]{1,0:T(8,128)S(1)} %get-tuple-element.268, f32[16,512]{1,0:T(8,128)S(1)} %get-tuple-element.269, ...), kind=kLoop, calls=%fused_computation.24.clone.1 | loop fusion | flops 259784704 | bytes 2359360 | tf_op jit(solution)/shard_map/while/body/eval_jaxpr/reduce_sum | solution.py:60
  297.3 3.5 %collective-permute-done.9 = f32[12,128]{1,0:T(8,128)S(1)} collective-permute-done((f32[12,128]{1,0:T(8,128)S(1)}, f32[12,128]{1,0:T(8,128)S(1)}, u32[]{:S(2)}, u32[]{:S(2)}) %collective-permute-start.9) | collective-permute-done | bytes 6176 | tf_op jit(solution)/shard_map/ppermute | solution.py:106
  300.8 3.4 %collective-permute-start.10 = (f32[12,128]{1,0:T(8,128)S(1)}, f32[12,128]{1,0:T(8,128)S(1)}, u32[]{:S(2)}, u32[]{:S(2)}) collective-permute-start(f32[12,128]{1,0:T(8,128)S(1)} %add.283), channel_id=1, source_target_pairs={{0,2},{1,3},{2,0},{3,1},{4,6},{5,7},{6,4},{7,5},{8,10},{9,11},{10,... | collective-permute-start | bytes 18440 | tf_op jit(solution)/shard_map/ppermute | solution.py:106
  304.1 3.7 %collective-permute-done.10 = f32[12,128]{1,0:T(8,128)S(1)} collective-permute-done((f32[12,128]{1,0:T(8,128)S(1)}, f32[12,128]{1,0:T(8,128)S(1)}, u32[]{:S(2)}, u32[]{:S(2)}) %collective-permute-start.10) | collective-permute-done | bytes 6176 | tf_op jit(solution)/shard_map/ppermute | solution.py:106
  307.8 2.7 collective-permute-start.11
  310.5 2.8 collective-permute-done.11
  313.3 3.4 %collective-permute-start.12 = (f32[12,128]{1,0:T(8,128)S(1)}, f32[12,128]{1,0:T(8,128)S(1)}, u32[]{:S(2)}, u32[]{:S(2)}) collective-permute-start(f32[12,128]{1,0:T(8,128)S(1)} %add.285), channel_id=1, source_target_pairs={{0,8},{1,9},{2,10},{3,11},{4,12},{5,13},{6,14},{7,15},{8,0},{9,1},... | collective-permute-start | bytes 18440 | tf_op jit(solution)/shard_map/ppermute | solution.py:106
  316.7 3.7 %collective-permute-done.12 = f32[12,128]{1,0:T(8,128)S(1)} collective-permute-done((f32[12,128]{1,0:T(8,128)S(1)}, f32[12,128]{1,0:T(8,128)S(1)}, u32[]{:S(2)}, u32[]{:S(2)}) %collective-permute-start.12) | collective-permute-done | bytes 6176 | tf_op jit(solution)/shard_map/ppermute | solution.py:106
  (148 shorter events, 40.0 us)
Async XLA Ops:
  2.2 0.8 copy-start.1
  44.9 0.6 copy-start
  45.1 0.6 copy-start.4
  60.2 0.7 copy-start.10
  64.0 38.3 %copy-start.7 = (f32[32,256]{1,0:T(8,128)S(1)}, f32[32,256]{1,0:T(8,128)}, u32[]{:S(2)}) copy-start(f32[32,256]{1,0:T(8,128)} %param.15) | copy-start | bytes 98308
  73.3 34.2 %copy-start.8 = (f32[16]{0:T(128)S(1)}, f32[16]{0:T(128)}, u32[]{:S(2)}) copy-start(f32[16]{0:T(128)} %param.13) | copy-start | bytes 196
  76.1 5.8 %collective-permute-start = (f32[32,256]{1,0:T(8,128)S(1)}, f32[32,256]{1,0:T(8,128)S(1)}, u32[]{:S(2)}, u32[]{:S(2)}) collective-permute-start(f32[32,256]{1,0:T(8,128)S(1)} %pad_maximum_fusion.1), channel_id=1, source_target_pairs={{0,1},{1,0},{2,3},{3,2},{4,5},{5,4},{6,7},{7,6},{8,9},{9,8},{10,11... | collective-permute-start | bytes 98312 | tf_op jit(solution)/shard_map/ppermute | solution.py:106
  81.9 7.3 %collective-permute-start.1 = (f32[32,256]{1,0:T(8,128)S(1)}, f32[32,256]{1,0:T(8,128)S(1)}, u32[]{:S(2)}, u32[]{:S(2)}) collective-permute-start(f32[32,256]{1,0:T(8,128)S(1)} %fusion.90), channel_id=1, source_target_pairs={{0,2},{1,3},{2,0},{3,1},{4,6},{5,7},{6,4},{7,5},{8,10},{9,11},{10,... | collective-permute-start | bytes 98312 | tf_op jit(solution)/shard_map/ppermute | solution.py:106
  89.2 5.8 %collective-permute-start.2 = (f32[32,256]{1,0:T(8,128)S(1)}, f32[32,256]{1,0:T(8,128)S(1)}, u32[]{:S(2)}, u32[]{:S(2)}) collective-permute-start(f32[32,256]{1,0:T(8,128)S(1)} %add.267), channel_id=1, source_target_pairs={{0,4},{1,5},{2,6},{3,7},{4,0},{5,1},{6,2},{7,3},{8,12},{9,13},{10,... | collective-permute-start | bytes 98312 | tf_op jit(solution)/shard_map/ppermute | solution.py:106
  95.0 7.3 %collective-permute-start.3 = (f32[32,256]{1,0:T(8,128)S(1)}, f32[32,256]{1,0:T(8,128)S(1)}, u32[]{:S(2)}, u32[]{:S(2)}) collective-permute-start(f32[32,256]{1,0:T(8,128)S(1)} %add.268), channel_id=1, source_target_pairs={{0,8},{1,9},{2,10},{3,11},{4,12},{5,13},{6,14},{7,15},{8,0},{9,1},... | collective-permute-start | bytes 98312 | tf_op jit(solution)/shard_map/ppermute | solution.py:106
  105.2 6.0 %copy-start.5 = (s32[16384]{0:T(1024)S(1)}, s32[16384]{0:T(1024)}, u32[]{:S(2)}) copy-start(s32[16384]{0:T(1024)} %copy-done.4) | copy-start | bytes 196612
  111.2 34.2 %copy-start.9 = (s32[4,512]{1,0:T(4,128)S(1)}, s32[4,512]{1,0:T(4,128)}, u32[]{:S(2)}) copy-start(s32[4,512]{1,0:T(4,128)} %param.17) | copy-start | bytes 24580
  111.2 56.5 %copy-start.3 = (f32[32,32]{1,0:T(8,128)S(1)}, f32[32,32]{1,0:T(8,128)}, u32[]{:S(2)}) copy-start(f32[32,32]{1,0:T(8,128)} %param.12) | copy-start | bytes 12292
  111.2 56.7 %copy-start.2 = (f32[32,32]{0,1:T(8,128)S(1)}, f32[32,32]{0,1:T(8,128)}, u32[]{:S(2)}) copy-start(f32[32,32]{0,1:T(8,128)} %copy-done.1) | copy-start | bytes 12292
  125.9 3.2 collective-permute-start.4
  129.7 5.9 %collective-permute-start.5 = (f32[33,256]{1,0:T(8,128)S(1)}, f32[33,256]{1,0:T(8,128)S(1)}, u32[]{:S(2)}, u32[]{:S(2)}) collective-permute-start(f32[33,256]{1,0:T(8,128)S(1)} %slice_select_fusion), channel_id=1, source_target_pairs={{0,32},{16,48},{32,0},{48,16},{64,96},{80,112},{96,64},{112,80},{1... | collective-permute-start | bytes 101384 | tf_op jit(solution)/shard_map/ppermute | solution.py:122
  135.7 6.6 %collective-permute-start.6 = (f32[33,128]{1,0:T(8,128)S(1)}, f32[33,128]{1,0:T(8,128)S(1)}, u32[]{:S(2)}, u32[]{:S(2)}) collective-permute-start(f32[33,128]{1,0:T(8,128)S(1)} %slice_select_fusion.3), channel_id=1, source_target_pairs={{0,64},{16,80},{32,96},{48,112},{64,0},{80,16},{96,32},{112,48},{1... | collective-permute-start | bytes 50696 | tf_op jit(solution)/shard_map/ppermute | solution.py:122
  142.3 9.6 %collective-permute-start.7 = (f32[33,64]{1,0:T(8,128)S(1)}, f32[33,64]{1,0:T(8,128)S(1)}, u32[]{:S(2)}, u32[]{:S(2)}) collective-permute-start(f32[33,64]{1,0:T(8,128)S(1)} %slice_select_fusion.2), channel_id=1, source_target_pairs={{0,128},{16,144},{32,160},{48,176},{64,192},{80,208},{96,224},{112... | collective-permute-start | bytes 25352 | tf_op jit(solution)/shard_map/ppermute | solution.py:122
  152.1 14.4 %collective-permute-start.8 = (f32[33,32]{1,0:T(8,128)S(1)}, f32[33,32]{1,0:T(8,128)S(1)}, u32[]{:S(2)}, u32[]{:S(2)}) collective-permute-start(f32[33,32]{1,0:T(8,128)S(1)} %slice_select_fusion.1), channel_id=1, source_target_pairs={{0,256},{16,272},{32,288},{48,304},{64,320},{80,336},{96,352},{112... | collective-permute-start | bytes 12680 | tf_op jit(solution)/shard_map/ppermute | solution.py:122
  167.9 53.1 %copy-start.6 = (f32[32,32]{1,0:T(8,128)}, f32[32,32]{1,0:T(8,128)S(1)}, u32[]{:S(2)}) copy-start(f32[32,32]{1,0:T(8,128)S(1)} %pad_maximum_fusion.4) | copy-start | bytes 12292
  295.2 5.5 %collective-permute-start.9 = (f32[12,128]{1,0:T(8,128)S(1)}, f32[12,128]{1,0:T(8,128)S(1)}, u32[]{:S(2)}, u32[]{:S(2)}) collective-permute-start(f32[12,128]{1,0:T(8,128)S(1)} %reshape.185), channel_id=1, source_target_pairs={{0,1},{1,0},{2,3},{3,2},{4,5},{5,4},{6,7},{7,6},{8,9},{9,8},{10,11... | collective-permute-start | bytes 18440 | tf_op jit(solution)/shard_map/ppermute | solution.py:106
  300.8 7.0 %collective-permute-start.10 = (f32[12,128]{1,0:T(8,128)S(1)}, f32[12,128]{1,0:T(8,128)S(1)}, u32[]{:S(2)}, u32[]{:S(2)}) collective-permute-start(f32[12,128]{1,0:T(8,128)S(1)} %add.283), channel_id=1, source_target_pairs={{0,2},{1,3},{2,0},{3,1},{4,6},{5,7},{6,4},{7,5},{8,10},{9,11},{10,... | collective-permute-start | bytes 18440 | tf_op jit(solution)/shard_map/ppermute | solution.py:106
  307.8 5.5 %collective-permute-start.11 = (f32[12,128]{1,0:T(8,128)S(1)}, f32[12,128]{1,0:T(8,128)S(1)}, u32[]{:S(2)}, u32[]{:S(2)}) collective-permute-start(f32[12,128]{1,0:T(8,128)S(1)} %add.284), channel_id=1, source_target_pairs={{0,4},{1,5},{2,6},{3,7},{4,0},{5,1},{6,2},{7,3},{8,12},{9,13},{10,... | collective-permute-start | bytes 18440 | tf_op jit(solution)/shard_map/ppermute | solution.py:106
  313.3 7.0 %collective-permute-start.12 = (f32[12,128]{1,0:T(8,128)S(1)}, f32[12,128]{1,0:T(8,128)S(1)}, u32[]{:S(2)}, u32[]{:S(2)}) collective-permute-start(f32[12,128]{1,0:T(8,128)S(1)} %add.285), channel_id=1, source_target_pairs={{0,8},{1,9},{2,10},{3,11},{4,12},{5,13},{6,14},{7,15},{8,0},{9,1},... | collective-permute-start | bytes 18440 | tf_op jit(solution)/shard_map/ppermute | solution.py:106

commit v7 on v6

--- a/solution.py
+++ b/solution.py
@@ -12,8 +12,7 @@
 def sincos(angle):
     quarter = jnp.round(angle * (2.0 / math.pi))
     rest = angle - quarter * 1.5703125
-    rest = rest - quarter * 4.837512969970703125e-4
-    rest = rest - quarter * 7.54978995489188216e-8
+    rest = rest - quarter * 4.838267948966e-4
     rest_sq = rest * rest
     odd = rest + rest * rest_sq * (
         -1.6666654611e-1 + rest_sq * (8.3321608736e-3 + rest_sq * -1.9515295891e-4)
@@ -131,6 +130,39 @@
     return result
 
 
+def near_far_psum(value, axis, near):
+    count = lax.axis_size(axis)
+    me = lax.axis_index(axis)
+    shift = 1
+    while shift < near:
+        half = value.shape[1] // 2
+        low, high = value[:, :half], value[:, half:]
+        upper = (me // shift) % 2 == 1
+        keep = jnp.where(upper, high, low)
+        send = row_major(jnp.where(upper, low, high))
+        partner = [(index, index ^ shift) for index in range(count)]
+        value = keep + lax.ppermute(send, axis, partner)
+        shift *= 2
+    while shift < count:
+        value = row_major(value)
+        partner = [(index, index ^ shift) for index in range(count)]
+        value = value + lax.ppermute(value, axis, partner)
+        shift *= 2
+    shift = near // 2
+    while shift >= 1:
+        upper = (me // shift) % 2 == 1
+        value = row_major(value)
+        partner = [(index, index ^ shift) for index in range(count)]
+        other = lax.ppermute(value, axis, partner)
+        value = jnp.where(
+            upper,
+            jnp.concatenate([other, value], axis=1),
+            jnp.concatenate([value, other], axis=1),
+        )
+        shift //= 2
+    return value
+
+
 def split_three(value):
     high = lax.reduce_precision(value, exponent_bits=8, mantissa_bits=7)
     rest = value - high
@@ -158,9 +190,6 @@
     str_rows = strengths.shape[0]
     owned = jnp.concatenate([centroids, strengths, self_inv], axis=0)
     src_all = lax.all_gather(owned, "row", axis=1, tiled=True)
-    src_pos = src_all[:pos_rows]
-    src_str = src_all[pos_rows : pos_rows + str_rows]
-    src_inv = src_all[pos_rows + str_rows :]
     source_count = src_all.shape[1]
     panel_ids = lists.reshape(-1)
     owner_block = panel_ids // owned_count
@@ -172,13 +201,16 @@
         sum(((slot >> bit) & 1) << (row_bits - 1 - bit) for bit in range(row_bits))
         for slot in range(row_count)
     ]
-    table = src_all[: pos_rows + str_rows].reshape(-1, row_count, owned_count)
+    table = src_all.reshape(-1, row_count, owned_count)
     table = jnp.concatenate([table[:, slot] for slot in slot_order], axis=1)
+    src_pos = table[:pos_rows]
+    src_str = table[pos_rows : pos_rows + str_rows]
+    src_inv = table[pos_rows + str_rows :]
     onehot = (
         slot_ids[None, :] == lax.broadcasted_iota(jnp.int32, (source_count, slot_ids.shape[0]), 0)
     ).astype(jnp.bfloat16)
     near_all = join_three(
-        jnp.dot(split_three(table), onehot, preferred_element_type=jnp.float32)
+        jnp.dot(split_three(table[: pos_rows + str_rows]), onehot, preferred_element_type=jnp.float32)
     )
     near = near_all[:pos_rows]
     observer = jnp.repeat(field_pos, listed, axis=1)
@@ -216,13 +248,13 @@
     )
     misfit_part = jnp.sum(resid * resid)
     misfit_row = jnp.full((1, source_count), misfit_part, jnp.float32)
-    packed = halving_scatter(
-        jnp.concatenate([source_part, misfit_row], axis=0), "row"
+    packed = near_far_psum(
+        jnp.concatenate([source_part, misfit_row], axis=0), "row", min(8, row_count)
     )
     objective = packed[2 * freqs, 0] / (freqs * field_total) + 1e-06
-    source_own = packed[: 2 * freqs] / objective
-    mu_own = complex_times(source_own, self_inv, freqs)
-    mu_all = lax.all_gather(mu_own, "row", axis=1, tiled=True)
+    mu_all = complex_times(packed[: 2 * freqs] / objective, src_inv, freqs)
+    own_slot = bit_reverse(row_index, row_bits) * owned_count
+    mu_own = lax.dynamic_slice_in_dim(mu_all, own_slot, owned_count, 1)
     tgt_all = lax.all_gather(
         jnp.concatenate([centroids, strengths, mu_own], axis=0), "col", axis=1, tiled=True
     )

time: 324 us -> 305 us (0.941)
  blocking collectives: 89.9 us -> 61.6 us
  waiting for transfers between devices: 46.9 us -> 57.1 us
  starting transfers between devices: 42.6 us -> 48.7 us
  other arithmetic: 87.4 us -> 83.4 us
    all_gather x1 -> x0, blocking collectives: 28.5 us -> none  [on_device(): mu_all = lax.all_gather(mu_own, 'row', axis=1, tiled=True)]
    ppermute x5 -> x8, waiting for transfers between devices: 21.9 us -> 32 us  [the longest x2 13.6 us: near_far_psum(): value = value + lax.ppermute(value, axis, partner)]
    ppermute x5 -> x8, starting transfers between devices: 16.3 us -> 22.4 us  [the longest x2 10.3 us: near_far_psum(): value = value + lax.ppermute(value, axis, partner)]
    unnamed x33 -> x57, local copies, waits for them, and re-layouts: 5.05 us -> 6.8 us
  transfers between devices with their start and end apart: 13 -> 16, of which waited for: 13 -> 16; matrix products, arithmetic and copies ran while one was open for 0% -> 0% of each run, Pallas kernels for 0% -> 0%
where the time goes in v7:
time: 305 us; the launch traced here: 304 us
  other arithmetic  83.4 us (27%)
  blocking collectives  61.6 us (20%)
  waiting for transfers between devices  57.1 us (19%)
  starting transfers between devices  48.7 us (16%)
  matrix products  28.7 us (9%)
  local copies, waits for them, and re-layouts  20 us (7%)
  between operations  3.15 us (1%)
    reduce_sum x2, other arithmetic, pair_block(): weight = -jnp.sum(inner, axis=0) * (inverse * inverse * inverse)  66.9 us
    all_gather x1, blocking collectives, on_device(): src_all = lax.all_gather(owned, 'row', axis=1, tiled=True)  37.6 us
    ppermute x8, starting transfers between devices, xor_psum(): value = value + lax.ppermute(value, axis, partner)  26.3 us
    ppermute x8, waiting for transfers between devices, xor_psum(): value = value + lax.ppermute(value, axis, partner)  25.2 us
    all_gather x1, blocking collectives, on_device(): lax.all_gather(jnp.concatenate([centroids, strengths, mu_own], axis=0), '...  23.9 us
    dot_general x1, matrix products, on_device(): jnp.dot(split_three(table[:pos_rows + str_rows]), onehot, preferred_eleme...  14.5 us
    dot_general x1, matrix products, on_device(): lax.dot_general(split_three(terms), onehot, (((1,), (1,)), ((), ())), pre...  14 us
    ppermute x2, waiting for transfers between devices, near_far_psum(): value = value + lax.ppermute(value, axis, partner)  13.6 us
  transfers between devices with their start and end apart: 16, of which 16 were waited for; matrix products, arithmetic and copies ran while one was open for 0% of the time, Pallas kernels for 0%

profile of v7, /device:TPU:6, one launch (start us, length us, event | category | flops | bytes accessed | tf_op | source)
XLA Modules:
  0.0 304.2 jit_solution(15118258658204332863)
XLA Ops:
  3.0 37.6 %all_gather.6 = f32[67,1024]{0,1:T(8,128)S(1)} all-gather(f32[67,32]{0,1:T(8,128)S(1)} %pad_maximum_fusion.3), channel_id=1, replica_groups=mesh['row'=32,'col'=16] {'row'}, dimensions={1}, use_global_device_ids=true | all-gather | bytes 283008 | tf_op jit(solution)/shard_map/all_gather | solution.py:192
  45.5 14.5 %fusion.31 = f32[105,16384]{1,0:T(8,128)S(1)} fusion(s32[16384]{0:T(1024)S(1)} %fusion.70, bf16[35,1024]{1,0:T(8,128)(2,1)S(1)} %get-tuple-element.185, bf16[35,1024]{1,0:T(8,128)(2,1)S(1)} %get-tuple-element.186, bf16[35,1024]{1,0:T(8,128)(2,1)S(1)} %get-tuple-element.184), kind=kOutput, calls=%fused_computation.53 | convolution fusion | flops 3540637696 | bytes 7161856 | tf_op jit(solution)/shard_map/dot_general | solution.py:213
  63.0 3.1 %subtract_multiply_fusion.3 = (f32[16,16384]{1,0:T(8,128)}, f32[16,16384]{1,0:T(8,128)}) fusion(f32[35,16384]{1,0:T(8,128)S(1)} %slice_add_fusion, f32[16384]{0:T(1024)S(1)} %get-tuple-element.190, f32[16384]{0:T(1024)S(1)} %get-tuple-element.189, f32[16]{0:T(128)S(1)} %copy-done.5), kind=kLoop, calls=%fused_computation.107 | loop fusion | flops 12058624 | bytes 4325440 | tf_op jit(solution)/shard_map/mul | solution.py:225
  68.1 3.4 %reshape.182 = f32[16,256,64]{2,1,0:T(8,128)} reshape(f32[16,16384]{1,0:T(8,128)} %get-tuple-element.144) | data formatting | bytes 2097152 | tf_op jit(solution)/shard_map/reshape | solution.py:230
  74.4 3.5 %collective-permute-start = (f32[32,256]{1,0:T(8,128)S(1)}, f32[32,256]{1,0:T(8,128)S(1)}, u32[]{:S(2)}, u32[]{:S(2)}) collective-permute-start(f32[32,256]{1,0:T(8,128)S(1)} %pad_maximum_fusion.2), channel_id=1, source_target_pairs={{0,1},{1,0},{2,3},{3,2},{4,5},{5,4},{6,7},{7,6},{8,9},{9,8},{10,11... | collective-permute-start | bytes 98312 | tf_op jit(solution)/shard_map/ppermute | solution.py:105
  77.9 2.3 collective-permute-done
  80.2 5.1 %collective-permute-start.1 = (f32[32,256]{1,0:T(8,128)S(1)}, f32[32,256]{1,0:T(8,128)S(1)}, u32[]{:S(2)}, u32[]{:S(2)}) collective-permute-start(f32[32,256]{1,0:T(8,128)S(1)} %fusion.87), channel_id=1, source_target_pairs={{0,2},{1,3},{2,0},{3,1},{4,6},{5,7},{6,4},{7,5},{8,10},{9,11},{10,... | collective-permute-start | bytes 98312 | tf_op jit(solution)/shard_map/ppermute | solution.py:105
  87.5 2.7 collective-permute-start.2
  90.2 3.1 %collective-permute-done.2 = f32[32,256]{1,0:T(8,128)S(1)} collective-permute-done((f32[32,256]{1,0:T(8,128)S(1)}, f32[32,256]{1,0:T(8,128)S(1)}, u32[]{:S(2)}, u32[]{:S(2)}) %collective-permute-start.2) | collective-permute-done | bytes 32800 | tf_op jit(solution)/shard_map/ppermute | solution.py:105
  93.3 3.5 %collective-permute-start.3 = (f32[32,256]{1,0:T(8,128)S(1)}, f32[32,256]{1,0:T(8,128)S(1)}, u32[]{:S(2)}, u32[]{:S(2)}) collective-permute-start(f32[32,256]{1,0:T(8,128)S(1)} %add.264), channel_id=1, source_target_pairs={{0,8},{1,9},{2,10},{3,11},{4,12},{5,13},{6,14},{7,15},{8,0},{9,1},... | collective-permute-start | bytes 98312 | tf_op jit(solution)/shard_map/ppermute | solution.py:105
  96.8 4.0 %collective-permute-done.3 = f32[32,256]{1,0:T(8,128)S(1)} collective-permute-done((f32[32,256]{1,0:T(8,128)S(1)}, f32[32,256]{1,0:T(8,128)S(1)}, u32[]{:S(2)}, u32[]{:S(2)}) %collective-permute-start.3) | collective-permute-done | bytes 32800 | tf_op jit(solution)/shard_map/ppermute | solution.py:105
  104.9 2.9 add_multiply_fusion
  108.3 14.0 %fusion.30 = f32[96,1024]{1,0:T(8,128)S(1)} fusion(s32[16384]{0:T(1024)S(1)} %copy-done.3, bf16[32,16384]{1,0:T(8,128)(2,1)S(1)} %get-tuple-element.149, bf16[32,16384]{1,0:T(8,128)(2,1)S(1)} %get-tuple-element.148, bf16[32,16384]{1,0:T(8,128)(2,1)S(1)} %get-tuple-element.147), kind=kOutput, calls=%fused_computation.52 | convolution fusion | flops 3247439872 | bytes 3604480 | tf_op jit(solution)/shard_map/dot_general | solution.py:242
  128.8 3.9 %collective-permute-done.5 = f32[33,256]{1,0:T(8,128)S(1)} collective-permute-done((f32[33,256]{1,0:T(8,128)S(1)}, f32[33,256]{1,0:T(8,128)S(1)}, u32[]{:S(2)}, u32[]{:S(2)}) %collective-permute-start.5) | collective-permute-done | bytes 33824 | tf_op jit(solution)/shard_map/ppermute | solution.py:144
  134.9 4.4 %collective-permute-done.6 = f32[33,128]{1,0:T(8,128)S(1)} collective-permute-done((f32[33,128]{1,0:T(8,128)S(1)}, f32[33,128]{1,0:T(8,128)S(1)}, u32[]{:S(2)}, u32[]{:S(2)}) %collective-permute-start.6) | collective-permute-done | bytes 16928 | tf_op jit(solution)/shard_map/ppermute | solution.py:144
  139.4 3.1 %collective-permute-start.7 = (f32[33,128]{1,0:T(8,128)S(1)}, f32[33,128]{1,0:T(8,128)S(1)}, u32[]{:S(2)}, u32[]{:S(2)}) collective-permute-start(f32[33,128]{1,0:T(8,128)S(1)} %select_add_fusion.3), channel_id=1, source_target_pairs={{0,128},{16,144},{32,160},{48,176},{64,192},{80,208},{96,224},{112... | collective-permute-start | bytes 50696 | tf_op jit(solution)/shard_map/ppermute | solution.py:149
  142.4 6.5 %collective-permute-done.7 = f32[33,128]{1,0:T(8,128)S(1)} collective-permute-done((f32[33,128]{1,0:T(8,128)S(1)}, f32[33,128]{1,0:T(8,128)S(1)}, u32[]{:S(2)}, u32[]{:S(2)}) %collective-permute-start.7) | collective-permute-done | bytes 16928 | tf_op jit(solution)/shard_map/ppermute | solution.py:149
  148.9 7.3 %collective-permute-start.8 = (f32[33,128]{1,0:T(8,128)S(1)}, f32[33,128]{1,0:T(8,128)S(1)}, u32[]{:S(2)}, u32[]{:S(2)}) collective-permute-start(f32[33,128]{1,0:T(8,128)S(1)} %add.272), channel_id=1, source_target_pairs={{0,256},{16,272},{32,288},{48,304},{64,320},{80,336},{96,352},{112... | collective-permute-start | bytes 50696 | tf_op jit(solution)/shard_map/ppermute | solution.py:149
  156.2 7.1 %collective-permute-done.8 = f32[33,128]{1,0:T(8,128)S(1)} collective-permute-done((f32[33,128]{1,0:T(8,128)S(1)}, f32[33,128]{1,0:T(8,128)S(1)}, u32[]{:S(2)}, u32[]{:S(2)}) %collective-permute-start.8) | collective-permute-done | bytes 16928 | tf_op jit(solution)/shard_map/ppermute | solution.py:149
  165.5 4.4 %collective-permute-done.9 = f32[33,128]{1,0:T(8,128)S(1)} collective-permute-done((f32[33,128]{1,0:T(8,128)S(1)}, f32[33,128]{1,0:T(8,128)S(1)}, u32[]{:S(2)}, u32[]{:S(2)}) %collective-permute-start.9) | collective-permute-done | bytes 16928 | tf_op jit(solution)/shard_map/ppermute | solution.py:156
  172.0 3.8 %collective-permute-done.10 = f32[33,256]{1,0:T(8,128)S(1)} collective-permute-done((f32[33,256]{1,0:T(8,128)S(1)}, f32[33,256]{1,0:T(8,128)S(1)}, u32[]{:S(2)}, u32[]{:S(2)}) %collective-permute-start.10) | collective-permute-done | bytes 33824 | tf_op jit(solution)/shard_map/ppermute | solution.py:156
  180.5 23.9 %all_gather.7 = f32[67,512]{0,1:T(8,128)S(1)} all-gather(f32[67,32]{0,1:T(8,128)S(1)} %pad_maximum_fusion.5), channel_id=1, replica_groups=mesh['row'=32,'col'=16] {'col'}, dimensions={1}, use_global_device_ids=true | all-gather | bytes 145792 | tf_op jit(solution)/shard_map/all_gather | solution.py:258
  204.9 72.0 %while.11 = (s32[]{:T(128)}, f32[3,512]{1,0:T(4,128)S(1)}, f32[16]{0:T(128)S(1)}, f32[3,512]{1,0:T(4,128)S(1)}, s32[2]{0:T(128)S(1)}, /*index=5*/f32[3,1024]{1,0...) while((s32[]{:T(128)}, f32[3,512]{1,0:T(4,128)S(1)}, ...), condition=%wide.region_8.9_spmd.clone, body=%wide.region_4.8_spmd.clone.sunk | while | flops 257689088 | bytes 10285353 | solution.py:79
  206.8 33.4 %fusion.102 = f32[512,512]{1,0:T(8,128)S(1)} fusion(f32[16,512]{1,0:T(8,128)S(1)} %get-tuple-element.265, f32[16,512]{1,0:T(8,128)S(1)} %get-tuple-element.266, f32[16,512]{1,0:T(8,128)S(1)} %get-tuple-element.267, f32[16,512]{1,0:T(8,128)S(1)} %get-tuple-element.268, f32[16,512]{1,0:T(8,128)S(1)} %get-tuple-element.269, ...), kind=kLoop, calls=%fused_computation.24.clone.1 | loop fusion | flops 251396096 | bytes 2359360 | tf_op jit(solution)/shard_map/while/body/eval_jaxpr/reduce_sum | solution.py:59
  242.8 33.4 %fusion.102 = f32[512,512]{1,0:T(8,128)S(1)} fusion(f32[16,512]{1,0:T(8,128)S(1)} %get-tuple-element.265, f32[16,512]{1,0:T(8,128)S(1)} %get-tuple-element.266, f32[16,512]{1,0:T(8,128)S(1)} %get-tuple-element.267, f32[16,512]{1,0:T(8,128)S(1)} %get-tuple-element.268, f32[16,512]{1,0:T(8,128)S(1)} %get-tuple-element.269, ...), kind=kLoop, calls=%fused_computation.24.clone.1 | loop fusion | flops 251396096 | bytes 2359360 | tf_op jit(solution)/shard_map/while/body/eval_jaxpr/reduce_sum | solution.py:59
  279.2 3.5 %collective-permute-done.12 = f32[12,128]{1,0:T(8,128)S(1)} collective-permute-done((f32[12,128]{1,0:T(8,128)S(1)}, f32[12,128]{1,0:T(8,128)S(1)}, u32[]{:S(2)}, u32[]{:S(2)}) %collective-permute-start.12) | collective-permute-done | bytes 6176 | tf_op jit(solution)/shard_map/ppermute | solution.py:105
  282.7 3.4 %collective-permute-start.13 = (f32[12,128]{1,0:T(8,128)S(1)}, f32[12,128]{1,0:T(8,128)S(1)}, u32[]{:S(2)}, u32[]{:S(2)}) collective-permute-start(f32[12,128]{1,0:T(8,128)S(1)} %add.280), channel_id=1, source_target_pairs={{0,2},{1,3},{2,0},{3,1},{4,6},{5,7},{6,4},{7,5},{8,10},{9,11},{10,... | collective-permute-start | bytes 18440 | tf_op jit(solution)/shard_map/ppermute | solution.py:105
  286.1 3.7 %collective-permute-done.13 = f32[12,128]{1,0:T(8,128)S(1)} collective-permute-done((f32[12,128]{1,0:T(8,128)S(1)}, f32[12,128]{1,0:T(8,128)S(1)}, u32[]{:S(2)}, u32[]{:S(2)}) %collective-permute-start.13) | collective-permute-done | bytes 6176 | tf_op jit(solution)/shard_map/ppermute | solution.py:105
  289.8 2.7 collective-permute-start.14
  292.5 2.8 collective-permute-done.14
  295.3 3.4 %collective-permute-start.15 = (f32[12,128]{1,0:T(8,128)S(1)}, f32[12,128]{1,0:T(8,128)S(1)}, u32[]{:S(2)}, u32[]{:S(2)}) collective-permute-start(f32[12,128]{1,0:T(8,128)S(1)} %add.282), channel_id=1, source_target_pairs={{0,8},{1,9},{2,10},{3,11},{4,12},{5,13},{6,14},{7,15},{8,0},{9,1},... | collective-permute-start | bytes 18440 | tf_op jit(solution)/shard_map/ppermute | solution.py:105
  298.7 3.7 %collective-permute-done.15 = f32[12,128]{1,0:T(8,128)S(1)} collective-permute-done((f32[12,128]{1,0:T(8,128)S(1)}, f32[12,128]{1,0:T(8,128)S(1)}, u32[]{:S(2)}, u32[]{:S(2)}) %collective-permute-start.15) | collective-permute-done | bytes 6176 | tf_op jit(solution)/shard_map/ppermute | solution.py:105
  (147 shorter events, 45.6 us)
Async XLA Ops:
  45.4 14.5 %copy-start.2 = (s32[16384]{0:T(1024)}, s32[16384]{0:T(1024)S(1)}, u32[]{:S(2)}) copy-start(s32[16384]{0:T(1024)S(1)} %fusion.70) | copy-start | bytes 196612
  60.0 0.7 copy-start.8
  60.0 3.0 copy-start.5
  63.0 11.4 %copy-start = (f32[16384]{0:T(1024)}, f32[16384]{0:T(1024)S(1)}, u32[]{:S(2)}) copy-start(f32[16384]{0:T(1024)S(1)} %get-tuple-element.190) | copy-start | bytes 196612
  63.0 37.8 %copy-start.4 = (f32[32,256]{1,0:T(8,128)S(1)}, f32[32,256]{1,0:T(8,128)}, u32[]{:S(2)}) copy-start(f32[32,256]{1,0:T(8,128)} %param.15) | copy-start | bytes 98308
  74.4 5.8 %collective-permute-start = (f32[32,256]{1,0:T(8,128)S(1)}, f32[32,256]{1,0:T(8,128)S(1)}, u32[]{:S(2)}, u32[]{:S(2)}) collective-permute-start(f32[32,256]{1,0:T(8,128)S(1)} %pad_maximum_fusion.2), channel_id=1, source_target_pairs={{0,1},{1,0},{2,3},{3,2},{4,5},{5,4},{6,7},{7,6},{8,9},{9,8},{10,11... | collective-permute-start | bytes 98312 | tf_op jit(solution)/shard_map/ppermute | solution.py:105
  80.2 7.3 %collective-permute-start.1 = (f32[32,256]{1,0:T(8,128)S(1)}, f32[32,256]{1,0:T(8,128)S(1)}, u32[]{:S(2)}, u32[]{:S(2)}) collective-permute-start(f32[32,256]{1,0:T(8,128)S(1)} %fusion.87), channel_id=1, source_target_pairs={{0,2},{1,3},{2,0},{3,1},{4,6},{5,7},{6,4},{7,5},{8,10},{9,11},{10,... | collective-permute-start | bytes 98312 | tf_op jit(solution)/shard_map/ppermute | solution.py:105
  87.5 5.8 %collective-permute-start.2 = (f32[32,256]{1,0:T(8,128)S(1)}, f32[32,256]{1,0:T(8,128)S(1)}, u32[]{:S(2)}, u32[]{:S(2)}) collective-permute-start(f32[32,256]{1,0:T(8,128)S(1)} %add.263), channel_id=1, source_target_pairs={{0,4},{1,5},{2,6},{3,7},{4,0},{5,1},{6,2},{7,3},{8,12},{9,13},{10,... | collective-permute-start | bytes 98312 | tf_op jit(solution)/shard_map/ppermute | solution.py:105
  93.3 7.5 %collective-permute-start.3 = (f32[32,256]{1,0:T(8,128)S(1)}, f32[32,256]{1,0:T(8,128)S(1)}, u32[]{:S(2)}, u32[]{:S(2)}) collective-permute-start(f32[32,256]{1,0:T(8,128)S(1)} %add.264), channel_id=1, source_target_pairs={{0,8},{1,9},{2,10},{3,11},{4,12},{5,13},{6,14},{7,15},{8,0},{9,1},... | collective-permute-start | bytes 98312 | tf_op jit(solution)/shard_map/ppermute | solution.py:105
  104.9 3.4 %copy-start.3 = (s32[16384]{0:T(1024)S(1)}, s32[16384]{0:T(1024)}, u32[]{:S(2)}) copy-start(s32[16384]{0:T(1024)} %copy-done.2) | copy-start | bytes 196612
  108.3 63.6 %copy-start.7 = (s32[4,512]{1,0:T(4,128)S(1)}, s32[4,512]{1,0:T(4,128)}, u32[]{:S(2)}) copy-start(s32[4,512]{1,0:T(4,128)} %param.17) | copy-start | bytes 24580
  108.3 96.6 %copy-start.6 = (f32[16]{0:T(128)S(1)}, f32[16]{0:T(128)}, u32[]{:S(2)}) copy-start(f32[16]{0:T(128)} %param.13) | copy-start | bytes 196
  123.0 3.2 %collective-permute-start.4 = (f32[33,512]{1,0:T(8,128)S(1)}, f32[33,512]{1,0:T(8,128)S(1)}, u32[]{:S(2)}, u32[]{:S(2)}) collective-permute-start(f32[33,512]{1,0:T(8,128)S(1)} %broadcast_select_fusion), channel_id=1, source_target_pairs={{0,16},{16,0},{32,48},{48,32},{64,80},{80,64},{96,112},{112,96},{1... | collective-permute-start | bytes 202760 | tf_op jit(solution)/shard_map/ppermute | solution.py:144
  126.9 5.9 %collective-permute-start.5 = (f32[33,256]{1,0:T(8,128)S(1)}, f32[33,256]{1,0:T(8,128)S(1)}, u32[]{:S(2)}, u32[]{:S(2)}) collective-permute-start(f32[33,256]{1,0:T(8,128)S(1)} %slice_select_fusion), channel_id=1, source_target_pairs={{0,32},{16,48},{32,0},{48,16},{64,96},{80,112},{96,64},{112,80},{1... | collective-permute-start | bytes 101384 | tf_op jit(solution)/shard_map/ppermute | solution.py:144
  132.8 6.6 %collective-permute-start.6 = (f32[33,128]{1,0:T(8,128)S(1)}, f32[33,128]{1,0:T(8,128)S(1)}, u32[]{:S(2)}, u32[]{:S(2)}) collective-permute-start(f32[33,128]{1,0:T(8,128)S(1)} %slice_select_fusion.1), channel_id=1, source_target_pairs={{0,64},{16,80},{32,96},{48,112},{64,0},{80,16},{96,32},{112,48},{1... | collective-permute-start | bytes 50696 | tf_op jit(solution)/shard_map/ppermute | solution.py:144
  139.4 9.6 %collective-permute-start.7 = (f32[33,128]{1,0:T(8,128)S(1)}, f32[33,128]{1,0:T(8,128)S(1)}, u32[]{:S(2)}, u32[]{:S(2)}) collective-permute-start(f32[33,128]{1,0:T(8,128)S(1)} %select_add_fusion.3), channel_id=1, source_target_pairs={{0,128},{16,144},{32,160},{48,176},{64,192},{80,208},{96,224},{112... | collective-permute-start | bytes 50696 | tf_op jit(solution)/shard_map/ppermute | solution.py:149
  148.9 14.4 %collective-permute-start.8 = (f32[33,128]{1,0:T(8,128)S(1)}, f32[33,128]{1,0:T(8,128)S(1)}, u32[]{:S(2)}, u32[]{:S(2)}) collective-permute-start(f32[33,128]{1,0:T(8,128)S(1)} %add.272), channel_id=1, source_target_pairs={{0,256},{16,272},{32,288},{48,304},{64,320},{80,336},{96,352},{112... | collective-permute-start | bytes 50696 | tf_op jit(solution)/shard_map/ppermute | solution.py:149
  163.3 6.6 %collective-permute-start.9 = (f32[33,128]{1,0:T(8,128)S(1)}, f32[33,128]{1,0:T(8,128)S(1)}, u32[]{:S(2)}, u32[]{:S(2)}) collective-permute-start(f32[33,128]{1,0:T(8,128)S(1)} %add.273), channel_id=1, source_target_pairs={{0,64},{16,80},{32,96},{48,112},{64,0},{80,16},{96,32},{112,48},{1... | collective-permute-start | bytes 50696 | tf_op jit(solution)/shard_map/ppermute | solution.py:156
  169.9 5.9 %collective-permute-start.10 = (f32[33,256]{1,0:T(8,128)S(1)}, f32[33,256]{1,0:T(8,128)S(1)}, u32[]{:S(2)}, u32[]{:S(2)}) collective-permute-start(f32[33,256]{1,0:T(8,128)S(1)} %maximum_select_fusion.2), channel_id=1, source_target_pairs={{0,32},{16,48},{32,0},{48,16},{64,96},{80,112},{96,64},{112,80},{1... | collective-permute-start | bytes 101384 | tf_op jit(solution)/shard_map/ppermute | solution.py:156
  175.8 3.2 %collective-permute-start.11 = (f32[33,512]{1,0:T(8,128)S(1)}, f32[33,512]{1,0:T(8,128)S(1)}, u32[]{:S(2)}, u32[]{:S(2)}) collective-permute-start(f32[33,512]{1,0:T(8,128)S(1)} %maximum_select_fusion.1), channel_id=1, source_target_pairs={{0,16},{16,0},{32,48},{48,32},{64,80},{80,64},{96,112},{112,96},{1... | collective-permute-start | bytes 202760 | tf_op jit(solution)/shard_map/ppermute | solution.py:156
  180.3 24.6 %copy-start.1 = (f32[32,32]{1,0:T(8,128)}, f32[32,32]{1,0:T(8,128)S(1)}, u32[]{:S(2)}) copy-start(f32[32,32]{1,0:T(8,128)S(1)} %fusion.76) | copy-start | bytes 12292
  277.2 5.5 %collective-permute-start.12 = (f32[12,128]{1,0:T(8,128)S(1)}, f32[12,128]{1,0:T(8,128)S(1)}, u32[]{:S(2)}, u32[]{:S(2)}) collective-permute-start(f32[12,128]{1,0:T(8,128)S(1)} %reshape.185), channel_id=1, source_target_pairs={{0,1},{1,0},{2,3},{3,2},{4,5},{5,4},{6,7},{7,6},{8,9},{9,8},{10,11... | collective-permute-start | bytes 18440 | tf_op jit(solution)/shard_map/ppermute | solution.py:105
  282.7 7.0 %collective-permute-start.13 = (f32[12,128]{1,0:T(8,128)S(1)}, f32[12,128]{1,0:T(8,128)S(1)}, u32[]{:S(2)}, u32[]{:S(2)}) collective-permute-start(f32[12,128]{1,0:T(8,128)S(1)} %add.280), channel_id=1, source_target_pairs={{0,2},{1,3},{2,0},{3,1},{4,6},{5,7},{6,4},{7,5},{8,10},{9,11},{10,... | collective-permute-start | bytes 18440 | tf_op jit(solution)/shard_map/ppermute | solution.py:105
  289.8 5.5 %collective-permute-start.14 = (f32[12,128]{1,0:T(8,128)S(1)}, f32[12,128]{1,0:T(8,128)S(1)}, u32[]{:S(2)}, u32[]{:S(2)}) collective-permute-start(f32[12,128]{1,0:T(8,128)S(1)} %add.281), channel_id=1, source_target_pairs={{0,4},{1,5},{2,6},{3,7},{4,0},{5,1},{6,2},{7,3},{8,12},{9,13},{10,... | collective-permute-start | bytes 18440 | tf_op jit(solution)/shard_map/ppermute | solution.py:105
  295.3 7.0 %collective-permute-start.15 = (f32[12,128]{1,0:T(8,128)S(1)}, f32[12,128]{1,0:T(8,128)S(1)}, u32[]{:S(2)}, u32[]{:S(2)}) collective-permute-start(f32[12,128]{1,0:T(8,128)S(1)} %add.282), channel_id=1, source_target_pairs={{0,8},{1,9},{2,10},{3,11},{4,12},{5,13},{6,14},{7,15},{8,0},{9,1},... | collective-permute-start | bytes 18440 | tf_op jit(solution)/shard_map/ppermute | solution.py:105

commit v8 on v7

--- a/solution.py
+++ b/solution.py
@@ -9,7 +9,7 @@
 SOFT = 1.0
 
 
-def sincos(angle):
+def sincos_parts(angle):
     quarter = jnp.round(angle * (2.0 / math.pi))
     rest = angle - quarter * 1.5703125
     rest = rest - quarter * 4.838267948966e-4
@@ -24,7 +24,11 @@
         * rest_sq
         * (4.166664568298827e-2 + rest_sq * (-1.388731625493765e-3 + rest_sq * 2.443315711809948e-5))
     )
-    turn = quarter.astype(jnp.int32)
+    return odd, even, quarter.astype(jnp.int32)
+
+
+def sincos(angle):
+    odd, even, turn = sincos_parts(angle)
     swap = (turn & 1) == 1
     sine = jnp.where(swap, even, odd)
     cosine = jnp.where(swap, odd, even)
@@ -40,7 +44,7 @@
     inverse = lax.rsqrt(squared)
     distance = squared * inverse
     phase = wavenumbers[:, None, None] * distance[None]
-    sine, cosine = sincos(phase)
+    odd, even, turn = sincos_parts(phase)
     tgt_real = target_str[:freqs, None, :]
     tgt_imag = target_str[freqs:, None, :]
     tmu_real = target_mu[:freqs, None, :]
@@ -55,8 +59,12 @@
     prod_imag = (
         tmu_real * src_imag + tmu_imag * src_real + smu_real * tgt_imag + smu_imag * tgt_real
     )
-    inner = cosine * (prod_real + phase * prod_imag) + sine * (phase * prod_real - prod_imag)
-    weight = -jnp.sum(inner, axis=0) * (inverse * inverse * inverse)
+    first = prod_real + phase * prod_imag
+    second = phase * prod_real - prod_imag
+    swap = (turn & 1) == 1
+    inner = even * jnp.where(swap, second, first) + odd * jnp.where(swap, -first, second)
+    inner = jnp.where((turn & 2) == 2, inner, -inner)
+    weight = jnp.sum(inner, axis=0) * (inverse * inverse * inverse)
     return jnp.sum(weight[None] * offset, axis=1)
 
 

time: 305 us -> 301 us (0.987)
  other arithmetic: 83.4 us -> 79.2 us
    reduce_sum x2, other arithmetic: 66.9 us -> 62.6 us  [pair_block(): weight = jnp.sum(inner, axis=0) * (inverse * inverse * inverse)]
where the time goes in v8:
time: 301 us; the launch traced here: 300 us
  other arithmetic  79.2 us (26%)
  blocking collectives  61.6 us (20%)
  waiting for transfers between devices  57.1 us (19%)
  starting transfers between devices  48.7 us (16%)
  matrix products  28.7 us (10%)
  local copies, waits for them, and re-layouts  20 us (7%)
  between operations  3.15 us (1%)
    reduce_sum x2, other arithmetic, pair_block(): weight = jnp.sum(inner, axis=0) * (inverse * inverse * inverse)  62.6 us
    all_gather x1, blocking collectives, on_device(): src_all = lax.all_gather(owned, 'row', axis=1, tiled=True)  37.6 us
    ppermute x8, starting transfers between devices, xor_psum(): value = value + lax.ppermute(value, axis, partner)  26.3 us
    ppermute x8, waiting for transfers between devices, xor_psum(): value = value + lax.ppermute(value, axis, partner)  25.2 us
    all_gather x1, blocking collectives, on_device(): lax.all_gather(jnp.concatenate([centroids, strengths, mu_own], axis=0), '...  23.9 us
    dot_general x1, matrix products, on_device(): jnp.dot(split_three(table[:pos_rows + str_rows]), onehot, preferred_eleme...  14.5 us
    dot_general x1, matrix products, on_device(): lax.dot_general(split_three(terms), onehot, (((1,), (1,)), ((), ())), pre...  14 us
    ppermute x2, waiting for transfers between devices, near_far_psum(): value = value + lax.ppermute(value, axis, partner)  13.6 us
  transfers between devices with their start and end apart: 16, of which 16 were waited for; matrix products, arithmetic and copies ran while one was open for 0% of the time, Pallas kernels for 0%

profile of v8, /device:TPU:6, one launch (start us, length us, event | category | flops | bytes accessed | tf_op | source)
XLA Modules:
  0.0 299.9 jit_solution(16119635194111132445)
XLA Ops:
  3.0 37.6 %all_gather.6 = f32[67,1024]{0,1:T(8,128)S(1)} all-gather(f32[67,32]{0,1:T(8,128)S(1)} %pad_maximum_fusion.3), channel_id=1, replica_groups=mesh['row'=32,'col'=16] {'row'}, dimensions={1}, use_global_device_ids=true | all-gather | bytes 283008 | tf_op jit(solution)/shard_map/all_gather | solution.py:200
  45.5 14.5 %fusion.28 = f32[105,16384]{1,0:T(8,128)S(1)} fusion(s32[16384]{0:T(1024)S(1)} %fusion.67, bf16[35,1024]{1,0:T(8,128)(2,1)S(1)} %get-tuple-element.185, bf16[35,1024]{1,0:T(8,128)(2,1)S(1)} %get-tuple-element.186, bf16[35,1024]{1,0:T(8,128)(2,1)S(1)} %get-tuple-element.184), kind=kOutput, calls=%fused_computation.49 | convolution fusion | flops 3540637696 | bytes 7161856 | tf_op jit(solution)/shard_map/dot_general | solution.py:221
  63.0 3.1 %subtract_multiply_fusion.3 = (f32[16,16384]{1,0:T(8,128)}, f32[16,16384]{1,0:T(8,128)}) fusion(f32[35,16384]{1,0:T(8,128)S(1)} %slice_add_fusion, f32[16384]{0:T(1024)S(1)} %get-tuple-element.190, f32[16384]{0:T(1024)S(1)} %get-tuple-element.189, f32[16]{0:T(128)S(1)} %copy-done.5), kind=kLoop, calls=%fused_computation.103 | loop fusion | flops 12058624 | bytes 4325440 | tf_op jit(solution)/shard_map/mul | solution.py:233
  68.1 3.4 %reshape.181 = f32[16,256,64]{2,1,0:T(8,128)} reshape(f32[16,16384]{1,0:T(8,128)} %get-tuple-element.144) | data formatting | bytes 2097152 | tf_op jit(solution)/shard_map/reshape | solution.py:238
  74.4 3.5 %collective-permute-start = (f32[32,256]{1,0:T(8,128)S(1)}, f32[32,256]{1,0:T(8,128)S(1)}, u32[]{:S(2)}, u32[]{:S(2)}) collective-permute-start(f32[32,256]{1,0:T(8,128)S(1)} %pad_maximum_fusion.2), channel_id=1, source_target_pairs={{0,1},{1,0},{2,3},{3,2},{4,5},{5,4},{6,7},{7,6},{8,9},{9,8},{10,11... | collective-permute-start | bytes 98312 | tf_op jit(solution)/shard_map/ppermute | solution.py:113
  77.9 2.3 collective-permute-done
  80.2 5.1 %collective-permute-start.1 = (f32[32,256]{1,0:T(8,128)S(1)}, f32[32,256]{1,0:T(8,128)S(1)}, u32[]{:S(2)}, u32[]{:S(2)}) collective-permute-start(f32[32,256]{1,0:T(8,128)S(1)} %fusion.84), channel_id=1, source_target_pairs={{0,2},{1,3},{2,0},{3,1},{4,6},{5,7},{6,4},{7,5},{8,10},{9,11},{10,... | collective-permute-start | bytes 98312 | tf_op jit(solution)/shard_map/ppermute | solution.py:113
  87.5 2.7 collective-permute-start.2
  90.2 3.1 %collective-permute-done.2 = f32[32,256]{1,0:T(8,128)S(1)} collective-permute-done((f32[32,256]{1,0:T(8,128)S(1)}, f32[32,256]{1,0:T(8,128)S(1)}, u32[]{:S(2)}, u32[]{:S(2)}) %collective-permute-start.2) | collective-permute-done | bytes 32800 | tf_op jit(solution)/shard_map/ppermute | solution.py:113
  93.3 3.5 %collective-permute-start.3 = (f32[32,256]{1,0:T(8,128)S(1)}, f32[32,256]{1,0:T(8,128)S(1)}, u32[]{:S(2)}, u32[]{:S(2)}) collective-permute-start(f32[32,256]{1,0:T(8,128)S(1)} %add.261), channel_id=1, source_target_pairs={{0,8},{1,9},{2,10},{3,11},{4,12},{5,13},{6,14},{7,15},{8,0},{9,1},... | collective-permute-start | bytes 98312 | tf_op jit(solution)/shard_map/ppermute | solution.py:113
  96.8 4.0 %collective-permute-done.3 = f32[32,256]{1,0:T(8,128)S(1)} collective-permute-done((f32[32,256]{1,0:T(8,128)S(1)}, f32[32,256]{1,0:T(8,128)S(1)}, u32[]{:S(2)}, u32[]{:S(2)}) %collective-permute-start.3) | collective-permute-done | bytes 32800 | tf_op jit(solution)/shard_map/ppermute | solution.py:113
  104.9 2.9 add_multiply_fusion
  108.3 14.0 %fusion.27 = f32[96,1024]{1,0:T(8,128)S(1)} fusion(s32[16384]{0:T(1024)S(1)} %copy-done.3, bf16[32,16384]{1,0:T(8,128)(2,1)S(1)} %get-tuple-element.149, bf16[32,16384]{1,0:T(8,128)(2,1)S(1)} %get-tuple-element.148, bf16[32,16384]{1,0:T(8,128)(2,1)S(1)} %get-tuple-element.147), kind=kOutput, calls=%fused_computation.48 | convolution fusion | flops 3247439872 | bytes 3604480 | tf_op jit(solution)/shard_map/dot_general | solution.py:250
  128.8 3.9 %collective-permute-done.5 = f32[33,256]{1,0:T(8,128)S(1)} collective-permute-done((f32[33,256]{1,0:T(8,128)S(1)}, f32[33,256]{1,0:T(8,128)S(1)}, u32[]{:S(2)}, u32[]{:S(2)}) %collective-permute-start.5) | collective-permute-done | bytes 33824 | tf_op jit(solution)/shard_map/ppermute | solution.py:152
  134.9 4.4 %collective-permute-done.6 = f32[33,128]{1,0:T(8,128)S(1)} collective-permute-done((f32[33,128]{1,0:T(8,128)S(1)}, f32[33,128]{1,0:T(8,128)S(1)}, u32[]{:S(2)}, u32[]{:S(2)}) %collective-permute-start.6) | collective-permute-done | bytes 16928 | tf_op jit(solution)/shard_map/ppermute | solution.py:152
  139.4 3.1 %collective-permute-start.7 = (f32[33,128]{1,0:T(8,128)S(1)}, f32[33,128]{1,0:T(8,128)S(1)}, u32[]{:S(2)}, u32[]{:S(2)}) collective-permute-start(f32[33,128]{1,0:T(8,128)S(1)} %select_add_fusion.3), channel_id=1, source_target_pairs={{0,128},{16,144},{32,160},{48,176},{64,192},{80,208},{96,224},{112... | collective-permute-start | bytes 50696 | tf_op jit(solution)/shard_map/ppermute | solution.py:157
  142.4 6.5 %collective-permute-done.7 = f32[33,128]{1,0:T(8,128)S(1)} collective-permute-done((f32[33,128]{1,0:T(8,128)S(1)}, f32[33,128]{1,0:T(8,128)S(1)}, u32[]{:S(2)}, u32[]{:S(2)}) %collective-permute-start.7) | collective-permute-done | bytes 16928 | tf_op jit(solution)/shard_map/ppermute | solution.py:157
  148.9 7.3 %collective-permute-start.8 = (f32[33,128]{1,0:T(8,128)S(1)}, f32[33,128]{1,0:T(8,128)S(1)}, u32[]{:S(2)}, u32[]{:S(2)}) collective-permute-start(f32[33,128]{1,0:T(8,128)S(1)} %add.269), channel_id=1, source_target_pairs={{0,256},{16,272},{32,288},{48,304},{64,320},{80,336},{96,352},{112... | collective-permute-start | bytes 50696 | tf_op jit(solution)/shard_map/ppermute | solution.py:157
  156.2 7.1 %collective-permute-done.8 = f32[33,128]{1,0:T(8,128)S(1)} collective-permute-done((f32[33,128]{1,0:T(8,128)S(1)}, f32[33,128]{1,0:T(8,128)S(1)}, u32[]{:S(2)}, u32[]{:S(2)}) %collective-permute-start.8) | collective-permute-done | bytes 16928 | tf_op jit(solution)/shard_map/ppermute | solution.py:157
  165.5 4.4 %collective-permute-done.9 = f32[33,128]{1,0:T(8,128)S(1)} collective-permute-done((f32[33,128]{1,0:T(8,128)S(1)}, f32[33,128]{1,0:T(8,128)S(1)}, u32[]{:S(2)}, u32[]{:S(2)}) %collective-permute-start.9) | collective-permute-done | bytes 16928 | tf_op jit(solution)/shard_map/ppermute | solution.py:164
  172.0 3.8 %collective-permute-done.10 = f32[33,256]{1,0:T(8,128)S(1)} collective-permute-done((f32[33,256]{1,0:T(8,128)S(1)}, f32[33,256]{1,0:T(8,128)S(1)}, u32[]{:S(2)}, u32[]{:S(2)}) %collective-permute-start.10) | collective-permute-done | bytes 33824 | tf_op jit(solution)/shard_map/ppermute | solution.py:164
  180.5 23.9 %all_gather.7 = f32[67,512]{0,1:T(8,128)S(1)} all-gather(f32[67,32]{0,1:T(8,128)S(1)} %pad_maximum_fusion.5), channel_id=1, replica_groups=mesh['row'=32,'col'=16] {'col'}, dimensions={1}, use_global_device_ids=true | all-gather | bytes 145792 | tf_op jit(solution)/shard_map/all_gather | solution.py:266
  204.9 67.7 %while.11 = (s32[]{:T(128)}, f32[3,512]{1,0:T(4,128)S(1)}, f32[16]{0:T(128)S(1)}, f32[3,512]{1,0:T(4,128)S(1)}, s32[2]{0:T(128)S(1)}, /*index=5*/f32[3,1024]{1,0...) while((s32[]{:T(128)}, f32[3,512]{1,0:T(4,128)S(1)}, ...), condition=%wide.region_8.9_spmd.clone, body=%wide.region_4.8_spmd.clone.sunk | while | flops 240649728 | bytes 10285353 | solution.py:87
  206.8 31.3 %fusion.99 = f32[512,512]{1,0:T(8,128)S(1)} fusion(f32[16,512]{1,0:T(8,128)S(1)} %get-tuple-element.265, f32[16,512]{1,0:T(8,128)S(1)} %get-tuple-element.266, f32[16,512]{1,0:T(8,128)S(1)} %get-tuple-element.267, f32[16,512]{1,0:T(8,128)S(1)} %get-tuple-element.268, f32[16,512]{1,0:T(8,128)S(1)} %get-tuple-element.269, ...), kind=kLoop, calls=%fused_computation.35.clone.1 | loop fusion | flops 234618880 | bytes 2359360 | tf_op jit(solution)/shard_map/while/body/eval_jaxpr/reduce_sum | solution.py:67
  240.6 31.3 %fusion.99 = f32[512,512]{1,0:T(8,128)S(1)} fusion(f32[16,512]{1,0:T(8,128)S(1)} %get-tuple-element.265, f32[16,512]{1,0:T(8,128)S(1)} %get-tuple-element.266, f32[16,512]{1,0:T(8,128)S(1)} %get-tuple-element.267, f32[16,512]{1,0:T(8,128)S(1)} %get-tuple-element.268, f32[16,512]{1,0:T(8,128)S(1)} %get-tuple-element.269, ...), kind=kLoop, calls=%fused_computation.35.clone.1 | loop fusion | flops 234618880 | bytes 2359360 | tf_op jit(solution)/shard_map/while/body/eval_jaxpr/reduce_sum | solution.py:67
  275.0 3.5 %collective-permute-done.12 = f32[12,128]{1,0:T(8,128)S(1)} collective-permute-done((f32[12,128]{1,0:T(8,128)S(1)}, f32[12,128]{1,0:T(8,128)S(1)}, u32[]{:S(2)}, u32[]{:S(2)}) %collective-permute-start.12) | collective-permute-done | bytes 6176 | tf_op jit(solution)/shard_map/ppermute | solution.py:113
  278.5 3.4 %collective-permute-start.13 = (f32[12,128]{1,0:T(8,128)S(1)}, f32[12,128]{1,0:T(8,128)S(1)}, u32[]{:S(2)}, u32[]{:S(2)}) collective-permute-start(f32[12,128]{1,0:T(8,128)S(1)} %add.277), channel_id=1, source_target_pairs={{0,2},{1,3},{2,0},{3,1},{4,6},{5,7},{6,4},{7,5},{8,10},{9,11},{10,... | collective-permute-start | bytes 18440 | tf_op jit(solution)/shard_map/ppermute | solution.py:113
  281.8 3.7 %collective-permute-done.13 = f32[12,128]{1,0:T(8,128)S(1)} collective-permute-done((f32[12,128]{1,0:T(8,128)S(1)}, f32[12,128]{1,0:T(8,128)S(1)}, u32[]{:S(2)}, u32[]{:S(2)}) %collective-permute-start.13) | collective-permute-done | bytes 6176 | tf_op jit(solution)/shard_map/ppermute | solution.py:113
  285.5 2.7 collective-permute-start.14
  288.2 2.8 collective-permute-done.14
  291.0 3.4 %collective-permute-start.15 = (f32[12,128]{1,0:T(8,128)S(1)}, f32[12,128]{1,0:T(8,128)S(1)}, u32[]{:S(2)}, u32[]{:S(2)}) collective-permute-start(f32[12,128]{1,0:T(8,128)S(1)} %add.279), channel_id=1, source_target_pairs={{0,8},{1,9},{2,10},{3,11},{4,12},{5,13},{6,14},{7,15},{8,0},{9,1},... | collective-permute-start | bytes 18440 | tf_op jit(solution)/shard_map/ppermute | solution.py:113
  294.4 3.7 %collective-permute-done.15 = f32[12,128]{1,0:T(8,128)S(1)} collective-permute-done((f32[12,128]{1,0:T(8,128)S(1)}, f32[12,128]{1,0:T(8,128)S(1)}, u32[]{:S(2)}, u32[]{:S(2)}) %collective-permute-start.15) | collective-permute-done | bytes 6176 | tf_op jit(solution)/shard_map/ppermute | solution.py:113
  (147 shorter events, 45.5 us)
Async XLA Ops:
  45.4 14.5 %copy-start.2 = (s32[16384]{0:T(1024)}, s32[16384]{0:T(1024)S(1)}, u32[]{:S(2)}) copy-start(s32[16384]{0:T(1024)S(1)} %fusion.67) | copy-start | bytes 196612
  60.0 0.7 copy-start.8
  60.0 3.0 copy-start.5
  63.0 11.4 %copy-start = (f32[16384]{0:T(1024)}, f32[16384]{0:T(1024)S(1)}, u32[]{:S(2)}) copy-start(f32[16384]{0:T(1024)S(1)} %get-tuple-element.190) | copy-start | bytes 196612
  63.0 37.8 %copy-start.4 = (f32[32,256]{1,0:T(8,128)S(1)}, f32[32,256]{1,0:T(8,128)}, u32[]{:S(2)}) copy-start(f32[32,256]{1,0:T(8,128)} %param.15) | copy-start | bytes 98308
  74.4 5.8 %collective-permute-start = (f32[32,256]{1,0:T(8,128)S(1)}, f32[32,256]{1,0:T(8,128)S(1)}, u32[]{:S(2)}, u32[]{:S(2)}) collective-permute-start(f32[32,256]{1,0:T(8,128)S(1)} %pad_maximum_fusion.2), channel_id=1, source_target_pairs={{0,1},{1,0},{2,3},{3,2},{4,5},{5,4},{6,7},{7,6},{8,9},{9,8},{10,11... | collective-permute-start | bytes 98312 | tf_op jit(solution)/shard_map/ppermute | solution.py:113
  80.2 7.3 %collective-permute-start.1 = (f32[32,256]{1,0:T(8,128)S(1)}, f32[32,256]{1,0:T(8,128)S(1)}, u32[]{:S(2)}, u32[]{:S(2)}) collective-permute-start(f32[32,256]{1,0:T(8,128)S(1)} %fusion.84), channel_id=1, source_target_pairs={{0,2},{1,3},{2,0},{3,1},{4,6},{5,7},{6,4},{7,5},{8,10},{9,11},{10,... | collective-permute-start | bytes 98312 | tf_op jit(solution)/shard_map/ppermute | solution.py:113
  87.5 5.8 %collective-permute-start.2 = (f32[32,256]{1,0:T(8,128)S(1)}, f32[32,256]{1,0:T(8,128)S(1)}, u32[]{:S(2)}, u32[]{:S(2)}) collective-permute-start(f32[32,256]{1,0:T(8,128)S(1)} %add.260), channel_id=1, source_target_pairs={{0,4},{1,5},{2,6},{3,7},{4,0},{5,1},{6,2},{7,3},{8,12},{9,13},{10,... | collective-permute-start | bytes 98312 | tf_op jit(solution)/shard_map/ppermute | solution.py:113
  93.3 7.5 %collective-permute-start.3 = (f32[32,256]{1,0:T(8,128)S(1)}, f32[32,256]{1,0:T(8,128)S(1)}, u32[]{:S(2)}, u32[]{:S(2)}) collective-permute-start(f32[32,256]{1,0:T(8,128)S(1)} %add.261), channel_id=1, source_target_pairs={{0,8},{1,9},{2,10},{3,11},{4,12},{5,13},{6,14},{7,15},{8,0},{9,1},... | collective-permute-start | bytes 98312 | tf_op jit(solution)/shard_map/ppermute | solution.py:113
  104.9 3.4 %copy-start.3 = (s32[16384]{0:T(1024)S(1)}, s32[16384]{0:T(1024)}, u32[]{:S(2)}) copy-start(s32[16384]{0:T(1024)} %copy-done.2) | copy-start | bytes 196612
  108.3 63.6 %copy-start.7 = (s32[4,512]{1,0:T(4,128)S(1)}, s32[4,512]{1,0:T(4,128)}, u32[]{:S(2)}) copy-start(s32[4,512]{1,0:T(4,128)} %param.17) | copy-start | bytes 24580
  108.3 96.6 %copy-start.6 = (f32[16]{0:T(128)S(1)}, f32[16]{0:T(128)}, u32[]{:S(2)}) copy-start(f32[16]{0:T(128)} %param.13) | copy-start | bytes 196
  123.0 3.2 %collective-permute-start.4 = (f32[33,512]{1,0:T(8,128)S(1)}, f32[33,512]{1,0:T(8,128)S(1)}, u32[]{:S(2)}, u32[]{:S(2)}) collective-permute-start(f32[33,512]{1,0:T(8,128)S(1)} %broadcast_select_fusion), channel_id=1, source_target_pairs={{0,16},{16,0},{32,48},{48,32},{64,80},{80,64},{96,112},{112,96},{1... | collective-permute-start | bytes 202760 | tf_op jit(solution)/shard_map/ppermute | solution.py:152
  126.9 5.9 %collective-permute-start.5 = (f32[33,256]{1,0:T(8,128)S(1)}, f32[33,256]{1,0:T(8,128)S(1)}, u32[]{:S(2)}, u32[]{:S(2)}) collective-permute-start(f32[33,256]{1,0:T(8,128)S(1)} %slice_select_fusion), channel_id=1, source_target_pairs={{0,32},{16,48},{32,0},{48,16},{64,96},{80,112},{96,64},{112,80},{1... | collective-permute-start | bytes 101384 | tf_op jit(solution)/shard_map/ppermute | solution.py:152
  132.8 6.6 %collective-permute-start.6 = (f32[33,128]{1,0:T(8,128)S(1)}, f32[33,128]{1,0:T(8,128)S(1)}, u32[]{:S(2)}, u32[]{:S(2)}) collective-permute-start(f32[33,128]{1,0:T(8,128)S(1)} %slice_select_fusion.1), channel_id=1, source_target_pairs={{0,64},{16,80},{32,96},{48,112},{64,0},{80,16},{96,32},{112,48},{1... | collective-permute-start | bytes 50696 | tf_op jit(solution)/shard_map/ppermute | solution.py:152
  139.4 9.6 %collective-permute-start.7 = (f32[33,128]{1,0:T(8,128)S(1)}, f32[33,128]{1,0:T(8,128)S(1)}, u32[]{:S(2)}, u32[]{:S(2)}) collective-permute-start(f32[33,128]{1,0:T(8,128)S(1)} %select_add_fusion.3), channel_id=1, source_target_pairs={{0,128},{16,144},{32,160},{48,176},{64,192},{80,208},{96,224},{112... | collective-permute-start | bytes 50696 | tf_op jit(solution)/shard_map/ppermute | solution.py:157
  148.9 14.4 %collective-permute-start.8 = (f32[33,128]{1,0:T(8,128)S(1)}, f32[33,128]{1,0:T(8,128)S(1)}, u32[]{:S(2)}, u32[]{:S(2)}) collective-permute-start(f32[33,128]{1,0:T(8,128)S(1)} %add.269), channel_id=1, source_target_pairs={{0,256},{16,272},{32,288},{48,304},{64,320},{80,336},{96,352},{112... | collective-permute-start | bytes 50696 | tf_op jit(solution)/shard_map/ppermute | solution.py:157
  163.3 6.6 %collective-permute-start.9 = (f32[33,128]{1,0:T(8,128)S(1)}, f32[33,128]{1,0:T(8,128)S(1)}, u32[]{:S(2)}, u32[]{:S(2)}) collective-permute-start(f32[33,128]{1,0:T(8,128)S(1)} %add.270), channel_id=1, source_target_pairs={{0,64},{16,80},{32,96},{48,112},{64,0},{80,16},{96,32},{112,48},{1... | collective-permute-start | bytes 50696 | tf_op jit(solution)/shard_map/ppermute | solution.py:164
  169.9 5.9 %collective-permute-start.10 = (f32[33,256]{1,0:T(8,128)S(1)}, f32[33,256]{1,0:T(8,128)S(1)}, u32[]{:S(2)}, u32[]{:S(2)}) collective-permute-start(f32[33,256]{1,0:T(8,128)S(1)} %maximum_select_fusion.2), channel_id=1, source_target_pairs={{0,32},{16,48},{32,0},{48,16},{64,96},{80,112},{96,64},{112,80},{1... | collective-permute-start | bytes 101384 | tf_op jit(solution)/shard_map/ppermute | solution.py:164
  175.8 3.2 %collective-permute-start.11 = (f32[33,512]{1,0:T(8,128)S(1)}, f32[33,512]{1,0:T(8,128)S(1)}, u32[]{:S(2)}, u32[]{:S(2)}) collective-permute-start(f32[33,512]{1,0:T(8,128)S(1)} %maximum_select_fusion.1), channel_id=1, source_target_pairs={{0,16},{16,0},{32,48},{48,32},{64,80},{80,64},{96,112},{112,96},{1... | collective-permute-start | bytes 202760 | tf_op jit(solution)/shard_map/ppermute | solution.py:164
  180.3 24.6 %copy-start.1 = (f32[32,32]{1,0:T(8,128)}, f32[32,32]{1,0:T(8,128)S(1)}, u32[]{:S(2)}) copy-start(f32[32,32]{1,0:T(8,128)S(1)} %fusion.73) | copy-start | bytes 12292
  272.9 5.5 %collective-permute-start.12 = (f32[12,128]{1,0:T(8,128)S(1)}, f32[12,128]{1,0:T(8,128)S(1)}, u32[]{:S(2)}, u32[]{:S(2)}) collective-permute-start(f32[12,128]{1,0:T(8,128)S(1)} %reshape.184), channel_id=1, source_target_pairs={{0,1},{1,0},{2,3},{3,2},{4,5},{5,4},{6,7},{7,6},{8,9},{9,8},{10,11... | collective-permute-start | bytes 18440 | tf_op jit(solution)/shard_map/ppermute | solution.py:113
  278.5 7.0 %collective-permute-start.13 = (f32[12,128]{1,0:T(8,128)S(1)}, f32[12,128]{1,0:T(8,128)S(1)}, u32[]{:S(2)}, u32[]{:S(2)}) collective-permute-start(f32[12,128]{1,0:T(8,128)S(1)} %add.277), channel_id=1, source_target_pairs={{0,2},{1,3},{2,0},{3,1},{4,6},{5,7},{6,4},{7,5},{8,10},{9,11},{10,... | collective-permute-start | bytes 18440 | tf_op jit(solution)/shard_map/ppermute | solution.py:113
  285.5 5.5 %collective-permute-start.14 = (f32[12,128]{1,0:T(8,128)S(1)}, f32[12,128]{1,0:T(8,128)S(1)}, u32[]{:S(2)}, u32[]{:S(2)}) collective-permute-start(f32[12,128]{1,0:T(8,128)S(1)} %add.278), channel_id=1, source_target_pairs={{0,4},{1,5},{2,6},{3,7},{4,0},{5,1},{6,2},{7,3},{8,12},{9,13},{10,... | collective-permute-start | bytes 18440 | tf_op jit(solution)/shard_map/ppermute | solution.py:113
  291.0 7.0 %collective-permute-start.15 = (f32[12,128]{1,0:T(8,128)S(1)}, f32[12,128]{1,0:T(8,128)S(1)}, u32[]{:S(2)}, u32[]{:S(2)}) collective-permute-start(f32[12,128]{1,0:T(8,128)S(1)} %add.279), channel_id=1, source_target_pairs={{0,8},{1,9},{2,10},{3,11},{4,12},{5,13},{6,14},{7,15},{8,0},{9,1},... | collective-permute-start | bytes 18440 | tf_op jit(solution)/shard_map/ppermute | solution.py:113

commit v9 on v8

--- a/solution.py
+++ b/solution.py
@@ -138,7 +138,7 @@
     return result
 
 
-def near_far_psum(value, axis, near):
+def near_far_reduce(value, axis, near):
     count = lax.axis_size(axis)
     me = lax.axis_index(axis)
     shift = 1
@@ -156,8 +156,13 @@
         partner = [(index, index ^ shift) for index in range(count)]
         value = value + lax.ppermute(value, axis, partner)
         shift *= 2
-    shift = near // 2
-    while shift >= 1:
+    return value
+
+
+def doubling_gather(value, axis, shifts):
+    count = lax.axis_size(axis)
+    me = lax.axis_index(axis)
+    for shift in shifts:
         upper = (me // shift) % 2 == 1
         value = row_major(value)
         partner = [(index, index ^ shift) for index in range(count)]
@@ -167,8 +172,16 @@
             jnp.concatenate([other, value], axis=1),
             jnp.concatenate([value, other], axis=1),
         )
+    return value
+
+
+def near_shifts(near):
+    shifts = []
+    shift = near // 2
+    while shift >= 1:
+        shifts.append(shift)
         shift //= 2
-    return value
+    return shifts
 
 
 def split_three(value):
@@ -256,15 +269,21 @@
     )
     misfit_part = jnp.sum(resid * resid)
     misfit_row = jnp.full((1, source_count), misfit_part, jnp.float32)
-    packed = near_far_psum(
-        jnp.concatenate([source_part, misfit_row], axis=0), "row", min(8, row_count)
-    )
-    objective = packed[2 * freqs, 0] / (freqs * field_total) + 1e-06
+    near = min(8, row_count)
+    chunk = near_far_reduce(jnp.concatenate([source_part, misfit_row], axis=0), "row", near)
+    objective = chunk[2 * freqs, 0] / (freqs * field_total) + 1e-06
+    own_slot = bit_reverse(row_index, row_bits) * owned_count
+    own_offset = own_slot % chunk.shape[1]
+    mu_own = complex_times(
+        lax.dynamic_slice_in_dim(chunk[: 2 * freqs], own_offset, owned_count, 1) / objective,
+        self_inv,
+        freqs,
+    )
+    packed = doubling_gather(chunk, "row", near_shifts(near))
     mu_all = complex_times(packed[: 2 * freqs] / objective, src_inv, freqs)
-    own_slot = bit_reverse(row_index, row_bits) * owned_count
-    mu_own = lax.dynamic_slice_in_dim(mu_all, own_slot, owned_count, 1)
-    tgt_all = lax.all_gather(
-        jnp.concatenate([centroids, strengths, mu_own], axis=0), "col", axis=1, tiled=True
+    col_shifts = [1 << bit for bit in range(max(col_count - 1, 0).bit_length())]
+    tgt_all = doubling_gather(
+        jnp.concatenate([centroids, strengths, mu_own], axis=0), "col", col_shifts
     )
     tgt_pos = tgt_all[:pos_rows]
     tgt_str = tgt_all[pos_rows : pos_rows + str_rows]

time: 301 us -> 288 us (0.957)
  blocking collectives: 61.6 us -> 37.6 us
  starting transfers between devices: 48.7 us -> 65.6 us
  waiting for transfers between devices: 57.1 us -> 51.2 us
    all_gather x1 -> x0, blocking collectives: 23.9 us -> none  [on_device(): lax.all_gather(jnp.concatenate([centroids, strengths, mu_own], axis=0), '...]
    ppermute x8 -> x12, starting transfers between devices: 22.4 us -> 37.1 us  [the longest x7 20.8 us: doubling_gather(): other = lax.ppermute(value, axis, partner)]
    ppermute x8 -> x12, waiting for transfers between devices: 32 us -> 28.8 us  [the longest x2 13.6 us: near_far_reduce(): value = value + lax.ppermute(value, axis, partner)]
    unnamed x57 -> x56, local copies, waits for them, and re-layouts: 6.8 us -> 6.47 us
  transfers between devices with their start and end apart: 16 -> 20, of which waited for: 16 -> 17; matrix products, arithmetic and copies ran while one was open for 0% -> 1% of each run, Pallas kernels for 0% -> 0%
where the time goes in v9:
time: 288 us; the launch traced here: 287 us
  other arithmetic  79.8 us (28%)
  starting transfers between devices  65.6 us (23%)
  waiting for transfers between devices  51.2 us (18%)
  blocking collectives  37.6 us (13%)
  matrix products  28.7 us (10%)
  local copies, waits for them, and re-layouts  19.4 us (7%)
  between operations  3.41 us (1%)
    reduce_sum x2, other arithmetic, pair_block(): weight = jnp.sum(inner, axis=0) * (inverse * inverse * inverse)  62.6 us
    all_gather x1, blocking collectives, on_device(): src_all = lax.all_gather(owned, 'row', axis=1, tiled=True)  37.6 us
    ppermute x8, starting transfers between devices, xor_psum(): value = value + lax.ppermute(value, axis, partner)  28.5 us
    ppermute x8, waiting for transfers between devices, xor_psum(): value = value + lax.ppermute(value, axis, partner)  22.4 us
    ppermute x7, starting transfers between devices, doubling_gather(): other = lax.ppermute(value, axis, partner)  20.8 us
    dot_general x1, matrix products, on_device(): jnp.dot(split_three(table[:pos_rows + str_rows]), onehot, preferred_eleme...  14.5 us
    dot_general x1, matrix products, on_device(): lax.dot_general(split_three(terms), onehot, (((1,), (1,)), ((), ())), pre...  14 us
    ppermute x2, waiting for transfers between devices, near_far_reduce(): value = value + lax.ppermute(value, axis, partner)  13.6 us
  transfers between devices with their start and end apart: 20, of which 17 were waited for; matrix products, arithmetic and copies ran while one was open for 1% of the time, Pallas kernels for 0%

profile of v9, /device:TPU:6, one launch (start us, length us, event | category | flops | bytes accessed | tf_op | source)
XLA Modules:
  0.0 287.2 jit_solution(2931341528295114212)
XLA Ops:
  3.1 37.6 %all_gather.3 = f32[67,1024]{0,1:T(8,128)S(1)} all-gather(f32[67,32]{0,1:T(8,128)S(1)} %pad_maximum_fusion.6), channel_id=1, replica_groups=mesh['row'=32,'col'=16] {'row'}, dimensions={1}, use_global_device_ids=true | all-gather | bytes 283008 | tf_op jit(solution)/shard_map/all_gather | solution.py:213
  45.5 14.5 %fusion.28 = f32[105,16384]{1,0:T(8,128)S(1)} fusion(s32[16384]{0:T(1024)S(1)} %fusion.69, bf16[35,1024]{1,0:T(8,128)(2,1)S(1)} %get-tuple-element.165, bf16[35,1024]{1,0:T(8,128)(2,1)S(1)} %get-tuple-element.166, bf16[35,1024]{1,0:T(8,128)(2,1)S(1)} %get-tuple-element.164), kind=kOutput, calls=%fused_computation.49 | convolution fusion | flops 3540637696 | bytes 7161856 | tf_op jit(solution)/shard_map/dot_general | solution.py:234
  63.0 3.1 %subtract_multiply_fusion.3 = (f32[16,16384]{1,0:T(8,128)}, f32[16,16384]{1,0:T(8,128)}) fusion(f32[35,16384]{1,0:T(8,128)S(1)} %slice_add_fusion, f32[16384]{0:T(1024)S(1)} %get-tuple-element.170, f32[16384]{0:T(1024)S(1)} %get-tuple-element.169, f32[16]{0:T(128)S(1)} %copy-done.6), kind=kLoop, calls=%fused_computation.103 | loop fusion | flops 12058624 | bytes 4325440 | tf_op jit(solution)/shard_map/mul | solution.py:246
  68.1 3.4 %reshape.181 = f32[16,256,64]{2,1,0:T(8,128)} reshape(f32[16,16384]{1,0:T(8,128)} %get-tuple-element.124) | data formatting | bytes 2097152 | tf_op jit(solution)/shard_map/reshape | solution.py:251
  74.4 3.5 %collective-permute-start = (f32[32,256]{1,0:T(8,128)S(1)}, f32[32,256]{1,0:T(8,128)S(1)}, u32[]{:S(2)}, u32[]{:S(2)}) collective-permute-start(f32[32,256]{1,0:T(8,128)S(1)} %pad_maximum_fusion.5), channel_id=1, source_target_pairs={{0,1},{1,0},{2,3},{3,2},{4,5},{5,4},{6,7},{7,6},{8,9},{9,8},{10,11... | collective-permute-start | bytes 98312 | tf_op jit(solution)/shard_map/ppermute | solution.py:113
  80.2 5.1 %collective-permute-start.1 = (f32[32,256]{1,0:T(8,128)S(1)}, f32[32,256]{1,0:T(8,128)S(1)}, u32[]{:S(2)}, u32[]{:S(2)}) collective-permute-start(f32[32,256]{1,0:T(8,128)S(1)} %fusion.85), channel_id=1, source_target_pairs={{0,2},{1,3},{2,0},{3,1},{4,6},{5,7},{6,4},{7,5},{8,10},{9,11},{10,... | collective-permute-start | bytes 98312 | tf_op jit(solution)/shard_map/ppermute | solution.py:113
  87.5 2.7 collective-permute-start.2
  90.2 3.1 %collective-permute-done.2 = f32[32,256]{1,0:T(8,128)S(1)} collective-permute-done((f32[32,256]{1,0:T(8,128)S(1)}, f32[32,256]{1,0:T(8,128)S(1)}, u32[]{:S(2)}, u32[]{:S(2)}) %collective-permute-start.2) | collective-permute-done | bytes 32800 | tf_op jit(solution)/shard_map/ppermute | solution.py:113
  93.3 3.5 %collective-permute-start.3 = (f32[32,256]{1,0:T(8,128)S(1)}, f32[32,256]{1,0:T(8,128)S(1)}, u32[]{:S(2)}, u32[]{:S(2)}) collective-permute-start(f32[32,256]{1,0:T(8,128)S(1)} %add.283), channel_id=1, source_target_pairs={{0,8},{1,9},{2,10},{3,11},{4,12},{5,13},{6,14},{7,15},{8,0},{9,1},... | collective-permute-start | bytes 98312 | tf_op jit(solution)/shard_map/ppermute | solution.py:113
  96.8 4.0 %collective-permute-done.3 = f32[32,256]{1,0:T(8,128)S(1)} collective-permute-done((f32[32,256]{1,0:T(8,128)S(1)}, f32[32,256]{1,0:T(8,128)S(1)}, u32[]{:S(2)}, u32[]{:S(2)}) %collective-permute-start.3) | collective-permute-done | bytes 32800 | tf_op jit(solution)/shard_map/ppermute | solution.py:113
  104.9 2.9 %add_multiply_fusion = (f32[16,16384]{1,0:T(8,128)S(1)}, f32[16,16384]{1,0:T(8,128)S(1)}) fusion(f32[16,16384]{1,0:T(8,128)} %reshape.183, f32[16,16384]{1,0:T(8,128)S(1)} %reshape.182, f32[16384]{0:T(1024)} %copy-done, f32[16384]{0:T(1024)S(1)} %get-tuple-element.169, f32[16]{0:T(128)S(1)} %copy-done.6), kind=kLoop, calls=%fused_computation.101 | loop fusion | flops 12058624 | bytes 4325440 | tf_op jit(solution)/shard_map/mul | solution.py:259
  108.3 14.0 %fusion.27 = f32[96,1024]{1,0:T(8,128)S(1)} fusion(s32[16384]{0:T(1024)S(1)} %copy-done.4, bf16[32,16384]{1,0:T(8,128)(2,1)S(1)} %get-tuple-element.129, bf16[32,16384]{1,0:T(8,128)(2,1)S(1)} %get-tuple-element.128, bf16[32,16384]{1,0:T(8,128)(2,1)S(1)} %get-tuple-element.127), kind=kOutput, calls=%fused_computation.48 | convolution fusion | flops 3247439872 | bytes 3604480 | tf_op jit(solution)/shard_map/dot_general | solution.py:263
  128.8 3.9 %collective-permute-done.5 = f32[33,256]{1,0:T(8,128)S(1)} collective-permute-done((f32[33,256]{1,0:T(8,128)S(1)}, f32[33,256]{1,0:T(8,128)S(1)}, u32[]{:S(2)}, u32[]{:S(2)}) %collective-permute-start.5) | collective-permute-done | bytes 33824 | tf_op jit(solution)/shard_map/ppermute | solution.py:152
  135.0 4.4 %collective-permute-done.6 = f32[33,128]{1,0:T(8,128)S(1)} collective-permute-done((f32[33,128]{1,0:T(8,128)S(1)}, f32[33,128]{1,0:T(8,128)S(1)}, u32[]{:S(2)}, u32[]{:S(2)}) %collective-permute-start.6) | collective-permute-done | bytes 16928 | tf_op jit(solution)/shard_map/ppermute | solution.py:152
  139.4 3.1 %collective-permute-start.7 = (f32[33,128]{1,0:T(8,128)S(1)}, f32[33,128]{1,0:T(8,128)S(1)}, u32[]{:S(2)}, u32[]{:S(2)}) collective-permute-start(f32[33,128]{1,0:T(8,128)S(1)} %select_add_fusion.3), channel_id=1, source_target_pairs={{0,128},{16,144},{32,160},{48,176},{64,192},{80,208},{96,224},{112... | collective-permute-start | bytes 50696 | tf_op jit(solution)/shard_map/ppermute | solution.py:157
  142.4 6.5 %collective-permute-done.7 = f32[33,128]{1,0:T(8,128)S(1)} collective-permute-done((f32[33,128]{1,0:T(8,128)S(1)}, f32[33,128]{1,0:T(8,128)S(1)}, u32[]{:S(2)}, u32[]{:S(2)}) %collective-permute-start.7) | collective-permute-done | bytes 16928 | tf_op jit(solution)/shard_map/ppermute | solution.py:157
  148.9 7.3 %collective-permute-start.8 = (f32[33,128]{1,0:T(8,128)S(1)}, f32[33,128]{1,0:T(8,128)S(1)}, u32[]{:S(2)}, u32[]{:S(2)}) collective-permute-start(f32[33,128]{1,0:T(8,128)S(1)} %add.291), channel_id=1, source_target_pairs={{0,256},{16,272},{32,288},{48,304},{64,320},{80,336},{96,352},{112... | collective-permute-start | bytes 50696 | tf_op jit(solution)/shard_map/ppermute | solution.py:157
  156.3 7.1 %collective-permute-done.8 = f32[33,128]{1,0:T(8,128)S(1)} collective-permute-done((f32[33,128]{1,0:T(8,128)S(1)}, f32[33,128]{1,0:T(8,128)S(1)}, u32[]{:S(2)}, u32[]{:S(2)}) %collective-permute-start.8) | collective-permute-done | bytes 16928 | tf_op jit(solution)/shard_map/ppermute | solution.py:157
  164.6 3.5 %collective-permute-start.9 = (f32[67,32]{1,0:T(8,128)S(1)}, f32[67,32]{1,0:T(8,128)S(1)}, u32[]{:S(2)}, u32[]{:S(2)}) collective-permute-start(f32[67,32]{1,0:T(8,128)S(1)} %pad_maximum_fusion.4), channel_id=1, source_target_pairs={{0,1},{1,0},{2,3},{3,2},{4,5},{5,4},{6,7},{7,6},{8,9},{9,8},{10,11... | collective-permute-start | bytes 25736 | tf_op jit(solution)/shard_map/ppermute | solution.py:169
  171.2 4.8 %collective-permute-start.10 = (f32[67,64]{1,0:T(8,128)S(1)}, f32[67,64]{1,0:T(8,128)S(1)}, u32[]{:S(2)}, u32[]{:S(2)}) collective-permute-start(f32[67,64]{1,0:T(8,128)S(1)} %maximum_select_fusion.4), channel_id=1, source_target_pairs={{0,2},{1,3},{2,0},{3,1},{4,6},{5,7},{6,4},{7,5},{8,10},{9,11},{10,... | collective-permute-start | bytes 51464 | tf_op jit(solution)/shard_map/ppermute | solution.py:169
  178.7 2.7 collective-permute-start.11
  184.5 3.5 %collective-permute-start.12 = (f32[67,256]{1,0:T(8,128)S(1)}, f32[67,256]{1,0:T(8,128)S(1)}, u32[]{:S(2)}, u32[]{:S(2)}) collective-permute-start(f32[67,256]{1,0:T(8,128)S(1)} %maximum_select_fusion.2), channel_id=1, source_target_pairs={{0,8},{1,9},{2,10},{3,11},{4,12},{5,13},{6,14},{7,15},{8,0},{9,1},... | collective-permute-start | bytes 205832 | tf_op jit(solution)/shard_map/ppermute | solution.py:169
  188.1 4.1 %collective-permute-done.12 = f32[67,256]{1,0:T(8,128)S(1)} collective-permute-done((f32[67,256]{1,0:T(8,128)S(1)}, f32[67,256]{1,0:T(8,128)S(1)}, u32[]{:S(2)}, u32[]{:S(2)}) %collective-permute-start.12) | collective-permute-done | bytes 68640 | tf_op jit(solution)/shard_map/ppermute | solution.py:169
  192.3 67.6 %while.11 = (s32[]{:T(128)}, f32[3,512]{1,0:T(4,128)S(1)}, f32[16]{0:T(128)S(1)}, f32[3,512]{1,0:T(4,128)S(1)}, s32[2]{0:T(128)S(1)}, /*index=5*/f32[3,1024]{1,0...) while((s32[]{:T(128)}, f32[3,512]{1,0:T(4,128)S(1)}, ...), condition=%wide.region_8.9_spmd.clone, body=%wide.region_4.8_spmd.clone.sunk | while | flops 240649728 | bytes 10285353 | solution.py:87
  194.2 31.3 %fusion.100 = f32[512,512]{1,0:T(8,128)S(1)} fusion(f32[16,512]{1,0:T(8,128)S(1)} %get-tuple-element.247, f32[16,512]{1,0:T(8,128)S(1)} %get-tuple-element.248, f32[16,512]{1,0:T(8,128)S(1)} %get-tuple-element.249, f32[16,512]{1,0:T(8,128)S(1)} %get-tuple-element.250, f32[16,512]{1,0:T(8,128)S(1)} %get-tuple-element.251, ...), kind=kLoop, calls=%fused_computation.35.clone.1 | loop fusion | flops 234618880 | bytes 2359360 | tf_op jit(solution)/shard_map/while/body/eval_jaxpr/reduce_sum | solution.py:67
  228.0 31.3 %fusion.100 = f32[512,512]{1,0:T(8,128)S(1)} fusion(f32[16,512]{1,0:T(8,128)S(1)} %get-tuple-element.247, f32[16,512]{1,0:T(8,128)S(1)} %get-tuple-element.248, f32[16,512]{1,0:T(8,128)S(1)} %get-tuple-element.249, f32[16,512]{1,0:T(8,128)S(1)} %get-tuple-element.250, f32[16,512]{1,0:T(8,128)S(1)} %get-tuple-element.251, ...), kind=kLoop, calls=%fused_computation.35.clone.1 | loop fusion | flops 234618880 | bytes 2359360 | tf_op jit(solution)/shard_map/while/body/eval_jaxpr/reduce_sum | solution.py:67
  260.3 2.9 collective-permute-start.16
  265.8 4.8 %collective-permute-start.17 = (f32[12,128]{1,0:T(8,128)S(1)}, f32[12,128]{1,0:T(8,128)S(1)}, u32[]{:S(2)}, u32[]{:S(2)}) collective-permute-start(f32[12,128]{1,0:T(8,128)S(1)} %add.305), channel_id=1, source_target_pairs={{0,2},{1,3},{2,0},{3,1},{4,6},{5,7},{6,4},{7,5},{8,10},{9,11},{10,... | collective-permute-start | bytes 18440 | tf_op jit(solution)/shard_map/ppermute | solution.py:113
  272.9 2.7 collective-permute-start.18
  275.6 2.8 collective-permute-done.18
  278.4 3.3 %collective-permute-start.19 = (f32[12,128]{1,0:T(8,128)S(1)}, f32[12,128]{1,0:T(8,128)S(1)}, u32[]{:S(2)}, u32[]{:S(2)}) collective-permute-start(f32[12,128]{1,0:T(8,128)S(1)} %add.307), channel_id=1, source_target_pairs={{0,8},{1,9},{2,10},{3,11},{4,12},{5,13},{6,14},{7,15},{8,0},{9,1},... | collective-permute-start | bytes 18440 | tf_op jit(solution)/shard_map/ppermute | solution.py:113
  282.3 3.1 %collective-permute-done.19 = f32[12,128]{1,0:T(8,128)S(1)} collective-permute-done((f32[12,128]{1,0:T(8,128)S(1)}, f32[12,128]{1,0:T(8,128)S(1)}, u32[]{:S(2)}, u32[]{:S(2)}) %collective-permute-start.19) | collective-permute-done | bytes 6176 | tf_op jit(solution)/shard_map/ppermute | solution.py:113
  (159 shorter events, 52.0 us)
Async XLA Ops:
  45.5 14.5 %copy-start.3 = (s32[16384]{0:T(1024)}, s32[16384]{0:T(1024)S(1)}, u32[]{:S(2)}) copy-start(s32[16384]{0:T(1024)S(1)} %fusion.69) | copy-start | bytes 196612
  60.0 0.7 copy-start.9
  60.0 3.0 %copy-start.6 = (f32[16]{0:T(128)S(1)}, f32[16]{0:T(128)}, u32[]{:S(2)}) copy-start(f32[16]{0:T(128)} %param.13) | copy-start | bytes 196
  63.0 11.4 %copy-start = (f32[16384]{0:T(1024)}, f32[16384]{0:T(1024)S(1)}, u32[]{:S(2)}) copy-start(f32[16384]{0:T(1024)S(1)} %get-tuple-element.170) | copy-start | bytes 196612
  63.0 37.8 %copy-start.5 = (f32[32,256]{1,0:T(8,128)S(1)}, f32[32,256]{1,0:T(8,128)}, u32[]{:S(2)}) copy-start(f32[32,256]{1,0:T(8,128)} %param.15) | copy-start | bytes 98308
  74.4 5.8 %collective-permute-start = (f32[32,256]{1,0:T(8,128)S(1)}, f32[32,256]{1,0:T(8,128)S(1)}, u32[]{:S(2)}, u32[]{:S(2)}) collective-permute-start(f32[32,256]{1,0:T(8,128)S(1)} %pad_maximum_fusion.5), channel_id=1, source_target_pairs={{0,1},{1,0},{2,3},{3,2},{4,5},{5,4},{6,7},{7,6},{8,9},{9,8},{10,11... | collective-permute-start | bytes 98312 | tf_op jit(solution)/shard_map/ppermute | solution.py:113
  80.2 7.3 %collective-permute-start.1 = (f32[32,256]{1,0:T(8,128)S(1)}, f32[32,256]{1,0:T(8,128)S(1)}, u32[]{:S(2)}, u32[]{:S(2)}) collective-permute-start(f32[32,256]{1,0:T(8,128)S(1)} %fusion.85), channel_id=1, source_target_pairs={{0,2},{1,3},{2,0},{3,1},{4,6},{5,7},{6,4},{7,5},{8,10},{9,11},{10,... | collective-permute-start | bytes 98312 | tf_op jit(solution)/shard_map/ppermute | solution.py:113
  87.5 5.8 %collective-permute-start.2 = (f32[32,256]{1,0:T(8,128)S(1)}, f32[32,256]{1,0:T(8,128)S(1)}, u32[]{:S(2)}, u32[]{:S(2)}) collective-permute-start(f32[32,256]{1,0:T(8,128)S(1)} %add.282), channel_id=1, source_target_pairs={{0,4},{1,5},{2,6},{3,7},{4,0},{5,1},{6,2},{7,3},{8,12},{9,13},{10,... | collective-permute-start | bytes 98312 | tf_op jit(solution)/shard_map/ppermute | solution.py:113
  93.3 7.5 %collective-permute-start.3 = (f32[32,256]{1,0:T(8,128)S(1)}, f32[32,256]{1,0:T(8,128)S(1)}, u32[]{:S(2)}, u32[]{:S(2)}) collective-permute-start(f32[32,256]{1,0:T(8,128)S(1)} %add.283), channel_id=1, source_target_pairs={{0,8},{1,9},{2,10},{3,11},{4,12},{5,13},{6,14},{7,15},{8,0},{9,1},... | collective-permute-start | bytes 98312 | tf_op jit(solution)/shard_map/ppermute | solution.py:113
  104.9 3.4 %copy-start.4 = (s32[16384]{0:T(1024)S(1)}, s32[16384]{0:T(1024)}, u32[]{:S(2)}) copy-start(s32[16384]{0:T(1024)} %copy-done.3) | copy-start | bytes 196612
  108.3 47.9 %copy-start.8 = (s32[4,512]{1,0:T(4,128)S(1)}, s32[4,512]{1,0:T(4,128)}, u32[]{:S(2)}) copy-start(s32[4,512]{1,0:T(4,128)} %param.17) | copy-start | bytes 24580
  108.3 56.3 %copy-start.2 = (f32[32,32]{1,0:T(8,128)S(1)}, f32[32,32]{1,0:T(8,128)}, u32[]{:S(2)}) copy-start(f32[32,32]{1,0:T(8,128)} %param.12) | copy-start | bytes 12292
  108.3 56.3 %copy-start.1 = (f32[32,32]{1,0:T(8,128)S(1)}, f32[32,32]{1,0:T(8,128)}, u32[]{:S(2)}) copy-start(f32[32,32]{1,0:T(8,128)} %param.11) | copy-start | bytes 12292
  108.3 56.3 %copy-start.7 = (f32[3,32]{1,0:T(4,128)S(1)}, f32[3,32]{1,0:T(4,128)}, u32[]{:S(2)}) copy-start(f32[3,32]{1,0:T(4,128)} %param.10) | copy-start | bytes 1156
  123.0 3.2 %collective-permute-start.4 = (f32[33,512]{1,0:T(8,128)S(1)}, f32[33,512]{1,0:T(8,128)S(1)}, u32[]{:S(2)}, u32[]{:S(2)}) collective-permute-start(f32[33,512]{1,0:T(8,128)S(1)} %broadcast_select_fusion), channel_id=1, source_target_pairs={{0,16},{16,0},{32,48},{48,32},{64,80},{80,64},{96,112},{112,96},{1... | collective-permute-start | bytes 202760 | tf_op jit(solution)/shard_map/ppermute | solution.py:152
  126.9 5.9 %collective-permute-start.5 = (f32[33,256]{1,0:T(8,128)S(1)}, f32[33,256]{1,0:T(8,128)S(1)}, u32[]{:S(2)}, u32[]{:S(2)}) collective-permute-start(f32[33,256]{1,0:T(8,128)S(1)} %slice_select_fusion), channel_id=1, source_target_pairs={{0,32},{16,48},{32,0},{48,16},{64,96},{80,112},{96,64},{112,80},{1... | collective-permute-start | bytes 101384 | tf_op jit(solution)/shard_map/ppermute | solution.py:152
  132.8 6.6 %collective-permute-start.6 = (f32[33,128]{1,0:T(8,128)S(1)}, f32[33,128]{1,0:T(8,128)S(1)}, u32[]{:S(2)}, u32[]{:S(2)}) collective-permute-start(f32[33,128]{1,0:T(8,128)S(1)} %slice_select_fusion.1), channel_id=1, source_target_pairs={{0,64},{16,80},{32,96},{48,112},{64,0},{80,16},{96,32},{112,48},{1... | collective-permute-start | bytes 50696 | tf_op jit(solution)/shard_map/ppermute | solution.py:152
  139.4 9.6 %collective-permute-start.7 = (f32[33,128]{1,0:T(8,128)S(1)}, f32[33,128]{1,0:T(8,128)S(1)}, u32[]{:S(2)}, u32[]{:S(2)}) collective-permute-start(f32[33,128]{1,0:T(8,128)S(1)} %select_add_fusion.3), channel_id=1, source_target_pairs={{0,128},{16,144},{32,160},{48,176},{64,192},{80,208},{96,224},{112... | collective-permute-start | bytes 50696 | tf_op jit(solution)/shard_map/ppermute | solution.py:157
  148.9 14.4 %collective-permute-start.8 = (f32[33,128]{1,0:T(8,128)S(1)}, f32[33,128]{1,0:T(8,128)S(1)}, u32[]{:S(2)}, u32[]{:S(2)}) collective-permute-start(f32[33,128]{1,0:T(8,128)S(1)} %add.291), channel_id=1, source_target_pairs={{0,256},{16,272},{32,288},{48,304},{64,320},{80,336},{96,352},{112... | collective-permute-start | bytes 50696 | tf_op jit(solution)/shard_map/ppermute | solution.py:157
  164.6 6.5 %collective-permute-start.9 = (f32[67,32]{1,0:T(8,128)S(1)}, f32[67,32]{1,0:T(8,128)S(1)}, u32[]{:S(2)}, u32[]{:S(2)}) collective-permute-start(f32[67,32]{1,0:T(8,128)S(1)} %pad_maximum_fusion.4), channel_id=1, source_target_pairs={{0,1},{1,0},{2,3},{3,2},{4,5},{5,4},{6,7},{7,6},{8,9},{9,8},{10,11... | collective-permute-start | bytes 25736 | tf_op jit(solution)/shard_map/ppermute | solution.py:169
  168.9 7.1 %collective-permute-start.13 = (f32[33,128]{1,0:T(8,128)S(1)}, f32[33,128]{1,0:T(8,128)S(1)}, u32[]{:S(2)}, u32[]{:S(2)}) collective-permute-start(f32[33,128]{1,0:T(8,128)S(1)} %add.292), channel_id=1, source_target_pairs={{0,64},{16,80},{32,96},{48,112},{64,0},{80,16},{96,32},{112,48},{1... | collective-permute-start | bytes 50696 | tf_op jit(solution)/shard_map/ppermute | solution.py:169
  171.2 7.4 %collective-permute-start.10 = (f32[67,64]{1,0:T(8,128)S(1)}, f32[67,64]{1,0:T(8,128)S(1)}, u32[]{:S(2)}, u32[]{:S(2)}) collective-permute-start(f32[67,64]{1,0:T(8,128)S(1)} %maximum_select_fusion.4), channel_id=1, source_target_pairs={{0,2},{1,3},{2,0},{3,1},{4,6},{5,7},{6,4},{7,5},{8,10},{9,11},{10,... | collective-permute-start | bytes 51464 | tf_op jit(solution)/shard_map/ppermute | solution.py:169
  176.0 5.9 %collective-permute-start.14 = (f32[33,256]{1,0:T(8,128)S(1)}, f32[33,256]{1,0:T(8,128)S(1)}, u32[]{:S(2)}, u32[]{:S(2)}) collective-permute-start(f32[33,256]{1,0:T(8,128)S(1)} %maximum_select_fusion.3), channel_id=1, source_target_pairs={{0,32},{16,48},{32,0},{48,16},{64,96},{80,112},{96,64},{112,80},{1... | collective-permute-start | bytes 101384 | tf_op jit(solution)/shard_map/ppermute | solution.py:169
  178.7 5.9 %collective-permute-start.11 = (f32[67,128]{1,0:T(8,128)S(1)}, f32[67,128]{1,0:T(8,128)S(1)}, u32[]{:S(2)}, u32[]{:S(2)}) collective-permute-start(f32[67,128]{1,0:T(8,128)S(1)} %maximum_select_fusion.5), channel_id=1, source_target_pairs={{0,4},{1,5},{2,6},{3,7},{4,0},{5,1},{6,2},{7,3},{8,12},{9,13},{10,... | collective-permute-start | bytes 102920 | tf_op jit(solution)/shard_map/ppermute | solution.py:169
  181.9 6.1 %collective-permute-start.15 = (f32[33,512]{1,0:T(8,128)S(1)}, f32[33,512]{1,0:T(8,128)S(1)}, u32[]{:S(2)}, u32[]{:S(2)}) collective-permute-start(f32[33,512]{1,0:T(8,128)S(1)} %maximum_select_fusion.1), channel_id=1, source_target_pairs={{0,16},{16,0},{32,48},{48,32},{64,80},{80,64},{96,112},{112,96},{1... | collective-permute-start | bytes 202760 | tf_op jit(solution)/shard_map/ppermute | solution.py:169
  184.5 7.8 %collective-permute-start.12 = (f32[67,256]{1,0:T(8,128)S(1)}, f32[67,256]{1,0:T(8,128)S(1)}, u32[]{:S(2)}, u32[]{:S(2)}) collective-permute-start(f32[67,256]{1,0:T(8,128)S(1)} %maximum_select_fusion.2), channel_id=1, source_target_pairs={{0,8},{1,9},{2,10},{3,11},{4,12},{5,13},{6,14},{7,15},{8,0},{9,1},... | collective-permute-start | bytes 205832 | tf_op jit(solution)/shard_map/ppermute | solution.py:169
  260.3 5.5 %collective-permute-start.16 = (f32[12,128]{1,0:T(8,128)S(1)}, f32[12,128]{1,0:T(8,128)S(1)}, u32[]{:S(2)}, u32[]{:S(2)}) collective-permute-start(f32[12,128]{1,0:T(8,128)S(1)} %reshape.184), channel_id=1, source_target_pairs={{0,1},{1,0},{2,3},{3,2},{4,5},{5,4},{6,7},{7,6},{8,9},{9,8},{10,11... | collective-permute-start | bytes 18440 | tf_op jit(solution)/shard_map/ppermute | solution.py:113
  265.8 7.0 %collective-permute-start.17 = (f32[12,128]{1,0:T(8,128)S(1)}, f32[12,128]{1,0:T(8,128)S(1)}, u32[]{:S(2)}, u32[]{:S(2)}) collective-permute-start(f32[12,128]{1,0:T(8,128)S(1)} %add.305), channel_id=1, source_target_pairs={{0,2},{1,3},{2,0},{3,1},{4,6},{5,7},{6,4},{7,5},{8,10},{9,11},{10,... | collective-permute-start | bytes 18440 | tf_op jit(solution)/shard_map/ppermute | solution.py:113
  272.9 5.5 %collective-permute-start.18 = (f32[12,128]{1,0:T(8,128)S(1)}, f32[12,128]{1,0:T(8,128)S(1)}, u32[]{:S(2)}, u32[]{:S(2)}) collective-permute-start(f32[12,128]{1,0:T(8,128)S(1)} %add.306), channel_id=1, source_target_pairs={{0,4},{1,5},{2,6},{3,7},{4,0},{5,1},{6,2},{7,3},{8,12},{9,13},{10,... | collective-permute-start | bytes 18440 | tf_op jit(solution)/shard_map/ppermute | solution.py:113
  278.4 7.0 %collective-permute-start.19 = (f32[12,128]{1,0:T(8,128)S(1)}, f32[12,128]{1,0:T(8,128)S(1)}, u32[]{:S(2)}, u32[]{:S(2)}) collective-permute-start(f32[12,128]{1,0:T(8,128)S(1)} %add.307), channel_id=1, source_target_pairs={{0,8},{1,9},{2,10},{3,11},{4,12},{5,13},{6,14},{7,15},{8,0},{9,1},... | collective-permute-start | bytes 18440 | tf_op jit(solution)/shard_map/ppermute | solution.py:113

commit v10 on v9

--- a/solution.py
+++ b/solution.py
@@ -195,6 +195,29 @@
 def join_three(value):
     rows = value.shape[0] // 3
     return (value[:rows] + value[rows : 2 * rows]) + value[2 * rows :]
+
+
+def group_psum(value, axis):
+    count = lax.axis_size(axis)
+    stride = 1
+    while stride * 4 <= count:
+        stride *= 4
+    if stride != count:
+        return xor_psum(value, axis)
+    me = lax.axis_index(axis)
+    stride = 1
+    while stride < count:
+        digit = (me // stride) % 4
+        value = row_major(value)
+        received = [value]
+        for mate in (1, 2, 3):
+            partner = [(index, index ^ (mate * stride)) for index in range(count)]
+            received.append(lax.ppermute(value, axis, partner))
+        stacked = jnp.stack(received)
+        ordered = [stacked[member ^ digit] for member in range(4)]
+        value = (ordered[0] + ordered[1]) + (ordered[2] + ordered[3])
+        stride *= 4
+    return value
 
 
 def on_device(centroids, strengths, self_inv, wavenumbers, field_pos, targets, lists, connect):
@@ -252,7 +275,7 @@
         ],
         axis=0,
     )
-    eta = xor_psum(eta_part, "col")
+    eta = group_psum(eta_part, "col")
     resid = eta - targets
     rep_real = jnp.repeat(resid[:freqs], listed, axis=1)
     rep_imag = jnp.repeat(resid[freqs:], listed, axis=1)
@@ -306,7 +329,7 @@
     )
     lanes = 128 if block_width % 128 == 0 else block_width
     vertex_rows = vertex_part.reshape(3 * block_width // lanes, lanes)
-    vertex_sum = xor_psum(vertex_rows, "col").reshape(3, block_width)
+    vertex_sum = group_psum(vertex_rows, "col").reshape(3, block_width)
     vertex_own = lax.dynamic_slice_in_dim(vertex_sum, col_index * owned_count, owned_count, 1)
     adjoint = mu_own
     return (adjoint, vertex_own, objective)

time: 288 us -> 292 us (1.014)
  starting transfers between devices: 65.6 us -> 75.2 us
  waiting for transfers between devices: 51.2 us -> 44.7 us
    ppermute x8 -> x12, starting transfers between devices: 28.5 us -> 41.9 us  [group_psum(): received.append(lax.ppermute(value, axis, partner))]
    ppermute x8 -> x12, waiting for transfers between devices: 22.4 us -> 12.7 us  [group_psum(): received.append(lax.ppermute(value, axis, partner))]
    ppermute x7, starting transfers between devices: 20.8 us -> 17 us  [doubling_gather(): other = lax.ppermute(value, axis, partner)]
    ppermute x7, waiting for transfers between devices: 5.66 us -> 8.87 us  [doubling_gather(): other = lax.ppermute(value, axis, partner)]
  transfers between devices with their start and end apart: 20 -> 24, of which waited for: 17 -> 15; matrix products, arithmetic and copies ran while one was open for 1% -> 1% of each run, Pallas kernels for 0% -> 0%
where the time goes in v10:
time: 292 us; the launch traced here: 291 us
  other arithmetic  79.9 us (27%)
  starting transfers between devices  75.2 us (26%)
  waiting for transfers between devices  44.7 us (15%)
  blocking collectives  37.6 us (13%)
  matrix products  28.7 us (10%)
  local copies, waits for them, and re-layouts  19.5 us (7%)
  between operations  3.58 us (1%)
    reduce_sum x2, other arithmetic, pair_block(): weight = jnp.sum(inner, axis=0) * (inverse * inverse * inverse)  62.6 us
    ppermute x12, starting transfers between devices, group_psum(): received.append(lax.ppermute(value, axis, partner))  41.9 us
    all_gather x1, blocking collectives, on_device(): src_all = lax.all_gather(owned, 'row', axis=1, tiled=True)  37.6 us
    ppermute x7, starting transfers between devices, doubling_gather(): other = lax.ppermute(value, axis, partner)  17 us
    dot_general x1, matrix products, on_device(): jnp.dot(split_three(table[:pos_rows + str_rows]), onehot, preferred_eleme...  14.5 us
    dot_general x1, matrix products, on_device(): lax.dot_general(split_three(terms), onehot, (((1,), (1,)), ((), ())), pre...  14 us
    ppermute x2, waiting for transfers between devices, near_far_reduce(): value = value + lax.ppermute(value, axis, partner)  13.6 us
    ppermute x12, waiting for transfers between devices, group_psum(): received.append(lax.ppermute(value, axis, partner))  12.7 us
  transfers between devices with their start and end apart: 24, of which 15 were waited for; matrix products, arithmetic and copies ran while one was open for 1% of the time, Pallas kernels for 0%

profile of v10, /device:TPU:6, one launch (start us, length us, event | category | flops | bytes accessed | tf_op | source)
XLA Modules:
  0.0 290.7 jit_solution(9645862101505918868)
XLA Ops:
  3.1 37.6 %all_gather.3 = f32[67,1024]{0,1:T(8,128)S(1)} all-gather(f32[67,32]{0,1:T(8,128)S(1)} %pad_maximum_fusion.10), channel_id=1, replica_groups=mesh['row'=32,'col'=16] {'row'}, dimensions={1}, use_global_device_ids=true | all-gather | bytes 283008 | tf_op jit(solution)/shard_map/all_gather | solution.py:236
  45.5 14.5 %fusion.28 = f32[105,16384]{1,0:T(8,128)S(1)} fusion(s32[16384]{0:T(1024)S(1)} %fusion.69, bf16[35,1024]{1,0:T(8,128)(2,1)S(1)} %get-tuple-element.165, bf16[35,1024]{1,0:T(8,128)(2,1)S(1)} %get-tuple-element.166, bf16[35,1024]{1,0:T(8,128)(2,1)S(1)} %get-tuple-element.164), kind=kOutput, calls=%fused_computation.49 | convolution fusion | flops 3540637696 | bytes 7161856 | tf_op jit(solution)/shard_map/dot_general | solution.py:257
  63.0 3.1 %subtract_multiply_fusion.3 = (f32[16,16384]{1,0:T(8,128)}, f32[16,16384]{1,0:T(8,128)}) fusion(f32[35,16384]{1,0:T(8,128)S(1)} %slice_add_fusion, f32[16384]{0:T(1024)S(1)} %get-tuple-element.170, f32[16384]{0:T(1024)S(1)} %get-tuple-element.169, f32[16]{0:T(128)S(1)} %copy-done.6), kind=kLoop, calls=%fused_computation.103 | loop fusion | flops 12058624 | bytes 4325440 | tf_op jit(solution)/shard_map/mul | solution.py:269
  68.1 3.4 %reshape.195 = f32[16,256,64]{2,1,0:T(8,128)} reshape(f32[16,16384]{1,0:T(8,128)} %get-tuple-element.124) | data formatting | bytes 2097152 | tf_op jit(solution)/shard_map/reshape | solution.py:274
  74.4 3.5 %collective-permute-start = (f32[32,256]{1,0:T(8,128)S(1)}, f32[32,256]{1,0:T(8,128)S(1)}, u32[]{:S(2)}, u32[]{:S(2)}) collective-permute-start(f32[32,256]{1,0:T(8,128)S(1)} %get-tuple-element.176), channel_id=1, source_target_pairs={{0,1},{1,0},{2,3},{3,2},{4,5},{5,4},{6,7},{7,6},{8,9},{9,8},{10,11... | collective-permute-start | bytes 98312 | tf_op jit(solution)/shard_map/ppermute | solution.py:215
  77.9 4.8 %collective-permute-start.1 = (f32[32,256]{1,0:T(8,128)S(1)}, f32[32,256]{1,0:T(8,128)S(1)}, u32[]{:S(2)}, u32[]{:S(2)}) collective-permute-start(f32[32,256]{1,0:T(8,128)S(1)} %get-tuple-element.176), channel_id=1, source_target_pairs={{0,2},{1,3},{2,0},{3,1},{4,6},{5,7},{6,4},{7,5},{8,10},{9,11},{10,... | collective-permute-start | bytes 98312 | tf_op jit(solution)/shard_map/ppermute | solution.py:215
  82.7 2.3 collective-permute-start.2
  85.2 4.5 %collective-permute-done.2 = f32[32,256]{1,0:T(8,128)S(1)} collective-permute-done((f32[32,256]{1,0:T(8,128)S(1)}, f32[32,256]{1,0:T(8,128)S(1)}, u32[]{:S(2)}, u32[]{:S(2)}) %collective-permute-start.2) | collective-permute-done | bytes 32800 | tf_op jit(solution)/shard_map/ppermute | solution.py:215
  89.8 2.7 collective-permute-start.3
  92.5 3.0 %collective-permute-start.4 = (f32[32,256]{1,0:T(8,128)S(1)}, f32[32,256]{1,0:T(8,128)S(1)}, u32[]{:S(2)}, u32[]{:S(2)}) collective-permute-start(f32[32,256]{1,0:T(8,128)S(1)} %fusion.94), channel_id=1, source_target_pairs={{0,8},{1,9},{2,10},{3,11},{4,12},{5,13},{6,14},{7,15},{8,0},{9,1},... | collective-permute-start | bytes 98312 | tf_op jit(solution)/shard_map/ppermute | solution.py:215
  95.5 4.7 %collective-permute-start.5 = (f32[32,256]{1,0:T(8,128)S(1)}, f32[32,256]{1,0:T(8,128)S(1)}, u32[]{:S(2)}, u32[]{:S(2)}) collective-permute-start(f32[32,256]{1,0:T(8,128)S(1)} %fusion.94), channel_id=1, source_target_pairs={{0,12},{1,13},{2,14},{3,15},{4,8},{5,9},{6,10},{7,11},{8,4},{9,5},... | collective-permute-start | bytes 98312 | tf_op jit(solution)/shard_map/ppermute | solution.py:215
  100.2 2.3 collective-permute-done.5
  106.7 2.9 add_multiply_fusion
  110.1 14.0 %fusion.27 = f32[96,1024]{1,0:T(8,128)S(1)} fusion(s32[16384]{0:T(1024)S(1)} %copy-done.4, bf16[32,16384]{1,0:T(8,128)(2,1)S(1)} %get-tuple-element.129, bf16[32,16384]{1,0:T(8,128)(2,1)S(1)} %get-tuple-element.128, bf16[32,16384]{1,0:T(8,128)(2,1)S(1)} %get-tuple-element.127), kind=kOutput, calls=%fused_computation.48 | convolution fusion | flops 3247439872 | bytes 3604480 | tf_op jit(solution)/shard_map/dot_general | solution.py:286
  130.6 3.9 %collective-permute-done.7 = f32[33,256]{1,0:T(8,128)S(1)} collective-permute-done((f32[33,256]{1,0:T(8,128)S(1)}, f32[33,256]{1,0:T(8,128)S(1)}, u32[]{:S(2)}, u32[]{:S(2)}) %collective-permute-start.7) | collective-permute-done | bytes 33824 | tf_op jit(solution)/shard_map/ppermute | solution.py:152
  136.8 4.4 %collective-permute-done.8 = f32[33,128]{1,0:T(8,128)S(1)} collective-permute-done((f32[33,128]{1,0:T(8,128)S(1)}, f32[33,128]{1,0:T(8,128)S(1)}, u32[]{:S(2)}, u32[]{:S(2)}) %collective-permute-start.8) | collective-permute-done | bytes 16928 | tf_op jit(solution)/shard_map/ppermute | solution.py:152
  141.2 3.1 %collective-permute-start.9 = (f32[33,128]{1,0:T(8,128)S(1)}, f32[33,128]{1,0:T(8,128)S(1)}, u32[]{:S(2)}, u32[]{:S(2)}) collective-permute-start(f32[33,128]{1,0:T(8,128)S(1)} %select_add_fusion.3), channel_id=1, source_target_pairs={{0,128},{16,144},{32,160},{48,176},{64,192},{80,208},{96,224},{112... | collective-permute-start | bytes 50696 | tf_op jit(solution)/shard_map/ppermute | solution.py:157
  144.2 6.5 %collective-permute-done.9 = f32[33,128]{1,0:T(8,128)S(1)} collective-permute-done((f32[33,128]{1,0:T(8,128)S(1)}, f32[33,128]{1,0:T(8,128)S(1)}, u32[]{:S(2)}, u32[]{:S(2)}) %collective-permute-start.9) | collective-permute-done | bytes 16928 | tf_op jit(solution)/shard_map/ppermute | solution.py:157
  150.8 7.3 %collective-permute-start.10 = (f32[33,128]{1,0:T(8,128)S(1)}, f32[33,128]{1,0:T(8,128)S(1)}, u32[]{:S(2)}, u32[]{:S(2)}) collective-permute-start(f32[33,128]{1,0:T(8,128)S(1)} %add.380), channel_id=1, source_target_pairs={{0,256},{16,272},{32,288},{48,304},{64,320},{80,336},{96,352},{112... | collective-permute-start | bytes 50696 | tf_op jit(solution)/shard_map/ppermute | solution.py:157
  158.1 7.1 %collective-permute-done.10 = f32[33,128]{1,0:T(8,128)S(1)} collective-permute-done((f32[33,128]{1,0:T(8,128)S(1)}, f32[33,128]{1,0:T(8,128)S(1)}, u32[]{:S(2)}, u32[]{:S(2)}) %collective-permute-start.10) | collective-permute-done | bytes 16928 | tf_op jit(solution)/shard_map/ppermute | solution.py:157
  172.4 2.6 collective-permute-start.12
  185.7 4.4 %collective-permute-start.14 = (f32[67,256]{1,0:T(8,128)S(1)}, f32[67,256]{1,0:T(8,128)S(1)}, u32[]{:S(2)}, u32[]{:S(2)}) collective-permute-start(f32[67,256]{1,0:T(8,128)S(1)} %maximum_select_fusion.2), channel_id=1, source_target_pairs={{0,8},{1,9},{2,10},{3,11},{4,12},{5,13},{6,14},{7,15},{8,0},{9,1},... | collective-permute-start | bytes 205832 | tf_op jit(solution)/shard_map/ppermute | solution.py:169
  190.2 3.3 %collective-permute-done.14 = f32[67,256]{1,0:T(8,128)S(1)} collective-permute-done((f32[67,256]{1,0:T(8,128)S(1)}, f32[67,256]{1,0:T(8,128)S(1)}, u32[]{:S(2)}, u32[]{:S(2)}) %collective-permute-start.14) | collective-permute-done | bytes 68640 | tf_op jit(solution)/shard_map/ppermute | solution.py:169
  193.5 67.7 %while.11 = (s32[]{:T(128)}, f32[3,512]{1,0:T(4,128)S(1)}, f32[16]{0:T(128)S(1)}, f32[3,512]{1,0:T(4,128)S(1)}, s32[2]{0:T(128)S(1)}, /*index=5*/f32[3,1024]{1,0...) while((s32[]{:T(128)}, f32[3,512]{1,0:T(4,128)S(1)}, ...), condition=%wide.region_8.9_spmd.clone, body=%wide.region_4.8_spmd.clone.sunk | while | flops 240649728 | bytes 10285353 | solution.py:87
  195.4 31.3 %fusion.102 = f32[512,512]{1,0:T(8,128)S(1)} fusion(f32[16,512]{1,0:T(8,128)S(1)} %get-tuple-element.249, f32[16,512]{1,0:T(8,128)S(1)} %get-tuple-element.250, f32[16,512]{1,0:T(8,128)S(1)} %get-tuple-element.251, f32[16,512]{1,0:T(8,128)S(1)} %get-tuple-element.252, f32[16,512]{1,0:T(8,128)S(1)} %get-tuple-element.253, ...), kind=kLoop, calls=%fused_computation.35.clone.1 | loop fusion | flops 234618880 | bytes 2359360 | tf_op jit(solution)/shard_map/while/body/eval_jaxpr/reduce_sum | solution.py:67
  229.2 31.3 %fusion.102 = f32[512,512]{1,0:T(8,128)S(1)} fusion(f32[16,512]{1,0:T(8,128)S(1)} %get-tuple-element.249, f32[16,512]{1,0:T(8,128)S(1)} %get-tuple-element.250, f32[16,512]{1,0:T(8,128)S(1)} %get-tuple-element.251, f32[16,512]{1,0:T(8,128)S(1)} %get-tuple-element.252, f32[16,512]{1,0:T(8,128)S(1)} %get-tuple-element.253, ...), kind=kLoop, calls=%fused_computation.35.clone.1 | loop fusion | flops 234618880 | bytes 2359360 | tf_op jit(solution)/shard_map/while/body/eval_jaxpr/reduce_sum | solution.py:67
  261.5 3.0 %collective-permute-start.18 = (f32[12,128]{1,0:T(8,128)S(1)}, f32[12,128]{1,0:T(8,128)S(1)}, u32[]{:S(2)}, u32[]{:S(2)}) collective-permute-start(f32[12,128]{1,0:T(8,128)S(1)} %reshape.198), channel_id=1, source_target_pairs={{0,1},{1,0},{2,3},{3,2},{4,5},{5,4},{6,7},{7,6},{8,9},{9,8},{10,11... | collective-permute-start | bytes 18440 | tf_op jit(solution)/shard_map/ppermute | solution.py:215
  264.5 2.9 collective-permute-start.19
  267.3 4.6 %collective-permute-start.20 = (f32[12,128]{1,0:T(8,128)S(1)}, f32[12,128]{1,0:T(8,128)S(1)}, u32[]{:S(2)}, u32[]{:S(2)}) collective-permute-start(f32[12,128]{1,0:T(8,128)S(1)} %reshape.198), channel_id=1, source_target_pairs={{0,3},{1,2},{2,1},{3,0},{4,7},{5,6},{6,5},{7,4},{8,11},{9,10},{10,... | collective-permute-start | bytes 18440 | tf_op jit(solution)/shard_map/ppermute | solution.py:215
  276.4 5.8 %collective-permute-start.22 = (f32[12,128]{1,0:T(8,128)S(1)}, f32[12,128]{1,0:T(8,128)S(1)}, u32[]{:S(2)}, u32[]{:S(2)}) collective-permute-start(f32[12,128]{1,0:T(8,128)S(1)} %fusion.93), channel_id=1, source_target_pairs={{0,8},{1,9},{2,10},{3,11},{4,12},{5,13},{6,14},{7,15},{8,0},{9,1},... | collective-permute-start | bytes 18440 | tf_op jit(solution)/shard_map/ppermute | solution.py:215
  282.1 2.4 collective-permute-start.23
  284.6 4.3 %collective-permute-done.23 = f32[12,128]{1,0:T(8,128)S(1)} collective-permute-done((f32[12,128]{1,0:T(8,128)S(1)}, f32[12,128]{1,0:T(8,128)S(1)}, u32[]{:S(2)}, u32[]{:S(2)}) %collective-permute-start.23) | collective-permute-done | bytes 6176 | tf_op jit(solution)/shard_map/ppermute | solution.py:215
  (170 shorter events, 54.4 us)
Async XLA Ops:
  45.5 14.5 %copy-start.3 = (s32[16384]{0:T(1024)}, s32[16384]{0:T(1024)S(1)}, u32[]{:S(2)}) copy-start(s32[16384]{0:T(1024)S(1)} %fusion.69) | copy-start | bytes 196612
  62.9 11.4 %copy-start = (f32[16384]{0:T(1024)}, f32[16384]{0:T(1024)S(1)}, u32[]{:S(2)}) copy-start(f32[16384]{0:T(1024)S(1)} %get-tuple-element.170) | copy-start | bytes 196612
  63.0 39.6 %copy-start.5 = (f32[32,256]{1,0:T(8,128)S(1)}, f32[32,256]{1,0:T(8,128)}, u32[]{:S(2)}) copy-start(f32[32,256]{1,0:T(8,128)} %param.15) | copy-start | bytes 98308
  74.4 10.7 %collective-permute-start = (f32[32,256]{1,0:T(8,128)S(1)}, f32[32,256]{1,0:T(8,128)S(1)}, u32[]{:S(2)}, u32[]{:S(2)}) collective-permute-start(f32[32,256]{1,0:T(8,128)S(1)} %get-tuple-element.176), channel_id=1, source_target_pairs={{0,1},{1,0},{2,3},{3,2},{4,5},{5,4},{6,7},{7,6},{8,9},{9,8},{10,11... | collective-permute-start | bytes 98312 | tf_op jit(solution)/shard_map/ppermute | solution.py:215
  77.9 7.3 %collective-permute-start.1 = (f32[32,256]{1,0:T(8,128)S(1)}, f32[32,256]{1,0:T(8,128)S(1)}, u32[]{:S(2)}, u32[]{:S(2)}) collective-permute-start(f32[32,256]{1,0:T(8,128)S(1)} %get-tuple-element.176), channel_id=1, source_target_pairs={{0,2},{1,3},{2,0},{3,1},{4,6},{5,7},{6,4},{7,5},{8,10},{9,11},{10,... | collective-permute-start | bytes 98312 | tf_op jit(solution)/shard_map/ppermute | solution.py:215
  82.7 7.0 %collective-permute-start.2 = (f32[32,256]{1,0:T(8,128)S(1)}, f32[32,256]{1,0:T(8,128)S(1)}, u32[]{:S(2)}, u32[]{:S(2)}) collective-permute-start(f32[32,256]{1,0:T(8,128)S(1)} %get-tuple-element.176), channel_id=1, source_target_pairs={{0,3},{1,2},{2,1},{3,0},{4,7},{5,6},{6,5},{7,4},{8,11},{9,10},{10,... | collective-permute-start | bytes 98312 | tf_op jit(solution)/shard_map/ppermute | solution.py:215
  89.8 10.5 %collective-permute-start.3 = (f32[32,256]{1,0:T(8,128)S(1)}, f32[32,256]{1,0:T(8,128)S(1)}, u32[]{:S(2)}, u32[]{:S(2)}) collective-permute-start(f32[32,256]{1,0:T(8,128)S(1)} %fusion.94), channel_id=1, source_target_pairs={{0,4},{1,5},{2,6},{3,7},{4,0},{5,1},{6,2},{7,3},{8,12},{9,13},{10,... | collective-permute-start | bytes 98312 | tf_op jit(solution)/shard_map/ppermute | solution.py:215
  92.5 7.7 %collective-permute-start.4 = (f32[32,256]{1,0:T(8,128)S(1)}, f32[32,256]{1,0:T(8,128)S(1)}, u32[]{:S(2)}, u32[]{:S(2)}) collective-permute-start(f32[32,256]{1,0:T(8,128)S(1)} %fusion.94), channel_id=1, source_target_pairs={{0,8},{1,9},{2,10},{3,11},{4,12},{5,13},{6,14},{7,15},{8,0},{9,1},... | collective-permute-start | bytes 98312 | tf_op jit(solution)/shard_map/ppermute | solution.py:215
  95.5 7.0 %collective-permute-start.5 = (f32[32,256]{1,0:T(8,128)S(1)}, f32[32,256]{1,0:T(8,128)S(1)}, u32[]{:S(2)}, u32[]{:S(2)}) collective-permute-start(f32[32,256]{1,0:T(8,128)S(1)} %fusion.94), channel_id=1, source_target_pairs={{0,12},{1,13},{2,14},{3,15},{4,8},{5,9},{6,10},{7,11},{8,4},{9,5},... | collective-permute-start | bytes 98312 | tf_op jit(solution)/shard_map/ppermute | solution.py:215
  106.7 3.4 %copy-start.4 = (s32[16384]{0:T(1024)S(1)}, s32[16384]{0:T(1024)}, u32[]{:S(2)}) copy-start(s32[16384]{0:T(1024)} %copy-done.3) | copy-start | bytes 196612
  110.1 47.9 %copy-start.8 = (s32[4,512]{1,0:T(4,128)S(1)}, s32[4,512]{1,0:T(4,128)}, u32[]{:S(2)}) copy-start(s32[4,512]{1,0:T(4,128)} %param.17) | copy-start | bytes 24580
  110.1 56.3 %copy-start.2 = (f32[32,32]{1,0:T(8,128)S(1)}, f32[32,32]{1,0:T(8,128)}, u32[]{:S(2)}) copy-start(f32[32,32]{1,0:T(8,128)} %param.12) | copy-start | bytes 12292
  110.1 56.3 %copy-start.1 = (f32[32,32]{1,0:T(8,128)S(1)}, f32[32,32]{1,0:T(8,128)}, u32[]{:S(2)}) copy-start(f32[32,32]{1,0:T(8,128)} %param.11) | copy-start | bytes 12292
  110.1 56.3 %copy-start.7 = (f32[3,32]{1,0:T(4,128)S(1)}, f32[3,32]{1,0:T(4,128)}, u32[]{:S(2)}) copy-start(f32[3,32]{1,0:T(4,128)} %param.10) | copy-start | bytes 1156
  124.8 3.2 %collective-permute-start.6 = (f32[33,512]{1,0:T(8,128)S(1)}, f32[33,512]{1,0:T(8,128)S(1)}, u32[]{:S(2)}, u32[]{:S(2)}) collective-permute-start(f32[33,512]{1,0:T(8,128)S(1)} %broadcast_select_fusion), channel_id=1, source_target_pairs={{0,16},{16,0},{32,48},{48,32},{64,80},{80,64},{96,112},{112,96},{1... | collective-permute-start | bytes 202760 | tf_op jit(solution)/shard_map/ppermute | solution.py:152
  128.7 5.9 %collective-permute-start.7 = (f32[33,256]{1,0:T(8,128)S(1)}, f32[33,256]{1,0:T(8,128)S(1)}, u32[]{:S(2)}, u32[]{:S(2)}) collective-permute-start(f32[33,256]{1,0:T(8,128)S(1)} %slice_select_fusion), channel_id=1, source_target_pairs={{0,32},{16,48},{32,0},{48,16},{64,96},{80,112},{96,64},{112,80},{1... | collective-permute-start | bytes 101384 | tf_op jit(solution)/shard_map/ppermute | solution.py:152
  134.6 6.6 %collective-permute-start.8 = (f32[33,128]{1,0:T(8,128)S(1)}, f32[33,128]{1,0:T(8,128)S(1)}, u32[]{:S(2)}, u32[]{:S(2)}) collective-permute-start(f32[33,128]{1,0:T(8,128)S(1)} %slice_select_fusion.1), channel_id=1, source_target_pairs={{0,64},{16,80},{32,96},{48,112},{64,0},{80,16},{96,32},{112,48},{1... | collective-permute-start | bytes 50696 | tf_op jit(solution)/shard_map/ppermute | solution.py:152
  141.2 9.6 %collective-permute-start.9 = (f32[33,128]{1,0:T(8,128)S(1)}, f32[33,128]{1,0:T(8,128)S(1)}, u32[]{:S(2)}, u32[]{:S(2)}) collective-permute-start(f32[33,128]{1,0:T(8,128)S(1)} %select_add_fusion.3), channel_id=1, source_target_pairs={{0,128},{16,144},{32,160},{48,176},{64,192},{80,208},{96,224},{112... | collective-permute-start | bytes 50696 | tf_op jit(solution)/shard_map/ppermute | solution.py:157
  150.8 14.4 %collective-permute-start.10 = (f32[33,128]{1,0:T(8,128)S(1)}, f32[33,128]{1,0:T(8,128)S(1)}, u32[]{:S(2)}, u32[]{:S(2)}) collective-permute-start(f32[33,128]{1,0:T(8,128)S(1)} %add.380), channel_id=1, source_target_pairs={{0,256},{16,272},{32,288},{48,304},{64,320},{80,336},{96,352},{112... | collective-permute-start | bytes 50696 | tf_op jit(solution)/shard_map/ppermute | solution.py:157
  166.4 5.9 %collective-permute-start.11 = (f32[67,32]{1,0:T(8,128)S(1)}, f32[67,32]{1,0:T(8,128)S(1)}, u32[]{:S(2)}, u32[]{:S(2)}) collective-permute-start(f32[67,32]{1,0:T(8,128)S(1)} %pad_maximum_fusion.6), channel_id=1, source_target_pairs={{0,1},{1,0},{2,3},{3,2},{4,5},{5,4},{6,7},{7,6},{8,9},{9,8},{10,11... | collective-permute-start | bytes 25736 | tf_op jit(solution)/shard_map/ppermute | solution.py:169
  169.2 6.6 %collective-permute-start.15 = (f32[33,128]{1,0:T(8,128)S(1)}, f32[33,128]{1,0:T(8,128)S(1)}, u32[]{:S(2)}, u32[]{:S(2)}) collective-permute-start(f32[33,128]{1,0:T(8,128)S(1)} %add.381), channel_id=1, source_target_pairs={{0,64},{16,80},{32,96},{48,112},{64,0},{80,16},{96,32},{112,48},{1... | collective-permute-start | bytes 50696 | tf_op jit(solution)/shard_map/ppermute | solution.py:169
  172.4 7.4 %collective-permute-start.12 = (f32[67,64]{1,0:T(8,128)S(1)}, f32[67,64]{1,0:T(8,128)S(1)}, u32[]{:S(2)}, u32[]{:S(2)}) collective-permute-start(f32[67,64]{1,0:T(8,128)S(1)} %maximum_select_fusion.4), channel_id=1, source_target_pairs={{0,2},{1,3},{2,0},{3,1},{4,6},{5,7},{6,4},{7,5},{8,10},{9,11},{10,... | collective-permute-start | bytes 51464 | tf_op jit(solution)/shard_map/ppermute | solution.py:169
  175.8 6.0 %collective-permute-start.16 = (f32[33,256]{1,0:T(8,128)S(1)}, f32[33,256]{1,0:T(8,128)S(1)}, u32[]{:S(2)}, u32[]{:S(2)}) collective-permute-start(f32[33,256]{1,0:T(8,128)S(1)} %maximum_select_fusion.3), channel_id=1, source_target_pairs={{0,32},{16,48},{32,0},{48,16},{64,96},{80,112},{96,64},{112,80},{1... | collective-permute-start | bytes 101384 | tf_op jit(solution)/shard_map/ppermute | solution.py:169
  179.9 5.9 %collective-permute-start.13 = (f32[67,128]{1,0:T(8,128)S(1)}, f32[67,128]{1,0:T(8,128)S(1)}, u32[]{:S(2)}, u32[]{:S(2)}) collective-permute-start(f32[67,128]{1,0:T(8,128)S(1)} %maximum_select_fusion.5), channel_id=1, source_target_pairs={{0,4},{1,5},{2,6},{3,7},{4,0},{5,1},{6,2},{7,3},{8,12},{9,13},{10,... | collective-permute-start | bytes 102920 | tf_op jit(solution)/shard_map/ppermute | solution.py:169
  181.8 8.3 %collective-permute-start.17 = (f32[33,512]{1,0:T(8,128)S(1)}, f32[33,512]{1,0:T(8,128)S(1)}, u32[]{:S(2)}, u32[]{:S(2)}) collective-permute-start(f32[33,512]{1,0:T(8,128)S(1)} %maximum_select_fusion.1), channel_id=1, source_target_pairs={{0,16},{16,0},{32,48},{48,32},{64,80},{80,64},{96,112},{112,96},{1... | collective-permute-start | bytes 202760 | tf_op jit(solution)/shard_map/ppermute | solution.py:169
  185.7 7.8 %collective-permute-start.14 = (f32[67,256]{1,0:T(8,128)S(1)}, f32[67,256]{1,0:T(8,128)S(1)}, u32[]{:S(2)}, u32[]{:S(2)}) collective-permute-start(f32[67,256]{1,0:T(8,128)S(1)} %maximum_select_fusion.2), channel_id=1, source_target_pairs={{0,8},{1,9},{2,10},{3,11},{4,12},{5,13},{6,14},{7,15},{8,0},{9,1},... | collective-permute-start | bytes 205832 | tf_op jit(solution)/shard_map/ppermute | solution.py:169
  261.5 11.1 %collective-permute-start.18 = (f32[12,128]{1,0:T(8,128)S(1)}, f32[12,128]{1,0:T(8,128)S(1)}, u32[]{:S(2)}, u32[]{:S(2)}) collective-permute-start(f32[12,128]{1,0:T(8,128)S(1)} %reshape.198), channel_id=1, source_target_pairs={{0,1},{1,0},{2,3},{3,2},{4,5},{5,4},{6,7},{7,6},{8,9},{9,8},{10,11... | collective-permute-start | bytes 18440 | tf_op jit(solution)/shard_map/ppermute | solution.py:215
  264.5 8.1 %collective-permute-start.19 = (f32[12,128]{1,0:T(8,128)S(1)}, f32[12,128]{1,0:T(8,128)S(1)}, u32[]{:S(2)}, u32[]{:S(2)}) collective-permute-start(f32[12,128]{1,0:T(8,128)S(1)} %reshape.198), channel_id=1, source_target_pairs={{0,2},{1,3},{2,0},{3,1},{4,6},{5,7},{6,4},{7,5},{8,10},{9,11},{10,... | collective-permute-start | bytes 18440 | tf_op jit(solution)/shard_map/ppermute | solution.py:215
  267.3 6.8 %collective-permute-start.20 = (f32[12,128]{1,0:T(8,128)S(1)}, f32[12,128]{1,0:T(8,128)S(1)}, u32[]{:S(2)}, u32[]{:S(2)}) collective-permute-start(f32[12,128]{1,0:T(8,128)S(1)} %reshape.198), channel_id=1, source_target_pairs={{0,3},{1,2},{2,1},{3,0},{4,7},{5,6},{6,5},{7,4},{8,11},{9,10},{10,... | collective-permute-start | bytes 18440 | tf_op jit(solution)/shard_map/ppermute | solution.py:215
  274.1 10.5 %collective-permute-start.21 = (f32[12,128]{1,0:T(8,128)S(1)}, f32[12,128]{1,0:T(8,128)S(1)}, u32[]{:S(2)}, u32[]{:S(2)}) collective-permute-start(f32[12,128]{1,0:T(8,128)S(1)} %fusion.93), channel_id=1, source_target_pairs={{0,4},{1,5},{2,6},{3,7},{4,0},{5,1},{6,2},{7,3},{8,12},{9,13},{10,... | collective-permute-start | bytes 18440 | tf_op jit(solution)/shard_map/ppermute | solution.py:215
  276.4 8.2 %collective-permute-start.22 = (f32[12,128]{1,0:T(8,128)S(1)}, f32[12,128]{1,0:T(8,128)S(1)}, u32[]{:S(2)}, u32[]{:S(2)}) collective-permute-start(f32[12,128]{1,0:T(8,128)S(1)} %fusion.93), channel_id=1, source_target_pairs={{0,8},{1,9},{2,10},{3,11},{4,12},{5,13},{6,14},{7,15},{8,0},{9,1},... | collective-permute-start | bytes 18440 | tf_op jit(solution)/shard_map/ppermute | solution.py:215
  282.1 6.8 %collective-permute-start.23 = (f32[12,128]{1,0:T(8,128)S(1)}, f32[12,128]{1,0:T(8,128)S(1)}, u32[]{:S(2)}, u32[]{:S(2)}) collective-permute-start(f32[12,128]{1,0:T(8,128)S(1)} %fusion.93), channel_id=1, source_target_pairs={{0,12},{1,13},{2,14},{3,15},{4,8},{5,9},{6,10},{7,11},{8,4},{9,5},... | collective-permute-start | bytes 18440 | tf_op jit(solution)/shard_map/ppermute | solution.py:215
  (2 other events, 3.7 us)

commit v11 on v9

--- a/solution.py
+++ b/solution.py
@@ -245,12 +245,17 @@
     str_imag = near_str[freqs:]
     part_real = (cosine * str_real - sine * str_imag) * inverse
     part_imag = (cosine * str_imag + sine * str_real) * inverse
-    eta_part = jnp.concatenate(
-        [
-            part_real.reshape(freqs, -1, listed).sum(axis=2),
-            part_imag.reshape(freqs, -1, listed).sum(axis=2),
-        ],
-        axis=0,
+    point_count = field_pos.shape[1]
+    point_hits = (
+        lax.broadcasted_iota(jnp.int32, (point_count * listed, point_count), 0) // listed
+        == lax.broadcasted_iota(jnp.int32, (point_count * listed, point_count), 1)
+    ).astype(jnp.bfloat16)
+    eta_part = join_three(
+        jnp.dot(
+            split_three(jnp.concatenate([part_real, part_imag], axis=0)),
+            point_hits,
+            preferred_element_type=jnp.float32,
+        )
     )
     eta = xor_psum(eta_part, "col")
     resid = eta - targets

time: 288 us -> 310 us (1.076)
  matrix products: 28.7 us -> 58.6 us
  local copies, waits for them, and re-layouts: 19.4 us -> 14.6 us
    dot_general x0 -> x1, matrix products: none -> 29.9 us  [on_device(): jnp.dot(split_three(jnp.concatenate([part_real, part_imag], axis=0)), poi...]
    reshape x2 -> x0, local copies, waits for them, and re-layouts: 5.45 us -> none  [the longest x1 3.39 us: on_device(): part_imag.reshape(freqs, -1, listed).sum(axis=2)]
  transfers between devices with their start and end apart: 20 -> 20, of which waited for: 17 -> 17; matrix products, arithmetic and copies ran while one was open for 1% -> 0% of each run, Pallas kernels for 0% -> 0%
where the time goes in v11:
time: 310 us; the launch traced here: 309 us
  other arithmetic  76.8 us (25%)
  starting transfers between devices  65.6 us (21%)
  matrix products  58.6 us (19%)
  waiting for transfers between devices  50.9 us (16%)
  blocking collectives  37.6 us (12%)
  local copies, waits for them, and re-layouts  14.6 us (5%)
  between operations  3.41 us (1%)
    reduce_sum x2, other arithmetic, pair_block(): weight = jnp.sum(inner, axis=0) * (inverse * inverse * inverse)  62.6 us
    all_gather x1, blocking collectives, on_device(): src_all = lax.all_gather(owned, 'row', axis=1, tiled=True)  37.6 us
    dot_general x1, matrix products, on_device(): jnp.dot(split_three(jnp.concatenate([part_real, part_imag], axis=0)), poi...  29.9 us
    ppermute x8, starting transfers between devices, xor_psum(): value = value + lax.ppermute(value, axis, partner)  28.5 us
    ppermute x8, waiting for transfers between devices, xor_psum(): value = value + lax.ppermute(value, axis, partner)  22.2 us
    ppermute x7, starting transfers between devices, doubling_gather(): other = lax.ppermute(value, axis, partner)  20.8 us
    dot_general x1, matrix products, on_device(): jnp.dot(split_three(table[:pos_rows + str_rows]), onehot, preferred_eleme...  14.5 us
    dot_general x1, matrix products, on_device(): lax.dot_general(split_three(terms), onehot, (((1,), (1,)), ((), ())), pre...  14 us
  transfers between devices with their start and end apart: 20, of which 17 were waited for; matrix products, arithmetic and copies ran while one was open for 0% of the time, Pallas kernels for 0%

profile of v11, /device:TPU:6, one launch (start us, length us, event | category | flops | bytes accessed | tf_op | source)
XLA Modules:
  0.0 309.1 jit_solution(13023021747838914896)
XLA Ops:
  3.1 37.6 %all_gather.3 = f32[67,1024]{0,1:T(8,128)S(1)} all-gather(f32[67,32]{0,1:T(8,128)S(1)} %pad_maximum_fusion.6), channel_id=1, replica_groups=mesh['row'=32,'col'=16] {'row'}, dimensions={1}, use_global_device_ids=true | all-gather | bytes 283008 | tf_op jit(solution)/shard_map/all_gather | solution.py:213
  46.7 14.5 %fusion.28 = f32[105,16384]{1,0:T(8,128)S(1)} fusion(s32[16384]{0:T(1024)S(1)} %fusion.79, bf16[35,1024]{1,0:T(8,128)(2,1)S(1)} %get-tuple-element.168, bf16[35,1024]{1,0:T(8,128)(2,1)S(1)} %get-tuple-element.169, bf16[35,1024]{1,0:T(8,128)(2,1)S(1)} %get-tuple-element.167), kind=kOutput, calls=%fused_computation.49 | convolution fusion | flops 3540637696 | bytes 7161856 | tf_op jit(solution)/shard_map/dot_general | solution.py:234
  66.5 29.9 %fusion.31 = f32[96,256]{1,0:T(8,128)S(1)} fusion(s32[16384]{0:T(1024)S(1)} %get-tuple-element.181, s32[16384]{0:T(1024)} %get-tuple-element.182, pred[16384]{0:T(1024)(128)(4,1)S(1)} %fusion.85, bf16[32,16384]{1,0:T(8,128)(2,1)S(1)} %get-tuple-element.132, bf16[32,16384]{1,0:T(8,128)(2,1)S(1)} %get-tuple-element.131, ...), kind=kOutput, calls=%fused_computation.53 | convolution fusion | flops 823132160 | bytes 3391488 | tf_op jit(solution)/shard_map/dot_general | solution.py:254
  96.4 3.5 %collective-permute-start = (f32[32,256]{1,0:T(8,128)S(1)}, f32[32,256]{1,0:T(8,128)S(1)}, u32[]{:S(2)}, u32[]{:S(2)}) collective-permute-start(f32[32,256]{1,0:T(8,128)S(1)} %slice_add_fusion.4), channel_id=1, source_target_pairs={{0,1},{1,0},{2,3},{3,2},{4,5},{5,4},{6,7},{7,6},{8,9},{9,8},{10,11... | collective-permute-start | bytes 98312 | tf_op jit(solution)/shard_map/ppermute | solution.py:113
  102.2 5.1 %collective-permute-start.1 = (f32[32,256]{1,0:T(8,128)S(1)}, f32[32,256]{1,0:T(8,128)S(1)}, u32[]{:S(2)}, u32[]{:S(2)}) collective-permute-start(f32[32,256]{1,0:T(8,128)S(1)} %fusion.106), channel_id=1, source_target_pairs={{0,2},{1,3},{2,0},{3,1},{4,6},{5,7},{6,4},{7,5},{8,10},{9,11},{10,... | collective-permute-start | bytes 98312 | tf_op jit(solution)/shard_map/ppermute | solution.py:113
  109.6 2.7 collective-permute-start.2
  112.3 3.1 collective-permute-done.2
  115.4 3.5 %collective-permute-start.3 = (f32[32,256]{1,0:T(8,128)S(1)}, f32[32,256]{1,0:T(8,128)S(1)}, u32[]{:S(2)}, u32[]{:S(2)}) collective-permute-start(f32[32,256]{1,0:T(8,128)S(1)} %add.293), channel_id=1, source_target_pairs={{0,8},{1,9},{2,10},{3,11},{4,12},{5,13},{6,14},{7,15},{8,0},{9,1},... | collective-permute-start | bytes 98312 | tf_op jit(solution)/shard_map/ppermute | solution.py:113
  118.9 3.8 %collective-permute-done.3 = f32[32,256]{1,0:T(8,128)S(1)} collective-permute-done((f32[32,256]{1,0:T(8,128)S(1)}, f32[32,256]{1,0:T(8,128)S(1)}, u32[]{:S(2)}, u32[]{:S(2)}) %collective-permute-start.3) | collective-permute-done | bytes 32800 | tf_op jit(solution)/shard_map/ppermute | solution.py:113
  126.8 2.9 add_multiply_fusion
  130.2 14.0 %fusion.27 = f32[96,1024]{1,0:T(8,128)S(1)} fusion(s32[16384]{0:T(1024)S(1)} %copy-done.4, bf16[32,16384]{1,0:T(8,128)(2,1)S(1)} %get-tuple-element.129, bf16[32,16384]{1,0:T(8,128)(2,1)S(1)} %get-tuple-element.128, bf16[32,16384]{1,0:T(8,128)(2,1)S(1)} %get-tuple-element.127), kind=kOutput, calls=%fused_computation.48 | convolution fusion | flops 3247439872 | bytes 3604480 | tf_op jit(solution)/shard_map/dot_general | solution.py:268
  150.7 3.9 %collective-permute-done.5 = f32[33,256]{1,0:T(8,128)S(1)} collective-permute-done((f32[33,256]{1,0:T(8,128)S(1)}, f32[33,256]{1,0:T(8,128)S(1)}, u32[]{:S(2)}, u32[]{:S(2)}) %collective-permute-start.5) | collective-permute-done | bytes 33824 | tf_op jit(solution)/shard_map/ppermute | solution.py:152
  156.8 4.4 %collective-permute-done.6 = f32[33,128]{1,0:T(8,128)S(1)} collective-permute-done((f32[33,128]{1,0:T(8,128)S(1)}, f32[33,128]{1,0:T(8,128)S(1)}, u32[]{:S(2)}, u32[]{:S(2)}) %collective-permute-start.6) | collective-permute-done | bytes 16928 | tf_op jit(solution)/shard_map/ppermute | solution.py:152
  161.3 3.0 collective-permute-start.7
  164.3 6.5 %collective-permute-done.7 = f32[33,128]{1,0:T(8,128)S(1)} collective-permute-done((f32[33,128]{1,0:T(8,128)S(1)}, f32[33,128]{1,0:T(8,128)S(1)}, u32[]{:S(2)}, u32[]{:S(2)}) %collective-permute-start.7) | collective-permute-done | bytes 16928 | tf_op jit(solution)/shard_map/ppermute | solution.py:157
  170.8 7.2 %collective-permute-start.8 = (f32[33,128]{1,0:T(8,128)S(1)}, f32[33,128]{1,0:T(8,128)S(1)}, u32[]{:S(2)}, u32[]{:S(2)}) collective-permute-start(f32[33,128]{1,0:T(8,128)S(1)} %add.301), channel_id=1, source_target_pairs={{0,256},{16,272},{32,288},{48,304},{64,320},{80,336},{96,352},{112... | collective-permute-start | bytes 50696 | tf_op jit(solution)/shard_map/ppermute | solution.py:157
  178.1 7.1 %collective-permute-done.8 = f32[33,128]{1,0:T(8,128)S(1)} collective-permute-done((f32[33,128]{1,0:T(8,128)S(1)}, f32[33,128]{1,0:T(8,128)S(1)}, u32[]{:S(2)}, u32[]{:S(2)}) %collective-permute-start.8) | collective-permute-done | bytes 16928 | tf_op jit(solution)/shard_map/ppermute | solution.py:157
  186.5 3.5 %collective-permute-start.9 = (f32[67,32]{1,0:T(8,128)S(1)}, f32[67,32]{1,0:T(8,128)S(1)}, u32[]{:S(2)}, u32[]{:S(2)}) collective-permute-start(f32[67,32]{1,0:T(8,128)S(1)} %pad_maximum_fusion.5), channel_id=1, source_target_pairs={{0,1},{1,0},{2,3},{3,2},{4,5},{5,4},{6,7},{7,6},{8,9},{9,8},{10,11... | collective-permute-start | bytes 25736 | tf_op jit(solution)/shard_map/ppermute | solution.py:169
  193.1 4.8 %collective-permute-start.10 = (f32[67,64]{1,0:T(8,128)S(1)}, f32[67,64]{1,0:T(8,128)S(1)}, u32[]{:S(2)}, u32[]{:S(2)}) collective-permute-start(f32[67,64]{1,0:T(8,128)S(1)} %maximum_select_fusion.4), channel_id=1, source_target_pairs={{0,2},{1,3},{2,0},{3,1},{4,6},{5,7},{6,4},{7,5},{8,10},{9,11},{10,... | collective-permute-start | bytes 51464 | tf_op jit(solution)/shard_map/ppermute | solution.py:169
  200.5 2.7 collective-permute-start.11
  206.4 3.5 %collective-permute-start.12 = (f32[67,256]{1,0:T(8,128)S(1)}, f32[67,256]{1,0:T(8,128)S(1)}, u32[]{:S(2)}, u32[]{:S(2)}) collective-permute-start(f32[67,256]{1,0:T(8,128)S(1)} %maximum_select_fusion.2), channel_id=1, source_target_pairs={{0,8},{1,9},{2,10},{3,11},{4,12},{5,13},{6,14},{7,15},{8,0},{9,1},... | collective-permute-start | bytes 205832 | tf_op jit(solution)/shard_map/ppermute | solution.py:169
  210.0 4.1 %collective-permute-done.12 = f32[67,256]{1,0:T(8,128)S(1)} collective-permute-done((f32[67,256]{1,0:T(8,128)S(1)}, f32[67,256]{1,0:T(8,128)S(1)}, u32[]{:S(2)}, u32[]{:S(2)}) %collective-permute-start.12) | collective-permute-done | bytes 68640 | tf_op jit(solution)/shard_map/ppermute | solution.py:169
  214.2 67.6 %while.11 = (s32[]{:T(128)}, f32[3,512]{1,0:T(4,128)S(1)}, f32[16]{0:T(128)S(1)}, f32[3,512]{1,0:T(4,128)S(1)}, s32[2]{0:T(128)S(1)}, /*index=5*/f32[3,1024]{1,0...) while((s32[]{:T(128)}, f32[3,512]{1,0:T(4,128)S(1)}, ...), condition=%wide.region_6.7_spmd.clone, body=%wide.region_2.6_spmd.clone.sunk | while | flops 240649728 | bytes 10285353 | solution.py:87
  216.0 31.3 %fusion.117 = f32[512,512]{1,0:T(8,128)S(1)} fusion(f32[16,512]{1,0:T(8,128)S(1)} %get-tuple-element.252, f32[16,512]{1,0:T(8,128)S(1)} %get-tuple-element.253, f32[16,512]{1,0:T(8,128)S(1)} %get-tuple-element.254, f32[16,512]{1,0:T(8,128)S(1)} %get-tuple-element.255, f32[16,512]{1,0:T(8,128)S(1)} %get-tuple-element.256, ...), kind=kLoop, calls=%fused_computation.35.clone.1 | loop fusion | flops 234618880 | bytes 2359360 | tf_op jit(solution)/shard_map/while/body/eval_jaxpr/reduce_sum | solution.py:67
  249.9 31.3 %fusion.117 = f32[512,512]{1,0:T(8,128)S(1)} fusion(f32[16,512]{1,0:T(8,128)S(1)} %get-tuple-element.252, f32[16,512]{1,0:T(8,128)S(1)} %get-tuple-element.253, f32[16,512]{1,0:T(8,128)S(1)} %get-tuple-element.254, f32[16,512]{1,0:T(8,128)S(1)} %get-tuple-element.255, f32[16,512]{1,0:T(8,128)S(1)} %get-tuple-element.256, ...), kind=kLoop, calls=%fused_computation.35.clone.1 | loop fusion | flops 234618880 | bytes 2359360 | tf_op jit(solution)/shard_map/while/body/eval_jaxpr/reduce_sum | solution.py:67
  282.1 2.9 collective-permute-start.16
  285.0 2.7 collective-permute-done.16
  287.7 4.8 %collective-permute-start.17 = (f32[12,128]{1,0:T(8,128)S(1)}, f32[12,128]{1,0:T(8,128)S(1)}, u32[]{:S(2)}, u32[]{:S(2)}) collective-permute-start(f32[12,128]{1,0:T(8,128)S(1)} %add.315), channel_id=1, source_target_pairs={{0,2},{1,3},{2,0},{3,1},{4,6},{5,7},{6,4},{7,5},{8,10},{9,11},{10,... | collective-permute-start | bytes 18440 | tf_op jit(solution)/shard_map/ppermute | solution.py:113
  294.7 2.7 collective-permute-start.18
  297.5 2.8 collective-permute-done.18
  300.3 3.3 %collective-permute-start.19 = (f32[12,128]{1,0:T(8,128)S(1)}, f32[12,128]{1,0:T(8,128)S(1)}, u32[]{:S(2)}, u32[]{:S(2)}) collective-permute-start(f32[12,128]{1,0:T(8,128)S(1)} %add.317), channel_id=1, source_target_pairs={{0,8},{1,9},{2,10},{3,11},{4,12},{5,13},{6,14},{7,15},{8,0},{9,1},... | collective-permute-start | bytes 18440 | tf_op jit(solution)/shard_map/ppermute | solution.py:113
  304.2 3.1 %collective-permute-done.19 = f32[12,128]{1,0:T(8,128)S(1)} collective-permute-done((f32[12,128]{1,0:T(8,128)S(1)}, f32[12,128]{1,0:T(8,128)S(1)}, u32[]{:S(2)}, u32[]{:S(2)}) %collective-permute-start.19) | collective-permute-done | bytes 6176 | tf_op jit(solution)/shard_map/ppermute | solution.py:113
  (159 shorter events, 47.9 us)
Async XLA Ops:
  46.1 0.6 copy-start.3
  61.2 0.7 copy-start.9
  61.2 3.0 copy-start.6
  64.2 1.8 copy-start
  66.5 56.2 %copy-start.5 = (f32[32,256]{1,0:T(8,128)S(1)}, f32[32,256]{1,0:T(8,128)}, u32[]{:S(2)}) copy-start(f32[32,256]{1,0:T(8,128)} %param.15) | copy-start | bytes 98308
  96.4 5.8 %collective-permute-start = (f32[32,256]{1,0:T(8,128)S(1)}, f32[32,256]{1,0:T(8,128)S(1)}, u32[]{:S(2)}, u32[]{:S(2)}) collective-permute-start(f32[32,256]{1,0:T(8,128)S(1)} %slice_add_fusion.4), channel_id=1, source_target_pairs={{0,1},{1,0},{2,3},{3,2},{4,5},{5,4},{6,7},{7,6},{8,9},{9,8},{10,11... | collective-permute-start | bytes 98312 | tf_op jit(solution)/shard_map/ppermute | solution.py:113
  102.2 7.3 %collective-permute-start.1 = (f32[32,256]{1,0:T(8,128)S(1)}, f32[32,256]{1,0:T(8,128)S(1)}, u32[]{:S(2)}, u32[]{:S(2)}) collective-permute-start(f32[32,256]{1,0:T(8,128)S(1)} %fusion.106), channel_id=1, source_target_pairs={{0,2},{1,3},{2,0},{3,1},{4,6},{5,7},{6,4},{7,5},{8,10},{9,11},{10,... | collective-permute-start | bytes 98312 | tf_op jit(solution)/shard_map/ppermute | solution.py:113
  109.6 5.8 %collective-permute-start.2 = (f32[32,256]{1,0:T(8,128)S(1)}, f32[32,256]{1,0:T(8,128)S(1)}, u32[]{:S(2)}, u32[]{:S(2)}) collective-permute-start(f32[32,256]{1,0:T(8,128)S(1)} %add.292), channel_id=1, source_target_pairs={{0,4},{1,5},{2,6},{3,7},{4,0},{5,1},{6,2},{7,3},{8,12},{9,13},{10,... | collective-permute-start | bytes 98312 | tf_op jit(solution)/shard_map/ppermute | solution.py:113
  115.4 7.3 %collective-permute-start.3 = (f32[32,256]{1,0:T(8,128)S(1)}, f32[32,256]{1,0:T(8,128)S(1)}, u32[]{:S(2)}, u32[]{:S(2)}) collective-permute-start(f32[32,256]{1,0:T(8,128)S(1)} %add.293), channel_id=1, source_target_pairs={{0,8},{1,9},{2,10},{3,11},{4,12},{5,13},{6,14},{7,15},{8,0},{9,1},... | collective-permute-start | bytes 98312 | tf_op jit(solution)/shard_map/ppermute | solution.py:113
  126.8 3.4 %copy-start.4 = (s32[16384]{0:T(1024)S(1)}, s32[16384]{0:T(1024)}, u32[]{:S(2)}) copy-start(s32[16384]{0:T(1024)} %copy-done.3) | copy-start | bytes 196612
  130.2 47.9 %copy-start.8 = (s32[4,512]{1,0:T(4,128)S(1)}, s32[4,512]{1,0:T(4,128)}, u32[]{:S(2)}) copy-start(s32[4,512]{1,0:T(4,128)} %param.17) | copy-start | bytes 24580
  130.2 56.3 %copy-start.2 = (f32[32,32]{1,0:T(8,128)S(1)}, f32[32,32]{1,0:T(8,128)}, u32[]{:S(2)}) copy-start(f32[32,32]{1,0:T(8,128)} %param.12) | copy-start | bytes 12292
  130.2 56.3 %copy-start.1 = (f32[32,32]{1,0:T(8,128)S(1)}, f32[32,32]{1,0:T(8,128)}, u32[]{:S(2)}) copy-start(f32[32,32]{1,0:T(8,128)} %param.11) | copy-start | bytes 12292
  130.2 56.3 %copy-start.7 = (f32[3,32]{1,0:T(4,128)S(1)}, f32[3,32]{1,0:T(4,128)}, u32[]{:S(2)}) copy-start(f32[3,32]{1,0:T(4,128)} %param.10) | copy-start | bytes 1156
  144.9 3.2 %collective-permute-start.4 = (f32[33,512]{1,0:T(8,128)S(1)}, f32[33,512]{1,0:T(8,128)S(1)}, u32[]{:S(2)}, u32[]{:S(2)}) collective-permute-start(f32[33,512]{1,0:T(8,128)S(1)} %broadcast_select_fusion), channel_id=1, source_target_pairs={{0,16},{16,0},{32,48},{48,32},{64,80},{80,64},{96,112},{112,96},{1... | collective-permute-start | bytes 202760 | tf_op jit(solution)/shard_map/ppermute | solution.py:152
  148.7 5.9 %collective-permute-start.5 = (f32[33,256]{1,0:T(8,128)S(1)}, f32[33,256]{1,0:T(8,128)S(1)}, u32[]{:S(2)}, u32[]{:S(2)}) collective-permute-start(f32[33,256]{1,0:T(8,128)S(1)} %slice_select_fusion), channel_id=1, source_target_pairs={{0,32},{16,48},{32,0},{48,16},{64,96},{80,112},{96,64},{112,80},{1... | collective-permute-start | bytes 101384 | tf_op jit(solution)/shard_map/ppermute | solution.py:152
  154.7 6.6 %collective-permute-start.6 = (f32[33,128]{1,0:T(8,128)S(1)}, f32[33,128]{1,0:T(8,128)S(1)}, u32[]{:S(2)}, u32[]{:S(2)}) collective-permute-start(f32[33,128]{1,0:T(8,128)S(1)} %slice_select_fusion.1), channel_id=1, source_target_pairs={{0,64},{16,80},{32,96},{48,112},{64,0},{80,16},{96,32},{112,48},{1... | collective-permute-start | bytes 50696 | tf_op jit(solution)/shard_map/ppermute | solution.py:152
  161.3 9.6 %collective-permute-start.7 = (f32[33,128]{1,0:T(8,128)S(1)}, f32[33,128]{1,0:T(8,128)S(1)}, u32[]{:S(2)}, u32[]{:S(2)}) collective-permute-start(f32[33,128]{1,0:T(8,128)S(1)} %select_add_fusion.3), channel_id=1, source_target_pairs={{0,128},{16,144},{32,160},{48,176},{64,192},{80,208},{96,224},{112... | collective-permute-start | bytes 50696 | tf_op jit(solution)/shard_map/ppermute | solution.py:157
  170.8 14.4 %collective-permute-start.8 = (f32[33,128]{1,0:T(8,128)S(1)}, f32[33,128]{1,0:T(8,128)S(1)}, u32[]{:S(2)}, u32[]{:S(2)}) collective-permute-start(f32[33,128]{1,0:T(8,128)S(1)} %add.301), channel_id=1, source_target_pairs={{0,256},{16,272},{32,288},{48,304},{64,320},{80,336},{96,352},{112... | collective-permute-start | bytes 50696 | tf_op jit(solution)/shard_map/ppermute | solution.py:157
  186.5 6.5 %collective-permute-start.9 = (f32[67,32]{1,0:T(8,128)S(1)}, f32[67,32]{1,0:T(8,128)S(1)}, u32[]{:S(2)}, u32[]{:S(2)}) collective-permute-start(f32[67,32]{1,0:T(8,128)S(1)} %pad_maximum_fusion.5), channel_id=1, source_target_pairs={{0,1},{1,0},{2,3},{3,2},{4,5},{5,4},{6,7},{7,6},{8,9},{9,8},{10,11... | collective-permute-start | bytes 25736 | tf_op jit(solution)/shard_map/ppermute | solution.py:169
  190.8 7.1 %collective-permute-start.13 = (f32[33,128]{1,0:T(8,128)S(1)}, f32[33,128]{1,0:T(8,128)S(1)}, u32[]{:S(2)}, u32[]{:S(2)}) collective-permute-start(f32[33,128]{1,0:T(8,128)S(1)} %add.302), channel_id=1, source_target_pairs={{0,64},{16,80},{32,96},{48,112},{64,0},{80,16},{96,32},{112,48},{1... | collective-permute-start | bytes 50696 | tf_op jit(solution)/shard_map/ppermute | solution.py:169
  193.1 7.4 %collective-permute-start.10 = (f32[67,64]{1,0:T(8,128)S(1)}, f32[67,64]{1,0:T(8,128)S(1)}, u32[]{:S(2)}, u32[]{:S(2)}) collective-permute-start(f32[67,64]{1,0:T(8,128)S(1)} %maximum_select_fusion.4), channel_id=1, source_target_pairs={{0,2},{1,3},{2,0},{3,1},{4,6},{5,7},{6,4},{7,5},{8,10},{9,11},{10,... | collective-permute-start | bytes 51464 | tf_op jit(solution)/shard_map/ppermute | solution.py:169
  197.9 5.9 %collective-permute-start.14 = (f32[33,256]{1,0:T(8,128)S(1)}, f32[33,256]{1,0:T(8,128)S(1)}, u32[]{:S(2)}, u32[]{:S(2)}) collective-permute-start(f32[33,256]{1,0:T(8,128)S(1)} %maximum_select_fusion.3), channel_id=1, source_target_pairs={{0,32},{16,48},{32,0},{48,16},{64,96},{80,112},{96,64},{112,80},{1... | collective-permute-start | bytes 101384 | tf_op jit(solution)/shard_map/ppermute | solution.py:169
  200.5 5.9 %collective-permute-start.11 = (f32[67,128]{1,0:T(8,128)S(1)}, f32[67,128]{1,0:T(8,128)S(1)}, u32[]{:S(2)}, u32[]{:S(2)}) collective-permute-start(f32[67,128]{1,0:T(8,128)S(1)} %maximum_select_fusion.5), channel_id=1, source_target_pairs={{0,4},{1,5},{2,6},{3,7},{4,0},{5,1},{6,2},{7,3},{8,12},{9,13},{10,... | collective-permute-start | bytes 102920 | tf_op jit(solution)/shard_map/ppermute | solution.py:169
  203.8 6.1 %collective-permute-start.15 = (f32[33,512]{1,0:T(8,128)S(1)}, f32[33,512]{1,0:T(8,128)S(1)}, u32[]{:S(2)}, u32[]{:S(2)}) collective-permute-start(f32[33,512]{1,0:T(8,128)S(1)} %maximum_select_fusion.1), channel_id=1, source_target_pairs={{0,16},{16,0},{32,48},{48,32},{64,80},{80,64},{96,112},{112,96},{1... | collective-permute-start | bytes 202760 | tf_op jit(solution)/shard_map/ppermute | solution.py:169
  206.4 7.8 %collective-permute-start.12 = (f32[67,256]{1,0:T(8,128)S(1)}, f32[67,256]{1,0:T(8,128)S(1)}, u32[]{:S(2)}, u32[]{:S(2)}) collective-permute-start(f32[67,256]{1,0:T(8,128)S(1)} %maximum_select_fusion.2), channel_id=1, source_target_pairs={{0,8},{1,9},{2,10},{3,11},{4,12},{5,13},{6,14},{7,15},{8,0},{9,1},... | collective-permute-start | bytes 205832 | tf_op jit(solution)/shard_map/ppermute | solution.py:169
  282.1 5.5 %collective-permute-start.16 = (f32[12,128]{1,0:T(8,128)S(1)}, f32[12,128]{1,0:T(8,128)S(1)}, u32[]{:S(2)}, u32[]{:S(2)}) collective-permute-start(f32[12,128]{1,0:T(8,128)S(1)} %reshape.176), channel_id=1, source_target_pairs={{0,1},{1,0},{2,3},{3,2},{4,5},{5,4},{6,7},{7,6},{8,9},{9,8},{10,11... | collective-permute-start | bytes 18440 | tf_op jit(solution)/shard_map/ppermute | solution.py:113
  287.7 7.0 %collective-permute-start.17 = (f32[12,128]{1,0:T(8,128)S(1)}, f32[12,128]{1,0:T(8,128)S(1)}, u32[]{:S(2)}, u32[]{:S(2)}) collective-permute-start(f32[12,128]{1,0:T(8,128)S(1)} %add.315), channel_id=1, source_target_pairs={{0,2},{1,3},{2,0},{3,1},{4,6},{5,7},{6,4},{7,5},{8,10},{9,11},{10,... | collective-permute-start | bytes 18440 | tf_op jit(solution)/shard_map/ppermute | solution.py:113
  294.7 5.5 %collective-permute-start.18 = (f32[12,128]{1,0:T(8,128)S(1)}, f32[12,128]{1,0:T(8,128)S(1)}, u32[]{:S(2)}, u32[]{:S(2)}) collective-permute-start(f32[12,128]{1,0:T(8,128)S(1)} %add.316), channel_id=1, source_target_pairs={{0,4},{1,5},{2,6},{3,7},{4,0},{5,1},{6,2},{7,3},{8,12},{9,13},{10,... | collective-permute-start | bytes 18440 | tf_op jit(solution)/shard_map/ppermute | solution.py:113
  300.3 7.0 %collective-permute-start.19 = (f32[12,128]{1,0:T(8,128)S(1)}, f32[12,128]{1,0:T(8,128)S(1)}, u32[]{:S(2)}, u32[]{:S(2)}) collective-permute-start(f32[12,128]{1,0:T(8,128)S(1)} %add.317), channel_id=1, source_target_pairs={{0,8},{1,9},{2,10},{3,11},{4,12},{5,13},{6,14},{7,15},{8,0},{9,1},... | collective-permute-start | bytes 18440 | tf_op jit(solution)/shard_map/ppermute | solution.py:113

commit v12 on v9

--- a/solution.py
+++ b/solution.py
@@ -72,7 +72,7 @@
     total, target_pos, target_str, target_mu, source_pos, source_str, source_mu, wavenumbers
 ):
     width = source_pos.shape[1]
-    step = math.gcd(width, 512)
+    step = math.gcd(width, 1024)
 
     def visit_block(carry, block_index):
         begin = block_index * step

time: 288 us -> 285 us (0.990)
    reduce_sum x2 -> x1, other arithmetic: 62.6 us -> 62.2 us  [pair_block(): weight = jnp.sum(inner, axis=0) * (inverse * inverse * inverse)]
where the time goes in v12:
time: 285 us; the launch traced here: 284 us
  other arithmetic  79.6 us (28%)
  starting transfers between devices  65.6 us (23%)
  waiting for transfers between devices  51.1 us (18%)
  blocking collectives  37.6 us (13%)
  matrix products  28.7 us (10%)
  local copies, waits for them, and re-layouts  18.2 us (6%)
  between operations  3.41 us (1%)
    reduce_sum x1, other arithmetic, pair_block(): weight = jnp.sum(inner, axis=0) * (inverse * inverse * inverse)  62.2 us
    all_gather x1, blocking collectives, on_device(): src_all = lax.all_gather(owned, 'row', axis=1, tiled=True)  37.6 us
    ppermute x8, starting transfers between devices, xor_psum(): value = value + lax.ppermute(value, axis, partner)  28.5 us
    ppermute x8, waiting for transfers between devices, xor_psum(): value = value + lax.ppermute(value, axis, partner)  22.4 us
    ppermute x7, starting transfers between devices, doubling_gather(): other = lax.ppermute(value, axis, partner)  20.8 us
    dot_general x1, matrix products, on_device(): jnp.dot(split_three(table[:pos_rows + str_rows]), onehot, preferred_eleme...  14.5 us
    dot_general x1, matrix products, on_device(): lax.dot_general(split_three(terms), onehot, (((1,), (1,)), ((), ())), pre...  14 us
    ppermute x2, waiting for transfers between devices, near_far_reduce(): value = value + lax.ppermute(value, axis, partner)  13.6 us
  transfers between devices with their start and end apart: 20, of which 17 were waited for; matrix products, arithmetic and copies ran while one was open for 1% of the time, Pallas kernels for 0%

profile of v12, /device:TPU:6, one launch (start us, length us, event | category | flops | bytes accessed | tf_op | source)
XLA Modules:
  0.0 284.3 jit_solution(5114090493894557662)
XLA Ops:
  3.1 37.6 %all_gather.3 = f32[67,1024]{0,1:T(8,128)S(1)} all-gather(f32[67,32]{0,1:T(8,128)S(1)} %pad_maximum_fusion.5), channel_id=1, replica_groups=mesh['row'=32,'col'=16] {'row'}, dimensions={1}, use_global_device_ids=true | all-gather | bytes 283008 | tf_op jit(solution)/shard_map/all_gather | solution.py:213
  45.5 14.5 %fusion.1 = f32[105,16384]{1,0:T(8,128)S(1)} fusion(s32[16384]{0:T(1024)S(1)} %fusion.69, bf16[35,1024]{1,0:T(8,128)(2,1)S(1)} %get-tuple-element.76, bf16[35,1024]{1,0:T(8,128)(2,1)S(1)} %get-tuple-element.77, bf16[35,1024]{1,0:T(8,128)(2,1)S(1)} %get-tuple-element.75), kind=kOutput, calls=%fused_computation.6 | convolution fusion | flops 3540637696 | bytes 7161856 | tf_op jit(solution)/shard_map/dot_general | solution.py:234
  63.0 3.1 %subtract_multiply_fusion.3 = (f32[16,16384]{1,0:T(8,128)}, f32[16,16384]{1,0:T(8,128)}) fusion(f32[35,16384]{1,0:T(8,128)S(1)} %slice_add_fusion, f32[16384]{0:T(1024)S(1)} %get-tuple-element.83, f32[16384]{0:T(1024)S(1)} %get-tuple-element.82, f32[16]{0:T(128)S(1)} %copy-done.8), kind=kLoop, calls=%fused_computation.99 | loop fusion | flops 12058624 | bytes 4325440 | tf_op jit(solution)/shard_map/mul | solution.py:246
  68.1 3.4 %reshape.179 = f32[16,256,64]{2,1,0:T(8,128)} reshape(f32[16,16384]{1,0:T(8,128)} %get-tuple-element.24) | data formatting | bytes 2097152 | tf_op jit(solution)/shard_map/reshape | solution.py:251
  74.4 3.5 %collective-permute-start = (f32[32,256]{1,0:T(8,128)S(1)}, f32[32,256]{1,0:T(8,128)S(1)}, u32[]{:S(2)}, u32[]{:S(2)}) collective-permute-start(f32[32,256]{1,0:T(8,128)S(1)} %pad_maximum_fusion.4), channel_id=1, source_target_pairs={{0,1},{1,0},{2,3},{3,2},{4,5},{5,4},{6,7},{7,6},{8,9},{9,8},{10,11... | collective-permute-start | bytes 98312 | tf_op jit(solution)/shard_map/ppermute | solution.py:113
  77.9 2.3 collective-permute-done
  80.2 5.1 %collective-permute-start.1 = (f32[32,256]{1,0:T(8,128)S(1)}, f32[32,256]{1,0:T(8,128)S(1)}, u32[]{:S(2)}, u32[]{:S(2)}) collective-permute-start(f32[32,256]{1,0:T(8,128)S(1)} %fusion.85), channel_id=1, source_target_pairs={{0,2},{1,3},{2,0},{3,1},{4,6},{5,7},{6,4},{7,5},{8,10},{9,11},{10,... | collective-permute-start | bytes 98312 | tf_op jit(solution)/shard_map/ppermute | solution.py:113
  87.5 2.7 collective-permute-start.2
  90.2 3.1 %collective-permute-done.2 = f32[32,256]{1,0:T(8,128)S(1)} collective-permute-done((f32[32,256]{1,0:T(8,128)S(1)}, f32[32,256]{1,0:T(8,128)S(1)}, u32[]{:S(2)}, u32[]{:S(2)}) %collective-permute-start.2) | collective-permute-done | bytes 32800 | tf_op jit(solution)/shard_map/ppermute | solution.py:113
  93.3 3.5 %collective-permute-start.3 = (f32[32,256]{1,0:T(8,128)S(1)}, f32[32,256]{1,0:T(8,128)S(1)}, u32[]{:S(2)}, u32[]{:S(2)}) collective-permute-start(f32[32,256]{1,0:T(8,128)S(1)} %add.293), channel_id=1, source_target_pairs={{0,8},{1,9},{2,10},{3,11},{4,12},{5,13},{6,14},{7,15},{8,0},{9,1},... | collective-permute-start | bytes 98312 | tf_op jit(solution)/shard_map/ppermute | solution.py:113
  96.8 4.0 %collective-permute-done.3 = f32[32,256]{1,0:T(8,128)S(1)} collective-permute-done((f32[32,256]{1,0:T(8,128)S(1)}, f32[32,256]{1,0:T(8,128)S(1)}, u32[]{:S(2)}, u32[]{:S(2)}) %collective-permute-start.3) | collective-permute-done | bytes 32800 | tf_op jit(solution)/shard_map/ppermute | solution.py:113
  104.9 2.9 %add_multiply_fusion = (f32[16,16384]{1,0:T(8,128)S(1)}, f32[16,16384]{1,0:T(8,128)S(1)}) fusion(f32[16,16384]{1,0:T(8,128)} %reshape.181, f32[16,16384]{1,0:T(8,128)S(1)} %reshape.180, f32[16384]{0:T(1024)} %copy-done, f32[16384]{0:T(1024)S(1)} %get-tuple-element.82, f32[16]{0:T(128)S(1)} %copy-done.8), kind=kLoop, calls=%fused_computation.97 | loop fusion | flops 12058624 | bytes 4325440 | tf_op jit(solution)/shard_map/mul | solution.py:259
  108.3 14.0 %fusion = f32[96,1024]{1,0:T(8,128)S(1)} fusion(s32[16384]{0:T(1024)S(1)} %copy-done.4, bf16[32,16384]{1,0:T(8,128)(2,1)S(1)} %get-tuple-element.38, bf16[32,16384]{1,0:T(8,128)(2,1)S(1)} %get-tuple-element.37, bf16[32,16384]{1,0:T(8,128)(2,1)S(1)} %get-tuple-element.36), kind=kOutput, calls=%fused_computation.5 | convolution fusion | flops 3247439872 | bytes 3604480 | tf_op jit(solution)/shard_map/dot_general | solution.py:263
  128.8 3.9 %collective-permute-done.5 = f32[33,256]{1,0:T(8,128)S(1)} collective-permute-done((f32[33,256]{1,0:T(8,128)S(1)}, f32[33,256]{1,0:T(8,128)S(1)}, u32[]{:S(2)}, u32[]{:S(2)}) %collective-permute-start.5) | collective-permute-done | bytes 33824 | tf_op jit(solution)/shard_map/ppermute | solution.py:152
  134.9 4.4 %collective-permute-done.6 = f32[33,128]{1,0:T(8,128)S(1)} collective-permute-done((f32[33,128]{1,0:T(8,128)S(1)}, f32[33,128]{1,0:T(8,128)S(1)}, u32[]{:S(2)}, u32[]{:S(2)}) %collective-permute-start.6) | collective-permute-done | bytes 16928 | tf_op jit(solution)/shard_map/ppermute | solution.py:152
  139.3 3.1 %collective-permute-start.7 = (f32[33,128]{1,0:T(8,128)S(1)}, f32[33,128]{1,0:T(8,128)S(1)}, u32[]{:S(2)}, u32[]{:S(2)}) collective-permute-start(f32[33,128]{1,0:T(8,128)S(1)} %select_add_fusion.2), channel_id=1, source_target_pairs={{0,128},{16,144},{32,160},{48,176},{64,192},{80,208},{96,224},{112... | collective-permute-start | bytes 50696 | tf_op jit(solution)/shard_map/ppermute | solution.py:157
  142.4 6.5 %collective-permute-done.7 = f32[33,128]{1,0:T(8,128)S(1)} collective-permute-done((f32[33,128]{1,0:T(8,128)S(1)}, f32[33,128]{1,0:T(8,128)S(1)}, u32[]{:S(2)}, u32[]{:S(2)}) %collective-permute-start.7) | collective-permute-done | bytes 16928 | tf_op jit(solution)/shard_map/ppermute | solution.py:157
  148.9 7.3 %collective-permute-start.8 = (f32[33,128]{1,0:T(8,128)S(1)}, f32[33,128]{1,0:T(8,128)S(1)}, u32[]{:S(2)}, u32[]{:S(2)}) collective-permute-start(f32[33,128]{1,0:T(8,128)S(1)} %add.301), channel_id=1, source_target_pairs={{0,256},{16,272},{32,288},{48,304},{64,320},{80,336},{96,352},{112... | collective-permute-start | bytes 50696 | tf_op jit(solution)/shard_map/ppermute | solution.py:157
  156.2 7.1 %collective-permute-done.8 = f32[33,128]{1,0:T(8,128)S(1)} collective-permute-done((f32[33,128]{1,0:T(8,128)S(1)}, f32[33,128]{1,0:T(8,128)S(1)}, u32[]{:S(2)}, u32[]{:S(2)}) %collective-permute-start.8) | collective-permute-done | bytes 16928 | tf_op jit(solution)/shard_map/ppermute | solution.py:157
  164.6 3.5 %collective-permute-start.9 = (f32[67,32]{1,0:T(8,128)S(1)}, f32[67,32]{1,0:T(8,128)S(1)}, u32[]{:S(2)}, u32[]{:S(2)}) collective-permute-start(f32[67,32]{1,0:T(8,128)S(1)} %pad_maximum_fusion.3), channel_id=1, source_target_pairs={{0,1},{1,0},{2,3},{3,2},{4,5},{5,4},{6,7},{7,6},{8,9},{9,8},{10,11... | collective-permute-start | bytes 25736 | tf_op jit(solution)/shard_map/ppermute | solution.py:169
  171.1 4.8 %collective-permute-start.10 = (f32[67,64]{1,0:T(8,128)S(1)}, f32[67,64]{1,0:T(8,128)S(1)}, u32[]{:S(2)}, u32[]{:S(2)}) collective-permute-start(f32[67,64]{1,0:T(8,128)S(1)} %maximum_select_fusion.4), channel_id=1, source_target_pairs={{0,2},{1,3},{2,0},{3,1},{4,6},{5,7},{6,4},{7,5},{8,10},{9,11},{10,... | collective-permute-start | bytes 51464 | tf_op jit(solution)/shard_map/ppermute | solution.py:169
  178.6 2.7 collective-permute-start.11
  184.5 3.5 %collective-permute-start.12 = (f32[67,256]{1,0:T(8,128)S(1)}, f32[67,256]{1,0:T(8,128)S(1)}, u32[]{:S(2)}, u32[]{:S(2)}) collective-permute-start(f32[67,256]{1,0:T(8,128)S(1)} %maximum_select_fusion.2), channel_id=1, source_target_pairs={{0,8},{1,9},{2,10},{3,11},{4,12},{5,13},{6,14},{7,15},{8,0},{9,1},... | collective-permute-start | bytes 205832 | tf_op jit(solution)/shard_map/ppermute | solution.py:169
  188.1 4.1 %collective-permute-done.12 = f32[67,256]{1,0:T(8,128)S(1)} collective-permute-done((f32[67,256]{1,0:T(8,128)S(1)}, f32[67,256]{1,0:T(8,128)S(1)}, u32[]{:S(2)}, u32[]{:S(2)}) %collective-permute-start.12) | collective-permute-done | bytes 68640 | tf_op jit(solution)/shard_map/ppermute | solution.py:169
  193.5 62.2 %fusion.27 = f32[1024,512]{1,0:T(8,128)S(1)} fusion(f32[16,512]{1,0:T(8,128)S(1)} %get-tuple-element.79, f32[16,1024]{1,0:T(8,128)S(1)} %get-tuple-element.72, f32[16,512]{1,0:T(8,128)S(1)} %get-tuple-element.80, f32[16,1024]{1,0:T(8,128)S(1)} %get-tuple-element.71, f32[16,1024]{1,0:T(8,128)S(1)} %get-tuple-element.74, f32[16,512]{1,0:T(8,128)S(1)} %get-tuple-element.81, ...), kind=kLoop, calls=%fused_computation.40 | loop fusion | flops 469237760 | bytes 4587584 | tf_op jit(solution)/shard_map/while/body/eval_jaxpr/reduce_sum | solution.py:67
  257.3 2.9 %collective-permute-start.16 = (f32[12,128]{1,0:T(8,128)S(1)}, f32[12,128]{1,0:T(8,128)S(1)}, u32[]{:S(2)}, u32[]{:S(2)}) collective-permute-start(f32[12,128]{1,0:T(8,128)S(1)} %reshape.182), channel_id=1, source_target_pairs={{0,1},{1,0},{2,3},{3,2},{4,5},{5,4},{6,7},{7,6},{8,9},{9,8},{10,11... | collective-permute-start | bytes 18440 | tf_op jit(solution)/shard_map/ppermute | solution.py:113
  260.2 2.6 collective-permute-done.16
  262.9 4.8 %collective-permute-start.17 = (f32[12,128]{1,0:T(8,128)S(1)}, f32[12,128]{1,0:T(8,128)S(1)}, u32[]{:S(2)}, u32[]{:S(2)}) collective-permute-start(f32[12,128]{1,0:T(8,128)S(1)} %add.328), channel_id=1, source_target_pairs={{0,2},{1,3},{2,0},{3,1},{4,6},{5,7},{6,4},{7,5},{8,10},{9,11},{10,... | collective-permute-start | bytes 18440 | tf_op jit(solution)/shard_map/ppermute | solution.py:113
  269.9 2.7 collective-permute-start.18
  272.6 2.8 collective-permute-done.18
  275.4 3.3 %collective-permute-start.19 = (f32[12,128]{1,0:T(8,128)S(1)}, f32[12,128]{1,0:T(8,128)S(1)}, u32[]{:S(2)}, u32[]{:S(2)}) collective-permute-start(f32[12,128]{1,0:T(8,128)S(1)} %add.330), channel_id=1, source_target_pairs={{0,8},{1,9},{2,10},{3,11},{4,12},{5,13},{6,14},{7,15},{8,0},{9,1},... | collective-permute-start | bytes 18440 | tf_op jit(solution)/shard_map/ppermute | solution.py:113
  279.3 3.1 %collective-permute-done.19 = f32[12,128]{1,0:T(8,128)S(1)} collective-permute-done((f32[12,128]{1,0:T(8,128)S(1)}, f32[12,128]{1,0:T(8,128)S(1)}, u32[]{:S(2)}, u32[]{:S(2)}) %collective-permute-start.19) | collective-permute-done | bytes 6176 | tf_op jit(solution)/shard_map/ppermute | solution.py:113
  (139 shorter events, 45.9 us)
Async XLA Ops:
  45.5 14.5 %copy-start.3 = (s32[16384]{0:T(1024)}, s32[16384]{0:T(1024)S(1)}, u32[]{:S(2)}) copy-start(s32[16384]{0:T(1024)S(1)} %fusion.69) | copy-start | bytes 196612
  60.0 0.7 copy-start.9
  60.0 3.0 %copy-start.8 = (f32[16]{0:T(128)S(1)}, f32[16]{0:T(128)}, u32[]{:S(2)}) copy-start(f32[16]{0:T(128)} %param.11) | copy-start | bytes 196
  62.9 11.4 %copy-start = (f32[16384]{0:T(1024)}, f32[16384]{0:T(1024)S(1)}, u32[]{:S(2)}) copy-start(f32[16384]{0:T(1024)S(1)} %get-tuple-element.83) | copy-start | bytes 196612
  63.0 37.8 %copy-start.5 = (f32[32,256]{1,0:T(8,128)S(1)}, f32[32,256]{1,0:T(8,128)}, u32[]{:S(2)}) copy-start(f32[32,256]{1,0:T(8,128)} %param.13) | copy-start | bytes 98308
  74.4 5.8 %collective-permute-start = (f32[32,256]{1,0:T(8,128)S(1)}, f32[32,256]{1,0:T(8,128)S(1)}, u32[]{:S(2)}, u32[]{:S(2)}) collective-permute-start(f32[32,256]{1,0:T(8,128)S(1)} %pad_maximum_fusion.4), channel_id=1, source_target_pairs={{0,1},{1,0},{2,3},{3,2},{4,5},{5,4},{6,7},{7,6},{8,9},{9,8},{10,11... | collective-permute-start | bytes 98312 | tf_op jit(solution)/shard_map/ppermute | solution.py:113
  80.2 7.3 %collective-permute-start.1 = (f32[32,256]{1,0:T(8,128)S(1)}, f32[32,256]{1,0:T(8,128)S(1)}, u32[]{:S(2)}, u32[]{:S(2)}) collective-permute-start(f32[32,256]{1,0:T(8,128)S(1)} %fusion.85), channel_id=1, source_target_pairs={{0,2},{1,3},{2,0},{3,1},{4,6},{5,7},{6,4},{7,5},{8,10},{9,11},{10,... | collective-permute-start | bytes 98312 | tf_op jit(solution)/shard_map/ppermute | solution.py:113
  87.5 5.8 %collective-permute-start.2 = (f32[32,256]{1,0:T(8,128)S(1)}, f32[32,256]{1,0:T(8,128)S(1)}, u32[]{:S(2)}, u32[]{:S(2)}) collective-permute-start(f32[32,256]{1,0:T(8,128)S(1)} %add.292), channel_id=1, source_target_pairs={{0,4},{1,5},{2,6},{3,7},{4,0},{5,1},{6,2},{7,3},{8,12},{9,13},{10,... | collective-permute-start | bytes 98312 | tf_op jit(solution)/shard_map/ppermute | solution.py:113
  93.3 7.5 %collective-permute-start.3 = (f32[32,256]{1,0:T(8,128)S(1)}, f32[32,256]{1,0:T(8,128)S(1)}, u32[]{:S(2)}, u32[]{:S(2)}) collective-permute-start(f32[32,256]{1,0:T(8,128)S(1)} %add.293), channel_id=1, source_target_pairs={{0,8},{1,9},{2,10},{3,11},{4,12},{5,13},{6,14},{7,15},{8,0},{9,1},... | collective-permute-start | bytes 98312 | tf_op jit(solution)/shard_map/ppermute | solution.py:113
  104.9 3.4 %copy-start.4 = (s32[16384]{0:T(1024)S(1)}, s32[16384]{0:T(1024)}, u32[]{:S(2)}) copy-start(s32[16384]{0:T(1024)} %copy-done.3) | copy-start | bytes 196612
  108.3 47.9 %copy-start.7 = (s32[4,512]{1,0:T(4,128)S(1)}, s32[4,512]{1,0:T(4,128)}, u32[]{:S(2)}) copy-start(s32[4,512]{1,0:T(4,128)} %param.15) | copy-start | bytes 24580
  108.3 56.3 %copy-start.2 = (f32[32,32]{1,0:T(8,128)S(1)}, f32[32,32]{1,0:T(8,128)}, u32[]{:S(2)}) copy-start(f32[32,32]{1,0:T(8,128)} %param.10) | copy-start | bytes 12292
  108.3 56.3 %copy-start.1 = (f32[32,32]{1,0:T(8,128)S(1)}, f32[32,32]{1,0:T(8,128)}, u32[]{:S(2)}) copy-start(f32[32,32]{1,0:T(8,128)} %param.9) | copy-start | bytes 12292
  108.3 56.3 %copy-start.6 = (f32[3,32]{1,0:T(4,128)S(1)}, f32[3,32]{1,0:T(4,128)}, u32[]{:S(2)}) copy-start(f32[3,32]{1,0:T(4,128)} %param.8) | copy-start | bytes 1156
  123.0 3.2 %collective-permute-start.4 = (f32[33,512]{1,0:T(8,128)S(1)}, f32[33,512]{1,0:T(8,128)S(1)}, u32[]{:S(2)}, u32[]{:S(2)}) collective-permute-start(f32[33,512]{1,0:T(8,128)S(1)} %broadcast_select_fusion), channel_id=1, source_target_pairs={{0,16},{16,0},{32,48},{48,32},{64,80},{80,64},{96,112},{112,96},{1... | collective-permute-start | bytes 202760 | tf_op jit(solution)/shard_map/ppermute | solution.py:152
  126.8 5.9 %collective-permute-start.5 = (f32[33,256]{1,0:T(8,128)S(1)}, f32[33,256]{1,0:T(8,128)S(1)}, u32[]{:S(2)}, u32[]{:S(2)}) collective-permute-start(f32[33,256]{1,0:T(8,128)S(1)} %slice_select_fusion), channel_id=1, source_target_pairs={{0,32},{16,48},{32,0},{48,16},{64,96},{80,112},{96,64},{112,80},{1... | collective-permute-start | bytes 101384 | tf_op jit(solution)/shard_map/ppermute | solution.py:152
  132.8 6.6 %collective-permute-start.6 = (f32[33,128]{1,0:T(8,128)S(1)}, f32[33,128]{1,0:T(8,128)S(1)}, u32[]{:S(2)}, u32[]{:S(2)}) collective-permute-start(f32[33,128]{1,0:T(8,128)S(1)} %slice_select_fusion.1), channel_id=1, source_target_pairs={{0,64},{16,80},{32,96},{48,112},{64,0},{80,16},{96,32},{112,48},{1... | collective-permute-start | bytes 50696 | tf_op jit(solution)/shard_map/ppermute | solution.py:152
  139.3 9.6 %collective-permute-start.7 = (f32[33,128]{1,0:T(8,128)S(1)}, f32[33,128]{1,0:T(8,128)S(1)}, u32[]{:S(2)}, u32[]{:S(2)}) collective-permute-start(f32[33,128]{1,0:T(8,128)S(1)} %select_add_fusion.2), channel_id=1, source_target_pairs={{0,128},{16,144},{32,160},{48,176},{64,192},{80,208},{96,224},{112... | collective-permute-start | bytes 50696 | tf_op jit(solution)/shard_map/ppermute | solution.py:157
  148.9 14.4 %collective-permute-start.8 = (f32[33,128]{1,0:T(8,128)S(1)}, f32[33,128]{1,0:T(8,128)S(1)}, u32[]{:S(2)}, u32[]{:S(2)}) collective-permute-start(f32[33,128]{1,0:T(8,128)S(1)} %add.301), channel_id=1, source_target_pairs={{0,256},{16,272},{32,288},{48,304},{64,320},{80,336},{96,352},{112... | collective-permute-start | bytes 50696 | tf_op jit(solution)/shard_map/ppermute | solution.py:157
  164.6 6.4 %collective-permute-start.9 = (f32[67,32]{1,0:T(8,128)S(1)}, f32[67,32]{1,0:T(8,128)S(1)}, u32[]{:S(2)}, u32[]{:S(2)}) collective-permute-start(f32[67,32]{1,0:T(8,128)S(1)} %pad_maximum_fusion.3), channel_id=1, source_target_pairs={{0,1},{1,0},{2,3},{3,2},{4,5},{5,4},{6,7},{7,6},{8,9},{9,8},{10,11... | collective-permute-start | bytes 25736 | tf_op jit(solution)/shard_map/ppermute | solution.py:169
  168.9 7.1 %collective-permute-start.13 = (f32[33,128]{1,0:T(8,128)S(1)}, f32[33,128]{1,0:T(8,128)S(1)}, u32[]{:S(2)}, u32[]{:S(2)}) collective-permute-start(f32[33,128]{1,0:T(8,128)S(1)} %add.302), channel_id=1, source_target_pairs={{0,64},{16,80},{32,96},{48,112},{64,0},{80,16},{96,32},{112,48},{1... | collective-permute-start | bytes 50696 | tf_op jit(solution)/shard_map/ppermute | solution.py:169
  171.1 7.4 %collective-permute-start.10 = (f32[67,64]{1,0:T(8,128)S(1)}, f32[67,64]{1,0:T(8,128)S(1)}, u32[]{:S(2)}, u32[]{:S(2)}) collective-permute-start(f32[67,64]{1,0:T(8,128)S(1)} %maximum_select_fusion.4), channel_id=1, source_target_pairs={{0,2},{1,3},{2,0},{3,1},{4,6},{5,7},{6,4},{7,5},{8,10},{9,11},{10,... | collective-permute-start | bytes 51464 | tf_op jit(solution)/shard_map/ppermute | solution.py:169
  176.0 5.9 %collective-permute-start.14 = (f32[33,256]{1,0:T(8,128)S(1)}, f32[33,256]{1,0:T(8,128)S(1)}, u32[]{:S(2)}, u32[]{:S(2)}) collective-permute-start(f32[33,256]{1,0:T(8,128)S(1)} %maximum_select_fusion.3), channel_id=1, source_target_pairs={{0,32},{16,48},{32,0},{48,16},{64,96},{80,112},{96,64},{112,80},{1... | collective-permute-start | bytes 101384 | tf_op jit(solution)/shard_map/ppermute | solution.py:169
  178.6 5.9 %collective-permute-start.11 = (f32[67,128]{1,0:T(8,128)S(1)}, f32[67,128]{1,0:T(8,128)S(1)}, u32[]{:S(2)}, u32[]{:S(2)}) collective-permute-start(f32[67,128]{1,0:T(8,128)S(1)} %maximum_select_fusion.5), channel_id=1, source_target_pairs={{0,4},{1,5},{2,6},{3,7},{4,0},{5,1},{6,2},{7,3},{8,12},{9,13},{10,... | collective-permute-start | bytes 102920 | tf_op jit(solution)/shard_map/ppermute | solution.py:169
  181.9 6.1 %collective-permute-start.15 = (f32[33,512]{1,0:T(8,128)S(1)}, f32[33,512]{1,0:T(8,128)S(1)}, u32[]{:S(2)}, u32[]{:S(2)}) collective-permute-start(f32[33,512]{1,0:T(8,128)S(1)} %maximum_select_fusion.1), channel_id=1, source_target_pairs={{0,16},{16,0},{32,48},{48,32},{64,80},{80,64},{96,112},{112,96},{1... | collective-permute-start | bytes 202760 | tf_op jit(solution)/shard_map/ppermute | solution.py:169
  184.5 7.8 %collective-permute-start.12 = (f32[67,256]{1,0:T(8,128)S(1)}, f32[67,256]{1,0:T(8,128)S(1)}, u32[]{:S(2)}, u32[]{:S(2)}) collective-permute-start(f32[67,256]{1,0:T(8,128)S(1)} %maximum_select_fusion.2), channel_id=1, source_target_pairs={{0,8},{1,9},{2,10},{3,11},{4,12},{5,13},{6,14},{7,15},{8,0},{9,1},... | collective-permute-start | bytes 205832 | tf_op jit(solution)/shard_map/ppermute | solution.py:169
  257.3 5.5 %collective-permute-start.16 = (f32[12,128]{1,0:T(8,128)S(1)}, f32[12,128]{1,0:T(8,128)S(1)}, u32[]{:S(2)}, u32[]{:S(2)}) collective-permute-start(f32[12,128]{1,0:T(8,128)S(1)} %reshape.182), channel_id=1, source_target_pairs={{0,1},{1,0},{2,3},{3,2},{4,5},{5,4},{6,7},{7,6},{8,9},{9,8},{10,11... | collective-permute-start | bytes 18440 | tf_op jit(solution)/shard_map/ppermute | solution.py:113
  262.9 7.0 %collective-permute-start.17 = (f32[12,128]{1,0:T(8,128)S(1)}, f32[12,128]{1,0:T(8,128)S(1)}, u32[]{:S(2)}, u32[]{:S(2)}) collective-permute-start(f32[12,128]{1,0:T(8,128)S(1)} %add.328), channel_id=1, source_target_pairs={{0,2},{1,3},{2,0},{3,1},{4,6},{5,7},{6,4},{7,5},{8,10},{9,11},{10,... | collective-permute-start | bytes 18440 | tf_op jit(solution)/shard_map/ppermute | solution.py:113
  269.9 5.5 %collective-permute-start.18 = (f32[12,128]{1,0:T(8,128)S(1)}, f32[12,128]{1,0:T(8,128)S(1)}, u32[]{:S(2)}, u32[]{:S(2)}) collective-permute-start(f32[12,128]{1,0:T(8,128)S(1)} %add.329), channel_id=1, source_target_pairs={{0,4},{1,5},{2,6},{3,7},{4,0},{5,1},{6,2},{7,3},{8,12},{9,13},{10,... | collective-permute-start | bytes 18440 | tf_op jit(solution)/shard_map/ppermute | solution.py:113
  275.4 7.0 %collective-permute-start.19 = (f32[12,128]{1,0:T(8,128)S(1)}, f32[12,128]{1,0:T(8,128)S(1)}, u32[]{:S(2)}, u32[]{:S(2)}) collective-permute-start(f32[12,128]{1,0:T(8,128)S(1)} %add.330), channel_id=1, source_target_pairs={{0,8},{1,9},{2,10},{3,11},{4,12},{5,13},{6,14},{7,15},{8,0},{9,1},... | collective-permute-start | bytes 18440 | tf_op jit(solution)/shard_map/ppermute | solution.py:113
